TPU v7x, 256 devices: a whole 4x4x8 slice. The times are simulated.
256 devices in a mesh: con: 4 (over z_hi), grid: 64 (over z_lo, y, x, core).
Axes of the slice: x: 4, y: 4, z: 8 (z_hi: 4, z_lo: 2; z = z_hi * 2 + z_lo), core: 2. Of those that a mesh axis runs over, the one named last changes fastest.
Arguments:
- velocity: bfloat16 [8, 2, 4096, 4096], P('con', None, 'grid'), may hold values from -6 to 6
- seed_adjoint: bfloat16 [8, 2, 4096, 4096], P('con', None, 'grid'), may hold values from -6 to 6
- land_mask: int32 [4096, 4096], P('grid'), may hold values from 0 to 2
- inv_x: bfloat16 [32, 128, 128], replicated, may hold values from -0.5 to 0.5
- inv_y: bfloat16 [32, 128, 128], replicated, may hold values from -0.5 to 0.5
- weights: float32 [8], P('con'), may hold values from 0.05 to 0.5
Outputs:
- velocity_adjoint: float32 [8, 2, 4096, 4096], P('con', None, 'grid')
Inputs may be any that keep to these rules, and one draw needn't show every extreme that they name: `land_mask`: 0 marks land, 1 a wet interior cell, 2 an open-boundary cell whose value is prescribed.
All inputs are finite; a program needn't handle non-finite values.
Results may differ from a plain program's by a relative error of at most 0.0039.
Values may be sent and summed in bfloat16 or wider, within the bound.
No kernel may reach another device: no remote copies, remote signals or barrier semaphores. Data moves between devices by JAX's collectives and lax.ppermute only.
A program may use at most 64 MiB of HBM per device.

v0:
```python
import jax
import jax.numpy as jnp
from jax import lax
from jax.sharding import PartitionSpec as P

BLK = 128


def local(velocity, seed_adjoint, land_mask, inv_x, inv_y, weights):
    nblocks = inv_x.shape[0]
    con_local = velocity.shape[0]
    cols_local = seed_adjoint.shape[2]
    full_side = seed_adjoint.shape[3]
    rows_local = velocity.shape[2]
    vel_float = velocity.astype(jnp.float32)
    weight_full = weights[:, None, None, None]
    local_squares = jnp.sum(weight_full * vel_float * vel_float, axis=(0, 1))
    squares = lax.psum(local_squares, "con")
    sea_bool = land_mask == 1
    sea_float = sea_bool.astype(jnp.float32)
    sea_turned = jnp.swapaxes(sea_bool, 0, 1).astype(jnp.bfloat16)
    blocks_x = seed_adjoint.reshape(con_local, 2, cols_local, nblocks, BLK)
    across = jnp.einsum("cpyki,kji->cpykj", blocks_x, inv_x, preferred_element_type=jnp.float32)
    across = across.astype(jnp.bfloat16).reshape(con_local, 2, cols_local, full_side)
    arrived = lax.all_to_all(across, "grid", split_axis=3, concat_axis=2, tiled=True)
    count = arrived.shape[0]
    masked = arrived * sea_turned[None, None]
    blocks_y = masked.reshape(count, 2, nblocks, BLK, rows_local)
    solved = jnp.einsum("cpkiu,kji->cpukj", blocks_y, inv_y, preferred_element_type=jnp.float32)
    rhs_adjoint = solved.reshape(count, 2, rows_local, nblocks * BLK)
    local_inner = jnp.sum(rhs_adjoint * vel_float, axis=(0, 1))
    inner = lax.psum(local_inner.astype(jnp.bfloat16), "con").astype(jnp.float32)
    speed = jnp.sqrt(0.25 + squares)
    first = -0.5 * sea_float * speed * rhs_adjoint
    second = -0.5 * sea_float * weight_full * vel_float * inner / speed
    return first + second


def solution(mesh):
    return jax.shard_map(
        local,
        mesh=mesh,
        in_specs=(
            P("con", None, "grid", None),
            P("con", None, "grid", None),
            P("grid", None),
            P(),
            P(),
            P("con"),
        ),
        out_specs=P("con", None, "grid", None),
        check_vma=False,
    )
```

profile of v0, /device:TPU:48, one launch (start us, length us, event | category | flops | bytes accessed | tf_op | source)
XLA Modules:
  0.0 234.4 jit_solution(3635252358337494409)
XLA Ops:
  6.5 1.6 copy-done
  8.1 3.3 %convert_bitcast_fusion = bf16[2,2,64,32,128]{4,2,1,0,3:T(8,128)(2,1)} fusion(bf16[32,128,128]{2,1,0:T(8,128)(2,1)} %param.9, bf16[2,2,64,4096]{3,2,1,0:T(8,128)(2,1)S(1)} %copy-done), kind=kOutput, calls=%fused_computation.16 | convolution fusion | flops 269484032 | bytes 5242880 | tf_op jit(solution)/shard_map/cpyki,kji->cpykj/dot_general | solution.py:23
  11.4 10.0 %copy.22 = bf16[2,2,64,32,128]{2,1,0,4,3:T(2,128)(2,1)} copy(bf16[2,2,64,32,128]{4,2,1,0,3:T(8,128)(2,1)} %convert_bitcast_fusion) | data formatting | bytes 4194304 | tf_op jit(solution)/shard_map/reshape | solution.py:24
  21.4 9.8 %reshape.31 = bf16[64,2,8192]{2,1,0:T(2,128)(2,1)} reshape(bf16[4096,2,2,64]{3,2,1,0:T(2,128)(2,1)} %bitcast.46) | data formatting | bytes 4194304
  31.3 9.1 %all-to-all-start = ((bf16[64,2,8192]{2,1,0:T(2,128)(2,1)}), bf16[64,2,8192]{2,1,0:T(2,128)(2,1)}, u32[]{:S(2)}, u32[]{:S(2)}) async-start(bf16[64,2,8192]{2,1,0:T(2,128)(2,1)} %reshape.31), calls=%async_computation | async-start | bytes 4194304 | tf_op jit(solution)/shard_map/all_to_all | solution.py:25
  40.4 0.2 all-reduce.5.cloned.1.call-start
  40.6 1.4 broadcast_select_fusion
  42.2 0.9 copy.26
  43.1 22.7 %all-to-all-done = bf16[64,2,8192]{2,1,0:T(2,128)(2,1)} async-done(((bf16[64,2,8192]{2,1,0:T(2,128)(2,1)}), bf16[64,2,8192]{2,1,0:T(2,128)(2,1)}, u32[]{:S(2)}, u32[]{:S(2)}) %all-to-all-start) | async-done | bytes 2097184 | tf_op jit(solution)/shard_map/all_to_all | solution.py:25
  65.8 9.8 %reshape.32 = bf16[4096,2,2,64]{3,2,1,0:T(2,128)(2,1)} reshape(bf16[64,2,8192]{2,1,0:T(2,128)(2,1)} %all-to-all-done) | data formatting | bytes 4194304
  75.6 6.8 %copy.38 = bf16[2,2,64,64,64]{2,3,4,1,0:T(8,128)(2,1)} copy(bf16[2,2,64,64,64]{2,1,0,4,3:T(2,128)(2,1)} %bitcast.47) | data formatting | bytes 4194304 | tf_op jit(solution)/shard_map/all_to_all | solution.py:25
  82.4 6.2 %all_to_all.16 = bf16[2,2,32,128,64]{3,2,4,1,0:T(8,128)(2,1)} reshape(bf16[2,2,64,64,64]{3,2,4,1,0:T(8,128)(2,1)} %bitcast.48) | data formatting | bytes 4194304 | tf_op jit(solution)/shard_map/all_to_all | solution.py:25
  88.6 2.0 broadcast_multiply_fusion.1
  90.6 1.2 convolution_bitcast_fusion
  91.8 0.4 copy-done.3
  92.2 2.4 %fusion.4 = (bf16[64,4096]{1,0:T(8,128)(2,1)}, f32[64,4096]{1,0:T(8,128)}) fusion(bf16[2,2,64,4096]{3,2,1,0:T(8,128)(2,1)S(1)} %copy-done.3, f32[32,2,2,8,8,128]{5,4,3,2,1,0:T(8,128)S(1)} %convolution_bitcast_fusion, f32[2]{0:T(128)S(1)} %copy-done.5), kind=kLoop, calls=%fused_computation.8 | loop fusion | flops 5767168 | bytes 7864328 | tf_op jit(solution)/shard_map/reduce_sum | solution.py:31
  94.7 0.7 all-reduce.3.cloned.1.call-update
  95.4 1.6 broadcast_multiply_fusion
  97.0 55.1 %all-reduce.5.cloned.1.call-done = bf16[64,4096]{1,0:T(8,128)(2,1)} async-done(((bf16[64,4096]{1,0:T(8,128)(2,1)}), bf16[64,4096]{1,0:T(8,128)(2,1)}) %all-reduce.5.cloned.1.call-update) | async-done | bytes 524304 | tf_op jit(solution)/shard_map/psum | solution.py:32
  152.2 1.1 convert_element_type.25
  153.3 66.5 %all-reduce.3.cloned.1.call-done = f32[64,4096]{1,0:T(8,128)} async-done(((f32[64,4096]{1,0:T(8,128)}), f32[64,4096]{1,0:T(8,128)}) %all-reduce.3.cloned.1.call-update) | async-done | bytes 1048592 | tf_op jit(solution)/shard_map/psum | solution.py:18
  219.8 1.8 fusion.13
  221.6 0.1 copy-done.2
  221.7 5.9 %fusion.3 = f32[2,2,64,4096]{3,2,1,0:T(8,128)} fusion(bf16[2,2,64,4096]{3,2,1,0:T(8,128)(2,1)} %param.6, f32[32,2,2,8,8,128]{5,4,3,2,1,0:T(8,128)} %copy-done.1, f32[64,4096]{1,0:T(8,128)S(1)} %get-tuple-element.10, f32[64,4096]{1,0:T(8,128)S(1)} %convert_element_type.25, f32[2,64,4096]{2,1,0:T(8,128)S(1)} %copy-done.2, f32[64,4096]{1,0:T(8,128)S(1)} %get-tuple-element.9), kind=kLoop, calls=%fused_computation.7 | loop fusion | flops 6291456 | bytes 15728640 | tf_op jit(solution)/shard_map/add | solution.py:36
  (12 shorter events, 0.2 us)
Async XLA Ops:
  6.5 1.6 copy-start
  31.3 34.5 %all-to-all-start = ((bf16[64,2,8192]{2,1,0:T(2,128)(2,1)}), bf16[64,2,8192]{2,1,0:T(2,128)(2,1)}, u32[]{:S(2)}, u32[]{:S(2)}) async-start(bf16[64,2,8192]{2,1,0:T(2,128)(2,1)} %reshape.31), calls=%async_computation | async-start | bytes 4194304 | tf_op jit(solution)/shard_map/all_to_all | solution.py:25
  40.4 111.8 %all-reduce.5.cloned.1.call-start = ((), (), s32[]{:S(2)}) async-start(), calls=%async_computation.2 | async-start | bytes 1048576 | tf_op jit(solution)/shard_map/psum | solution.py:32
  88.6 2.0 copy-start.4
  90.6 1.6 copy-start.3
  90.6 1.6 copy-start.5
  92.2 2.4 %copy-start.1 = (f32[32,2,2,8,8,128]{5,4,3,2,1,0:T(8,128)}, f32[32,2,2,8,8,128]{5,4,3,2,1,0:T(8,128)S(1)}, u32[]{:S(2)}) copy-start(f32[32,2,2,8,8,128]{5,4,3,2,1,0:T(8,128)S(1)} %convolution_bitcast_fusion) | copy-start | bytes 12582916
  94.6 125.1 %all-reduce.3.cloned.1.call-start = ((), (), s32[]{:S(2)}) async-start(), calls=%async_computation.1 | async-start | bytes 2097152 | tf_op jit(solution)/shard_map/psum | solution.py:18
  219.8 1.9 copy-start.2
Sparse Core Ops, SparseCore 0:
  94.8 57.3 all-reduce.4
  154.8 64.9 all-reduce.2
where the time goes:
time: 238 us; the launch traced here: 234 us
  waiting for transfers between devices  145 us (61%)
  local copies, waits for them, and re-layouts  45.7 us (19%)
  other arithmetic  16.3 us (7%)
  between operations  13.5 us (6%)
  starting transfers between devices  9.38 us (4%)
  matrix products  4.45 us (2%)
    psum x1, waiting for transfers between devices, local(): squares = lax.psum(local_squares, 'con')  66.5 us
    psum x1, waiting for transfers between devices, local(): lax.psum(local_inner.astype(jnp.bfloat16), 'con').astype(jnp.float32)  55.1 us
    all_to_all x1, waiting for transfers between devices, local(): lax.all_to_all(across, 'grid', split_axis=3, concat_axis=2, tiled=True)  22.7 us
    unnamed x15, local copies, waits for them, and re-layouts  22.7 us
    all_to_all x2, local copies, waits for them, and re-layouts, local(): lax.all_to_all(across, 'grid', split_axis=3, concat_axis=2, tiled=True)  13 us
    reshape x1, local copies, waits for them, and re-layouts, local(): across.astype(jnp.bfloat16).reshape(con_local, 2, cols_local, full_side)  10 us
    all_to_all x1, starting transfers between devices, local(): lax.all_to_all(across, 'grid', split_axis=3, concat_axis=2, tiled=True)  9.11 us
    add x1, other arithmetic, local(): return first + second  5.88 us
  transfers between devices with their start and end apart: 3, of which 3 were waited for; matrix products, arithmetic and copies ran while one was open for 2% of the time, Pallas kernels for 0%

commit v1 on v0

--- a/solution.py
+++ b/solution.py
@@ -4,6 +4,26 @@
 from jax.sharding import PartitionSpec as P
 
 BLK = 128
+
+
+def con_sum(part, link_type):
+    count = lax.axis_size("con")
+    me = lax.axis_index("con")
+    rows = part.shape[0]
+    quarters = part.reshape((count, rows // count) + part.shape[1:])
+    total = lax.dynamic_index_in_dim(quarters, me, 0, keepdims=False).astype(jnp.float32)
+    for shift in range(1, count):
+        pairs = [(i, (i + shift) % count) for i in range(count)]
+        piece = lax.dynamic_index_in_dim(quarters, (me + shift) % count, 0, keepdims=False)
+        total = total + lax.ppermute(piece.astype(link_type), "con", pairs).astype(jnp.float32)
+    mine = total.astype(link_type)
+    pieces = [mine]
+    for shift in range(1, count):
+        pairs = [(i, (i + shift) % count) for i in range(count)]
+        pieces.append(lax.ppermute(mine, "con", pairs))
+    ordered = jnp.stack([pieces[(-t) % count] for t in range(count)])
+    gathered = jnp.roll(ordered, me, axis=0)
+    return gathered.reshape(part.shape).astype(jnp.float32)
 
 
 def local(velocity, seed_adjoint, land_mask, inv_x, inv_y, weights):
@@ -15,7 +35,8 @@
     vel_float = velocity.astype(jnp.float32)
     weight_full = weights[:, None, None, None]
     local_squares = jnp.sum(weight_full * vel_float * vel_float, axis=(0, 1))
-    squares = lax.psum(local_squares, "con")
+    local_squares, seed_adjoint = lax.optimization_barrier((local_squares, seed_adjoint))
+    squares = con_sum(local_squares, jnp.float32)
     sea_bool = land_mask == 1
     sea_float = sea_bool.astype(jnp.float32)
     sea_turned = jnp.swapaxes(sea_bool, 0, 1).astype(jnp.bfloat16)
@@ -29,7 +50,7 @@
     solved = jnp.einsum("cpkiu,kji->cpukj", blocks_y, inv_y, preferred_element_type=jnp.float32)
     rhs_adjoint = solved.reshape(count, 2, rows_local, nblocks * BLK)
     local_inner = jnp.sum(rhs_adjoint * vel_float, axis=(0, 1))
-    inner = lax.psum(local_inner.astype(jnp.bfloat16), "con").astype(jnp.float32)
+    inner = con_sum(local_inner, jnp.bfloat16)
     speed = jnp.sqrt(0.25 + squares)
     first = -0.5 * sea_float * speed * rhs_adjoint
     second = -0.5 * sea_float * weight_full * vel_float * inner / speed

time: 238 us -> 192 us (0.81)
  the two profiles are of different devices: /device:TPU:48 before, /device:TPU:72 now
where the time goes in v1:
time: 192 us; the launch traced here: 191 us
  waiting for transfers between devices  84.7 us (44%)
  local copies, waits for them, and re-layouts  50.1 us (26%)
  starting transfers between devices  39.4 us (21%)
  other arithmetic  13.2 us (7%)
  matrix products  3.26 us (2%)
    ppermute x6, waiting for transfers between devices, con_sum(): pieces.append(lax.ppermute(mine, 'con', pairs))  54 us
    ppermute x6, waiting for transfers between devices, con_sum(): lax.ppermute(piece.astype(link_type), 'con', pairs).astype(jnp.float32)  30.7 us
    unnamed x29, local copies, waits for them, and re-layouts  25.4 us
    ppermute x6, starting transfers between devices, con_sum(): lax.ppermute(piece.astype(link_type), 'con', pairs).astype(jnp.float32)  15.5 us
    ppermute x6, starting transfers between devices, con_sum(): pieces.append(lax.ppermute(mine, 'con', pairs))  13.6 us
    all_to_all x2, local copies, waits for them, and re-layouts, local(): lax.all_to_all(across, 'grid', split_axis=3, concat_axis=2, tiled=True)  13 us
    all_to_all x1, starting transfers between devices, local(): lax.all_to_all(across, 'grid', split_axis=3, concat_axis=2, tiled=True)  10.4 us
    reshape x1, local copies, waits for them, and re-layouts, local(): across.astype(jnp.bfloat16).reshape(con_local, 2, cols_local, full_side)  10 us
  transfers between devices with their start and end apart: 13, of which 6 were waited for; matrix products, arithmetic and copies ran while one was open for 16% of the time, Pallas kernels for 0%

profile of v1, /device:TPU:72, one launch (start us, length us, event | category | flops | bytes accessed | tf_op | source)
XLA Modules:
  0.0 191.0 jit_solution(8168276822233743305)
XLA Ops:
  0.0 2.5 %fusion = f32[64,4096]{1,0:T(8,128)S(1)} fusion(bf16[2,2,64,4096]{3,2,1,0:T(8,128)(2,1)} %param.6, f32[2]{0:T(128)} %param.11), kind=kLoop, calls=%fused_computation.4 | loop fusion | flops 3932160 | bytes 3145736 | tf_op jit(solution)/shard_map/reduce_sum | solution.py:37
  3.4 4.5 %collective-permute-start = (f32[16,4096]{1,0:T(8,128)}, f32[16,4096]{1,0:T(8,128)}, u32[]{:S(2)}, u32[]{:S(2)}) collective-permute-start(f32[16,4096]{1,0:T(8,128)} %get-tuple-element.18), channel_id=1, source_target_pairs={{0,64},{64,128},{128,192},{192,0},{1,65},{65,129},{129,193},{193,1... | collective-permute-start | bytes 786440 | tf_op jit(solution)/shard_map/ppermute | solution.py:18
  7.9 3.8 %collective-permute-start.1 = (f32[16,4096]{1,0:T(8,128)S(1)}, f32[16,4096]{1,0:T(8,128)}, u32[]{:S(2)}, u32[]{:S(2)}) collective-permute-start(f32[16,4096]{1,0:T(8,128)S(1)} %get-tuple-element.20), channel_id=1, source_target_pairs={{0,128},{64,192},{128,0},{192,64},{1,129},{65,193},{129,1},{193,65... | collective-permute-start | bytes 786440 | tf_op jit(solution)/shard_map/ppermute | solution.py:18
  11.7 13.7 %collective-permute-done = f32[16,4096]{1,0:T(8,128)} collective-permute-done((f32[16,4096]{1,0:T(8,128)}, f32[16,4096]{1,0:T(8,128)}, u32[]{:S(2)}, u32[]{:S(2)}) %collective-permute-start) | collective-permute-done | bytes 262176 | tf_op jit(solution)/shard_map/ppermute | solution.py:18
  25.4 9.5 %collective-permute-done.2 = f32[16,4096]{1,0:T(8,128)} collective-permute-done((f32[16,4096]{1,0:T(8,128)}, f32[16,4096]{1,0:T(8,128)}, u32[]{:S(2)}, u32[]{:S(2)}) %collective-permute-start.2) | collective-permute-done | bytes 262176 | tf_op jit(solution)/shard_map/ppermute | solution.py:18
  34.9 1.9 bitcast_dynamic-update-slice_fusion.6
  36.8 2.1 %convert_bitcast_fusion = bf16[2,2,64,32,128]{4,2,1,0,3:T(8,128)(2,1)} fusion(bf16[32,128,128]{2,1,0:T(8,128)(2,1)S(1)} %copy-done.3, bf16[2,2,64,4096]{3,2,1,0:T(8,128)(2,1)S(1)} %copy-done), kind=kOutput, calls=%fused_computation.16 | convolution fusion | flops 269484032 | bytes 5242880 | tf_op jit(solution)/shard_map/cpyki,kji->cpykj/dot_general | solution.py:44
  38.9 10.0 %copy.22 = bf16[2,2,64,32,128]{2,1,0,4,3:T(2,128)(2,1)} copy(bf16[2,2,64,32,128]{4,2,1,0,3:T(8,128)(2,1)} %convert_bitcast_fusion) | data formatting | bytes 4194304 | tf_op jit(solution)/shard_map/reshape | solution.py:45
  48.9 9.8 %reshape.59 = bf16[64,2,8192]{2,1,0:T(2,128)(2,1)} reshape(bf16[4096,2,2,64]{3,2,1,0:T(2,128)(2,1)} %bitcast.105) | data formatting | bytes 4194304
  58.8 10.4 %all-to-all-start = ((bf16[64,2,8192]{2,1,0:T(2,128)(2,1)}), bf16[64,2,8192]{2,1,0:T(2,128)(2,1)}, u32[]{:S(2)}, u32[]{:S(2)}) async-start(bf16[64,2,8192]{2,1,0:T(2,128)(2,1)} %reshape.59), calls=%async_computation | async-start | bytes 4194304 | tf_op jit(solution)/shard_map/all_to_all | solution.py:46
  69.1 2.0 %collective-permute-start.5 = (f32[16,4096]{1,0:T(8,128)S(1)}, f32[16,4096]{1,0:T(8,128)S(1)}, u32[]{:S(2)}, u32[]{:S(2)}) collective-permute-start(f32[16,4096]{1,0:T(8,128)S(1)} %get-tuple-element.14), channel_id=1, source_target_pairs={{0,64},{64,128},{128,192},{192,0},{1,65},{65,129},{129,193},{193,1... | collective-permute-start | bytes 786440 | tf_op jit(solution)/shard_map/ppermute | solution.py:23
  71.1 2.0 %collective-permute-start.4 = (f32[16,4096]{1,0:T(8,128)S(1)}, f32[16,4096]{1,0:T(8,128)S(1)}, u32[]{:S(2)}, u32[]{:S(2)}) collective-permute-start(f32[16,4096]{1,0:T(8,128)S(1)} %get-tuple-element.14), channel_id=1, source_target_pairs={{0,128},{64,192},{128,0},{192,64},{1,129},{65,193},{129,1},{193,65... | collective-permute-start | bytes 786440 | tf_op jit(solution)/shard_map/ppermute | solution.py:23
  73.8 46.0 %collective-permute-done.4 = f32[16,4096]{1,0:T(8,128)S(1)} collective-permute-done((f32[16,4096]{1,0:T(8,128)S(1)}, f32[16,4096]{1,0:T(8,128)S(1)}, u32[]{:S(2)}, u32[]{:S(2)}) %collective-permute-start.4) | collective-permute-done | bytes 262176 | tf_op jit(solution)/shard_map/ppermute | solution.py:23
  127.9 9.8 %reshape.60 = bf16[4096,2,2,64]{3,2,1,0:T(2,128)(2,1)} reshape(bf16[64,2,8192]{2,1,0:T(2,128)(2,1)} %all-to-all-done) | data formatting | bytes 4194304
  137.7 6.8 %copy.38 = bf16[2,2,64,64,64]{2,3,4,1,0:T(8,128)(2,1)} copy(bf16[2,2,64,64,64]{2,1,0,4,3:T(2,128)(2,1)} %bitcast.106) | data formatting | bytes 4194304 | tf_op jit(solution)/shard_map/all_to_all | solution.py:46
  144.5 6.2 %all_to_all.16 = bf16[2,2,32,128,64]{3,2,4,1,0:T(8,128)(2,1)} reshape(bf16[2,2,64,64,64]{3,2,4,1,0:T(8,128)(2,1)} %bitcast.107) | data formatting | bytes 4194304 | tf_op jit(solution)/shard_map/all_to_all | solution.py:46
  150.7 2.0 %broadcast_multiply_fusion.1 = bf16[2,2,32,128,64]{3,2,4,1,0:T(8,128)(2,1)S(1)} fusion(bf16[2,2,32,128,64]{3,2,4,1,0:T(8,128)(2,1)} %all_to_all.16, bf16[32,128,64]{1,0,2:T(8,128)(2,1)} %bitcast.113), kind=kLoop, calls=%fused_computation.20 | loop fusion | flops 1048576 | bytes 4718592 | tf_op jit(solution)/shard_map/mul | solution.py:48
  155.0 2.9 %collective-permute-start.8 = (bf16[16,4096]{1,0:T(8,128)(2,1)S(1)}, bf16[16,4096]{1,0:T(8,128)(2,1)S(1)}, u32[]{:S(2)}, u32[]{:S(2)}) collective-permute-start(bf16[16,4096]{1,0:T(8,128)(2,1)S(1)} %get-tuple-element.16), channel_id=1, source_target_pairs={{0,192},{64,0},{128,64},{192,128},{1,193},{65,1},{129,65},{193,129... | collective-permute-start | bytes 393224 | tf_op jit(solution)/shard_map/ppermute | solution.py:18
  157.9 4.2 %collective-permute-start.7 = (bf16[16,4096]{1,0:T(8,128)(2,1)S(1)}, bf16[16,4096]{1,0:T(8,128)(2,1)S(1)}, u32[]{:S(2)}, u32[]{:S(2)}) collective-permute-start(bf16[16,4096]{1,0:T(8,128)(2,1)S(1)} %get-tuple-element.17), channel_id=1, source_target_pairs={{0,128},{64,192},{128,0},{192,64},{1,129},{65,193},{129,1},{193,65... | collective-permute-start | bytes 393224 | tf_op jit(solution)/shard_map/ppermute | solution.py:18
  162.8 6.9 %collective-permute-done.7 = bf16[16,4096]{1,0:T(8,128)(2,1)S(1)} collective-permute-done((bf16[16,4096]{1,0:T(8,128)(2,1)S(1)}, bf16[16,4096]{1,0:T(8,128)(2,1)S(1)}, u32[]{:S(2)}, u32[]{:S(2)}) %collective-permute-start.7) | collective-permute-done | bytes 131104 | tf_op jit(solution)/shard_map/ppermute | solution.py:18
  170.1 4.2 %collective-permute-start.11 = (bf16[16,4096]{1,0:T(8,128)(2,1)S(1)}, bf16[16,4096]{1,0:T(8,128)(2,1)S(1)}, u32[]{:S(2)}, u32[]{:S(2)}) collective-permute-start(bf16[16,4096]{1,0:T(8,128)(2,1)S(1)} %get-tuple-element.12), channel_id=1, source_target_pairs={{0,64},{64,128},{128,192},{192,0},{1,65},{65,129},{129,193},{193,1... | collective-permute-start | bytes 393224 | tf_op jit(solution)/shard_map/ppermute | solution.py:23
  174.3 5.4 %collective-permute-start.10 = (bf16[16,4096]{1,0:T(8,128)(2,1)S(1)}, bf16[16,4096]{1,0:T(8,128)(2,1)S(1)}, u32[]{:S(2)}, u32[]{:S(2)}) collective-permute-start(bf16[16,4096]{1,0:T(8,128)(2,1)S(1)} %get-tuple-element.12), channel_id=1, source_target_pairs={{0,128},{64,192},{128,0},{192,64},{1,129},{65,193},{129,1},{193,65... | collective-permute-start | bytes 393224 | tf_op jit(solution)/shard_map/ppermute | solution.py:23
  179.7 8.0 %collective-permute-done.10 = bf16[16,4096]{1,0:T(8,128)(2,1)S(1)} collective-permute-done((bf16[16,4096]{1,0:T(8,128)(2,1)S(1)}, bf16[16,4096]{1,0:T(8,128)(2,1)S(1)}, u32[]{:S(2)}, u32[]{:S(2)}) %collective-permute-start.10) | collective-permute-done | bytes 131104 | tf_op jit(solution)/shard_map/ppermute | solution.py:23
  188.0 3.0 %fusion.3 = f32[2,2,64,4096]{3,2,1,0:T(8,128)} fusion(bf16[2,2,64,4096]{3,2,1,0:T(8,128)(2,1)S(1)} %copy-done.1, f32[32,2,2,8,8,128]{5,4,3,2,1,0:T(8,128)S(1)} %convolution_bitcast_fusion, f32[64,4096]{1,0:T(8,128)S(1)} %bitcast.108, f32[64,4096]{1,0:T(8,128)S(1)} %bitcast_convert_fusion, f32[2,64,4096]{2,1,0:T(8,128)S(1)} %broadcast_multiply_fusion, ...), kind=kLoop, calls=%fused_computation.7 | loop fusion | flops 6291456 | bytes 15728640 | tf_op jit(solution)/shard_map/add | solution.py:57
  (53 shorter events, 13.4 us)
Async XLA Ops:
  0.0 36.8 %copy-start = (bf16[2,2,64,4096]{3,2,1,0:T(8,128)(2,1)S(1)}, bf16[2,2,64,4096]{3,2,1,0:T(8,128)(2,1)}, u32[]{:S(2)}) copy-start(bf16[2,2,64,4096]{3,2,1,0:T(8,128)(2,1)} %param.7) | copy-start | bytes 6291460
  3.4 22.0 %collective-permute-start = (f32[16,4096]{1,0:T(8,128)}, f32[16,4096]{1,0:T(8,128)}, u32[]{:S(2)}, u32[]{:S(2)}) collective-permute-start(f32[16,4096]{1,0:T(8,128)} %get-tuple-element.18), channel_id=1, source_target_pairs={{0,64},{64,128},{128,192},{192,0},{1,65},{65,129},{129,193},{193,1... | collective-permute-start | bytes 786440 | tf_op jit(solution)/shard_map/ppermute | solution.py:18
  7.9 27.0 %collective-permute-start.2 = (f32[16,4096]{1,0:T(8,128)}, f32[16,4096]{1,0:T(8,128)}, u32[]{:S(2)}, u32[]{:S(2)}) collective-permute-start(f32[16,4096]{1,0:T(8,128)} %get-tuple-element.19), channel_id=1, source_target_pairs={{0,192},{64,0},{128,64},{192,128},{1,193},{65,1},{129,65},{193,129... | collective-permute-start | bytes 786440 | tf_op jit(solution)/shard_map/ppermute | solution.py:18
  7.9 27.0 %collective-permute-start.1 = (f32[16,4096]{1,0:T(8,128)S(1)}, f32[16,4096]{1,0:T(8,128)}, u32[]{:S(2)}, u32[]{:S(2)}) collective-permute-start(f32[16,4096]{1,0:T(8,128)S(1)} %get-tuple-element.20), channel_id=1, source_target_pairs={{0,128},{64,192},{128,0},{192,64},{1,129},{65,193},{129,1},{193,65... | collective-permute-start | bytes 786440 | tf_op jit(solution)/shard_map/ppermute | solution.py:18
  11.7 25.1 %copy-start.3 = (bf16[32,128,128]{2,1,0:T(8,128)(2,1)S(1)}, bf16[32,128,128]{2,1,0:T(8,128)(2,1)}, u32[]{:S(2)}) copy-start(bf16[32,128,128]{2,1,0:T(8,128)(2,1)} %param.9) | copy-start | bytes 3145732
  36.8 36.3 %collective-permute-start.3 = (f32[16,4096]{1,0:T(8,128)S(1)}, f32[16,4096]{1,0:T(8,128)S(1)}, u32[]{:S(2)}, u32[]{:S(2)}) collective-permute-start(f32[16,4096]{1,0:T(8,128)S(1)} %get-tuple-element.14), channel_id=1, source_target_pairs={{0,192},{64,0},{128,64},{192,128},{1,193},{65,1},{129,65},{193,129... | collective-permute-start | bytes 786440 | tf_op jit(solution)/shard_map/ppermute | solution.py:23
  58.8 69.1 %all-to-all-start = ((bf16[64,2,8192]{2,1,0:T(2,128)(2,1)}), bf16[64,2,8192]{2,1,0:T(2,128)(2,1)}, u32[]{:S(2)}, u32[]{:S(2)}) async-start(bf16[64,2,8192]{2,1,0:T(2,128)(2,1)} %reshape.59), calls=%async_computation | async-start | bytes 4194304 | tf_op jit(solution)/shard_map/all_to_all | solution.py:46
  69.1 51.4 %collective-permute-start.5 = (f32[16,4096]{1,0:T(8,128)S(1)}, f32[16,4096]{1,0:T(8,128)S(1)}, u32[]{:S(2)}, u32[]{:S(2)}) collective-permute-start(f32[16,4096]{1,0:T(8,128)S(1)} %get-tuple-element.14), channel_id=1, source_target_pairs={{0,64},{64,128},{128,192},{192,0},{1,65},{65,129},{129,193},{193,1... | collective-permute-start | bytes 786440 | tf_op jit(solution)/shard_map/ppermute | solution.py:23
  71.1 48.7 %collective-permute-start.4 = (f32[16,4096]{1,0:T(8,128)S(1)}, f32[16,4096]{1,0:T(8,128)S(1)}, u32[]{:S(2)}, u32[]{:S(2)}) collective-permute-start(f32[16,4096]{1,0:T(8,128)S(1)} %get-tuple-element.14), channel_id=1, source_target_pairs={{0,128},{64,192},{128,0},{192,64},{1,129},{65,193},{129,1},{193,65... | collective-permute-start | bytes 786440 | tf_op jit(solution)/shard_map/ppermute | solution.py:23
  121.2 4.4 %copy-start.5 = (s32[64,4096]{1,0:T(8,128)S(1)}, s32[64,4096]{1,0:T(8,128)}, u32[]{:S(2)}) copy-start(s32[64,4096]{1,0:T(8,128)} %param.8) | copy-start | bytes 3145732
  150.7 2.0 %copy-start.4 = (bf16[32,128,128]{2,1,0:T(8,128)(2,1)S(1)}, bf16[32,128,128]{2,1,0:T(8,128)(2,1)}, u32[]{:S(2)}) copy-start(bf16[32,128,128]{2,1,0:T(8,128)(2,1)} %param.10) | copy-start | bytes 3145732
  152.7 1.6 copy-start.1
  154.8 15.1 %copy-start.6 = (f32[2]{0:T(128)S(1)}, f32[2]{0:T(128)}, u32[]{:S(2)}) copy-start(f32[2]{0:T(128)} %param.11) | copy-start | bytes 28
  154.9 7.3 %collective-permute-start.6 = (bf16[16,4096]{1,0:T(8,128)(2,1)S(1)}, bf16[16,4096]{1,0:T(8,128)(2,1)S(1)}, u32[]{:S(2)}, u32[]{:S(2)}) collective-permute-start(bf16[16,4096]{1,0:T(8,128)(2,1)S(1)} %get-tuple-element.15), channel_id=1, source_target_pairs={{0,64},{64,128},{128,192},{192,0},{1,65},{65,129},{129,193},{193,1... | collective-permute-start | bytes 393224 | tf_op jit(solution)/shard_map/ppermute | solution.py:18
  155.0 7.9 %collective-permute-start.8 = (bf16[16,4096]{1,0:T(8,128)(2,1)S(1)}, bf16[16,4096]{1,0:T(8,128)(2,1)S(1)}, u32[]{:S(2)}, u32[]{:S(2)}) collective-permute-start(bf16[16,4096]{1,0:T(8,128)(2,1)S(1)} %get-tuple-element.16), channel_id=1, source_target_pairs={{0,192},{64,0},{128,64},{192,128},{1,193},{65,1},{129,65},{193,129... | collective-permute-start | bytes 393224 | tf_op jit(solution)/shard_map/ppermute | solution.py:18
  157.9 11.8 %collective-permute-start.7 = (bf16[16,4096]{1,0:T(8,128)(2,1)S(1)}, bf16[16,4096]{1,0:T(8,128)(2,1)S(1)}, u32[]{:S(2)}, u32[]{:S(2)}) collective-permute-start(bf16[16,4096]{1,0:T(8,128)(2,1)S(1)} %get-tuple-element.17), channel_id=1, source_target_pairs={{0,128},{64,192},{128,0},{192,64},{1,129},{65,193},{129,1},{193,65... | collective-permute-start | bytes 393224 | tf_op jit(solution)/shard_map/ppermute | solution.py:18
  169.8 9.9 %collective-permute-start.9 = (bf16[16,4096]{1,0:T(8,128)(2,1)S(1)}, bf16[16,4096]{1,0:T(8,128)(2,1)S(1)}, u32[]{:S(2)}, u32[]{:S(2)}) collective-permute-start(bf16[16,4096]{1,0:T(8,128)(2,1)S(1)} %get-tuple-element.12), channel_id=1, source_target_pairs={{0,192},{64,0},{128,64},{192,128},{1,193},{65,1},{129,65},{193,129... | collective-permute-start | bytes 393224 | tf_op jit(solution)/shard_map/ppermute | solution.py:23
  170.1 17.6 %collective-permute-start.11 = (bf16[16,4096]{1,0:T(8,128)(2,1)S(1)}, bf16[16,4096]{1,0:T(8,128)(2,1)S(1)}, u32[]{:S(2)}, u32[]{:S(2)}) collective-permute-start(bf16[16,4096]{1,0:T(8,128)(2,1)S(1)} %get-tuple-element.12), channel_id=1, source_target_pairs={{0,64},{64,128},{128,192},{192,0},{1,65},{65,129},{129,193},{193,1... | collective-permute-start | bytes 393224 | tf_op jit(solution)/shard_map/ppermute | solution.py:23
  174.3 13.4 %collective-permute-start.10 = (bf16[16,4096]{1,0:T(8,128)(2,1)S(1)}, bf16[16,4096]{1,0:T(8,128)(2,1)S(1)}, u32[]{:S(2)}, u32[]{:S(2)}) collective-permute-start(bf16[16,4096]{1,0:T(8,128)(2,1)S(1)} %get-tuple-element.12), channel_id=1, source_target_pairs={{0,128},{64,192},{128,0},{192,64},{1,129},{65,193},{129,1},{193,65... | collective-permute-start | bytes 393224 | tf_op jit(solution)/shard_map/ppermute | solution.py:23
  179.7 8.3 %copy-start.2 = (f32[64,4096]{1,0:T(8,128)S(1)}, f32[64,4096]{1,0:T(8,128)}, u32[]{:S(2)}) copy-start(f32[64,4096]{1,0:T(8,128)} %get-tuple-element.9) | copy-start | bytes 3145732

commit v2 on v1

--- a/solution.py
+++ b/solution.py
@@ -35,14 +35,14 @@
     vel_float = velocity.astype(jnp.float32)
     weight_full = weights[:, None, None, None]
     local_squares = jnp.sum(weight_full * vel_float * vel_float, axis=(0, 1))
-    local_squares, seed_adjoint = lax.optimization_barrier((local_squares, seed_adjoint))
-    squares = con_sum(local_squares, jnp.float32)
     sea_bool = land_mask == 1
     sea_float = sea_bool.astype(jnp.float32)
     sea_turned = jnp.swapaxes(sea_bool, 0, 1).astype(jnp.bfloat16)
     blocks_x = seed_adjoint.reshape(con_local, 2, cols_local, nblocks, BLK)
     across = jnp.einsum("cpyki,kji->cpykj", blocks_x, inv_x, preferred_element_type=jnp.float32)
     across = across.astype(jnp.bfloat16).reshape(con_local, 2, cols_local, full_side)
+    across, local_squares = lax.optimization_barrier((across, local_squares))
+    squares = con_sum(local_squares, jnp.bfloat16)
     arrived = lax.all_to_all(across, "grid", split_axis=3, concat_axis=2, tiled=True)
     count = arrived.shape[0]
     masked = arrived * sea_turned[None, None]

time: 192 us -> 167 us (0.87)
  the two profiles are of different devices: /device:TPU:72 before, /device:TPU:48 now
where the time goes in v2:
time: 167 us; the launch traced here: 164 us
  waiting for transfers between devices  61.1 us (37%)
  local copies, waits for them, and re-layouts  49 us (29%)
  starting transfers between devices  39.5 us (24%)
  other arithmetic  11.4 us (7%)
  matrix products  3.11 us (2%)
    ppermute x6, waiting for transfers between devices, con_sum(): lax.ppermute(piece.astype(link_type), 'con', pairs).astype(jnp.float32)  38.6 us
    unnamed x19, local copies, waits for them, and re-layouts  23.3 us
    ppermute x6, waiting for transfers between devices, con_sum(): pieces.append(lax.ppermute(mine, 'con', pairs))  22.5 us
    ppermute x6, starting transfers between devices, con_sum(): lax.ppermute(piece.astype(link_type), 'con', pairs).astype(jnp.float32)  16.6 us
    ppermute x6, starting transfers between devices, con_sum(): pieces.append(lax.ppermute(mine, 'con', pairs))  13.8 us
    all_to_all x2, local copies, waits for them, and re-layouts, local(): lax.all_to_all(across, 'grid', split_axis=3, concat_axis=2, tiled=True)  13 us
    optimization_barrier x1, local copies, waits for them, and re-layouts, local(): across, local_squares = lax.optimization_barrier((across, local_squares))  9.98 us
    all_to_all x1, starting transfers between devices, local(): lax.all_to_all(across, 'grid', split_axis=3, concat_axis=2, tiled=True)  9.11 us
  transfers between devices with their start and end apart: 13, of which 9 were waited for; matrix products, arithmetic and copies ran while one was open for 4% of the time, Pallas kernels for 0%

profile of v2, /device:TPU:48, one launch (start us, length us, event | category | flops | bytes accessed | tf_op | source)
XLA Modules:
  0.0 164.3 jit_solution(18258100601399318666)
XLA Ops:
  6.1 10.0 %copy.16 = bf16[2,2,64,4096]{2,1,0,3:T(2,128)(2,1)} copy(bf16[2,2,64,4096]{3,2,1,0:T(8,128)(2,1)} %bitcast.96) | data formatting | bytes 4194304 | tf_op jit(solution)/shard_map/optimization_barrier | solution.py:44
  16.1 9.8 %reshape.64 = bf16[64,2,8192]{2,1,0:T(2,128)(2,1)} reshape(bf16[4096,2,2,64]{3,2,1,0:T(2,128)(2,1)} %bitcast.92) | data formatting | bytes 4194304
  26.0 9.1 %all-to-all-start = ((bf16[64,2,8192]{2,1,0:T(2,128)(2,1)}), bf16[64,2,8192]{2,1,0:T(2,128)(2,1)}, u32[]{:S(2)}, u32[]{:S(2)}) async-start(bf16[64,2,8192]{2,1,0:T(2,128)(2,1)} %reshape.64), calls=%async_computation | async-start | bytes 4194304 | tf_op jit(solution)/shard_map/all_to_all | solution.py:46
  35.9 3.3 %collective-permute-start = (bf16[16,4096]{1,0:T(8,128)(2,1)}, bf16[16,4096]{1,0:T(8,128)(2,1)S(1)}, u32[]{:S(2)}, u32[]{:S(2)}) collective-permute-start(bf16[16,4096]{1,0:T(8,128)(2,1)} %get-tuple-element.15), channel_id=1, source_target_pairs={{0,64},{64,128},{128,192},{192,0},{1,65},{65,129},{129,193},{193,1... | collective-permute-start | bytes 393224 | tf_op jit(solution)/shard_map/ppermute | solution.py:18
  39.2 2.1 %collective-permute-start.2 = (bf16[16,4096]{1,0:T(8,128)(2,1)}, bf16[16,4096]{1,0:T(8,128)(2,1)S(1)}, u32[]{:S(2)}, u32[]{:S(2)}) collective-permute-start(bf16[16,4096]{1,0:T(8,128)(2,1)} %get-tuple-element.16), channel_id=1, source_target_pairs={{0,192},{64,0},{128,64},{192,128},{1,193},{65,1},{129,65},{193,129... | collective-permute-start | bytes 393224 | tf_op jit(solution)/shard_map/ppermute | solution.py:18
  41.3 5.0 %collective-permute-start.1 = (bf16[16,4096]{1,0:T(8,128)(2,1)S(1)}, bf16[16,4096]{1,0:T(8,128)(2,1)}, u32[]{:S(2)}, u32[]{:S(2)}) collective-permute-start(bf16[16,4096]{1,0:T(8,128)(2,1)S(1)} %get-tuple-element.17), channel_id=1, source_target_pairs={{0,128},{64,192},{128,0},{192,64},{1,129},{65,193},{129,1},{193,65... | collective-permute-start | bytes 393224 | tf_op jit(solution)/shard_map/ppermute | solution.py:18
  46.3 22.8 %collective-permute-done.2 = bf16[16,4096]{1,0:T(8,128)(2,1)S(1)} collective-permute-done((bf16[16,4096]{1,0:T(8,128)(2,1)}, bf16[16,4096]{1,0:T(8,128)(2,1)S(1)}, u32[]{:S(2)}, u32[]{:S(2)}) %collective-permute-start.2) | collective-permute-done | bytes 131104 | tf_op jit(solution)/shard_map/ppermute | solution.py:18
  69.1 5.8 %collective-permute-done.1 = bf16[16,4096]{1,0:T(8,128)(2,1)} collective-permute-done((bf16[16,4096]{1,0:T(8,128)(2,1)S(1)}, bf16[16,4096]{1,0:T(8,128)(2,1)}, u32[]{:S(2)}, u32[]{:S(2)}) %collective-permute-start.1) | collective-permute-done | bytes 131104 | tf_op jit(solution)/shard_map/ppermute | solution.py:18
  75.9 4.4 %collective-permute-start.5 = (bf16[16,4096]{1,0:T(8,128)(2,1)S(1)}, bf16[16,4096]{1,0:T(8,128)(2,1)S(1)}, u32[]{:S(2)}, u32[]{:S(2)}) collective-permute-start(bf16[16,4096]{1,0:T(8,128)(2,1)S(1)} %fusion.33), channel_id=1, source_target_pairs={{0,64},{64,128},{128,192},{192,0},{1,65},{65,129},{129,193},{193,1... | collective-permute-start | bytes 393224 | tf_op jit(solution)/shard_map/ppermute | solution.py:23
  80.2 3.7 %collective-permute-start.3 = (bf16[16,4096]{1,0:T(8,128)(2,1)S(1)}, bf16[16,4096]{1,0:T(8,128)(2,1)S(1)}, u32[]{:S(2)}, u32[]{:S(2)}) collective-permute-start(bf16[16,4096]{1,0:T(8,128)(2,1)S(1)} %fusion.33), channel_id=1, source_target_pairs={{0,192},{64,0},{128,64},{192,128},{1,193},{65,1},{129,65},{193,129... | collective-permute-start | bytes 393224 | tf_op jit(solution)/shard_map/ppermute | solution.py:23
  83.9 6.8 %collective-permute-done.5 = bf16[16,4096]{1,0:T(8,128)(2,1)S(1)} collective-permute-done((bf16[16,4096]{1,0:T(8,128)(2,1)S(1)}, bf16[16,4096]{1,0:T(8,128)(2,1)S(1)}, u32[]{:S(2)}, u32[]{:S(2)}) %collective-permute-start.5) | collective-permute-done | bytes 131104 | tf_op jit(solution)/shard_map/ppermute | solution.py:23
  90.7 4.8 %collective-permute-done.4 = bf16[16,4096]{1,0:T(8,128)(2,1)S(1)} collective-permute-done((bf16[16,4096]{1,0:T(8,128)(2,1)S(1)}, bf16[16,4096]{1,0:T(8,128)(2,1)S(1)}, u32[]{:S(2)}, u32[]{:S(2)}) %collective-permute-start.4) | collective-permute-done | bytes 131104 | tf_op jit(solution)/shard_map/ppermute | solution.py:23
  100.4 9.8 %reshape.65 = bf16[4096,2,2,64]{3,2,1,0:T(2,128)(2,1)} reshape(bf16[64,2,8192]{2,1,0:T(2,128)(2,1)} %all-to-all-done) | data formatting | bytes 4194304
  110.1 6.8 %copy.38 = bf16[2,2,64,64,64]{2,3,4,1,0:T(8,128)(2,1)} copy(bf16[2,2,64,64,64]{2,1,0,4,3:T(2,128)(2,1)} %bitcast.93) | data formatting | bytes 4194304 | tf_op jit(solution)/shard_map/all_to_all | solution.py:46
  117.0 6.2 %all_to_all.16 = bf16[2,2,32,128,64]{3,2,4,1,0:T(8,128)(2,1)} reshape(bf16[2,2,64,64,64]{3,2,4,1,0:T(8,128)(2,1)} %bitcast.94) | data formatting | bytes 4194304 | tf_op jit(solution)/shard_map/all_to_all | solution.py:46
  127.3 2.3 %collective-permute-start.6 = (bf16[16,4096]{1,0:T(8,128)(2,1)S(1)}, bf16[16,4096]{1,0:T(8,128)(2,1)S(1)}, u32[]{:S(2)}, u32[]{:S(2)}) collective-permute-start(bf16[16,4096]{1,0:T(8,128)(2,1)S(1)} %get-tuple-element.12), channel_id=1, source_target_pairs={{0,64},{64,128},{128,192},{192,0},{1,65},{65,129},{129,193},{193,1... | collective-permute-start | bytes 393224 | tf_op jit(solution)/shard_map/ppermute | solution.py:18
  131.5 2.0 %collective-permute-start.7 = (bf16[16,4096]{1,0:T(8,128)(2,1)S(1)}, bf16[16,4096]{1,0:T(8,128)(2,1)S(1)}, u32[]{:S(2)}, u32[]{:S(2)}) collective-permute-start(bf16[16,4096]{1,0:T(8,128)(2,1)S(1)} %get-tuple-element.14), channel_id=1, source_target_pairs={{0,128},{64,192},{128,0},{192,64},{1,129},{65,193},{129,1},{193,65... | collective-permute-start | bytes 393224 | tf_op jit(solution)/shard_map/ppermute | solution.py:18
  133.6 6.2 %collective-permute-done.6 = bf16[16,4096]{1,0:T(8,128)(2,1)S(1)} collective-permute-done((bf16[16,4096]{1,0:T(8,128)(2,1)S(1)}, bf16[16,4096]{1,0:T(8,128)(2,1)S(1)}, u32[]{:S(2)}, u32[]{:S(2)}) %collective-permute-start.6) | collective-permute-done | bytes 131104 | tf_op jit(solution)/shard_map/ppermute | solution.py:18
  139.8 3.8 %collective-permute-done.7 = bf16[16,4096]{1,0:T(8,128)(2,1)S(1)} collective-permute-done((bf16[16,4096]{1,0:T(8,128)(2,1)S(1)}, bf16[16,4096]{1,0:T(8,128)(2,1)S(1)}, u32[]{:S(2)}, u32[]{:S(2)}) %collective-permute-start.7) | collective-permute-done | bytes 131104 | tf_op jit(solution)/shard_map/ppermute | solution.py:18
  144.0 4.8 %collective-permute-start.10 = (bf16[16,4096]{1,0:T(8,128)(2,1)S(1)}, bf16[16,4096]{1,0:T(8,128)(2,1)S(1)}, u32[]{:S(2)}, u32[]{:S(2)}) collective-permute-start(bf16[16,4096]{1,0:T(8,128)(2,1)S(1)} %fusion.30), channel_id=1, source_target_pairs={{0,128},{64,192},{128,0},{192,64},{1,129},{65,193},{129,1},{193,65... | collective-permute-start | bytes 393224 | tf_op jit(solution)/shard_map/ppermute | solution.py:23
  149.7 5.1 %collective-permute-done.11 = bf16[16,4096]{1,0:T(8,128)(2,1)S(1)} collective-permute-done((bf16[16,4096]{1,0:T(8,128)(2,1)S(1)}, bf16[16,4096]{1,0:T(8,128)(2,1)S(1)}, u32[]{:S(2)}, u32[]{:S(2)}) %collective-permute-start.11) | collective-permute-done | bytes 131104 | tf_op jit(solution)/shard_map/ppermute | solution.py:23
  154.8 2.6 %collective-permute-done.10 = bf16[16,4096]{1,0:T(8,128)(2,1)S(1)} collective-permute-done((bf16[16,4096]{1,0:T(8,128)(2,1)S(1)}, bf16[16,4096]{1,0:T(8,128)(2,1)S(1)}, u32[]{:S(2)}, u32[]{:S(2)}) %collective-permute-start.10) | collective-permute-done | bytes 131104 | tf_op jit(solution)/shard_map/ppermute | solution.py:23
  157.4 3.2 %collective-permute-done.9 = bf16[16,4096]{1,0:T(8,128)(2,1)S(1)} collective-permute-done((bf16[16,4096]{1,0:T(8,128)(2,1)S(1)}, bf16[16,4096]{1,0:T(8,128)(2,1)S(1)}, u32[]{:S(2)}, u32[]{:S(2)}) %collective-permute-start.9) | collective-permute-done | bytes 131104 | tf_op jit(solution)/shard_map/ppermute | solution.py:23
  161.4 3.0 %fusion.3 = f32[2,2,64,4096]{3,2,1,0:T(8,128)} fusion(bf16[2,2,64,4096]{3,2,1,0:T(8,128)(2,1)S(1)} %copy-done.2, f32[32,2,2,8,8,128]{5,4,3,2,1,0:T(8,128)S(1)} %convolution_bitcast_fusion, f32[64,4096]{1,0:T(8,128)S(1)} %bitcast.95, f32[64,4096]{1,0:T(8,128)S(1)} %bitcast_convert_fusion, f32[2,64,4096]{2,1,0:T(8,128)S(1)} %broadcast_multiply_fusion, ...), kind=kLoop, calls=%fused_computation.7 | loop fusion | flops 6291456 | bytes 15728640 | tf_op jit(solution)/shard_map/add | solution.py:57
  (42 shorter events, 20.8 us)
Async XLA Ops:
  0.0 1.6 copy-start
  3.5 1.9 %copy-start.1 = (bf16[2,2,64,4096]{3,2,1,0:T(8,128)(2,1)S(1)}, bf16[2,2,64,4096]{3,2,1,0:T(8,128)(2,1)}, u32[]{:S(2)}) copy-start(bf16[2,2,64,4096]{3,2,1,0:T(8,128)(2,1)} %param.8) | copy-start | bytes 6291460
  3.5 1.9 %copy-start.7 = (f32[2]{0:T(128)S(1)}, f32[2]{0:T(128)}, u32[]{:S(2)}) copy-start(f32[2]{0:T(128)} %param.13) | copy-start | bytes 28
  26.0 74.4 %all-to-all-start = ((bf16[64,2,8192]{2,1,0:T(2,128)(2,1)}), bf16[64,2,8192]{2,1,0:T(2,128)(2,1)}, u32[]{:S(2)}, u32[]{:S(2)}) async-start(bf16[64,2,8192]{2,1,0:T(2,128)(2,1)} %reshape.64), calls=%async_computation | async-start | bytes 4194304 | tf_op jit(solution)/shard_map/all_to_all | solution.py:46
  35.9 10.4 %collective-permute-start = (bf16[16,4096]{1,0:T(8,128)(2,1)}, bf16[16,4096]{1,0:T(8,128)(2,1)S(1)}, u32[]{:S(2)}, u32[]{:S(2)}) collective-permute-start(bf16[16,4096]{1,0:T(8,128)(2,1)} %get-tuple-element.15), channel_id=1, source_target_pairs={{0,64},{64,128},{128,192},{192,0},{1,65},{65,129},{129,193},{193,1... | collective-permute-start | bytes 393224 | tf_op jit(solution)/shard_map/ppermute | solution.py:18
  39.2 30.0 %collective-permute-start.2 = (bf16[16,4096]{1,0:T(8,128)(2,1)}, bf16[16,4096]{1,0:T(8,128)(2,1)S(1)}, u32[]{:S(2)}, u32[]{:S(2)}) collective-permute-start(bf16[16,4096]{1,0:T(8,128)(2,1)} %get-tuple-element.16), channel_id=1, source_target_pairs={{0,192},{64,0},{128,64},{192,128},{1,193},{65,1},{129,65},{193,129... | collective-permute-start | bytes 393224 | tf_op jit(solution)/shard_map/ppermute | solution.py:18
  41.3 33.6 %collective-permute-start.1 = (bf16[16,4096]{1,0:T(8,128)(2,1)S(1)}, bf16[16,4096]{1,0:T(8,128)(2,1)}, u32[]{:S(2)}, u32[]{:S(2)}) collective-permute-start(bf16[16,4096]{1,0:T(8,128)(2,1)S(1)} %get-tuple-element.17), channel_id=1, source_target_pairs={{0,128},{64,192},{128,0},{192,64},{1,129},{65,193},{129,1},{193,65... | collective-permute-start | bytes 393224 | tf_op jit(solution)/shard_map/ppermute | solution.py:18
  75.9 14.8 %collective-permute-start.5 = (bf16[16,4096]{1,0:T(8,128)(2,1)S(1)}, bf16[16,4096]{1,0:T(8,128)(2,1)S(1)}, u32[]{:S(2)}, u32[]{:S(2)}) collective-permute-start(bf16[16,4096]{1,0:T(8,128)(2,1)S(1)} %fusion.33), channel_id=1, source_target_pairs={{0,64},{64,128},{128,192},{192,0},{1,65},{65,129},{129,193},{193,1... | collective-permute-start | bytes 393224 | tf_op jit(solution)/shard_map/ppermute | solution.py:23
  80.2 15.3 %collective-permute-start.4 = (bf16[16,4096]{1,0:T(8,128)(2,1)S(1)}, bf16[16,4096]{1,0:T(8,128)(2,1)S(1)}, u32[]{:S(2)}, u32[]{:S(2)}) collective-permute-start(bf16[16,4096]{1,0:T(8,128)(2,1)S(1)} %fusion.33), channel_id=1, source_target_pairs={{0,128},{64,192},{128,0},{192,64},{1,129},{65,193},{129,1},{193,65... | collective-permute-start | bytes 393224 | tf_op jit(solution)/shard_map/ppermute | solution.py:23
  80.2 15.3 %collective-permute-start.3 = (bf16[16,4096]{1,0:T(8,128)(2,1)S(1)}, bf16[16,4096]{1,0:T(8,128)(2,1)S(1)}, u32[]{:S(2)}, u32[]{:S(2)}) collective-permute-start(bf16[16,4096]{1,0:T(8,128)(2,1)S(1)} %fusion.33), channel_id=1, source_target_pairs={{0,192},{64,0},{128,64},{192,128},{1,193},{65,1},{129,65},{193,129... | collective-permute-start | bytes 393224 | tf_op jit(solution)/shard_map/ppermute | solution.py:23
  83.9 14.2 %copy-start.5 = (s32[64,4096]{1,0:T(8,128)S(1)}, s32[64,4096]{1,0:T(8,128)}, u32[]{:S(2)}) copy-start(s32[64,4096]{1,0:T(8,128)} %param.10) | copy-start | bytes 3145732
  95.6 0.7 copy-start.6
  123.2 2.0 %copy-start.4 = (bf16[32,128,128]{2,1,0:T(8,128)(2,1)S(1)}, bf16[32,128,128]{2,1,0:T(8,128)(2,1)}, u32[]{:S(2)}) copy-start(bf16[32,128,128]{2,1,0:T(8,128)(2,1)} %param.12) | copy-start | bytes 3145732
  125.2 1.6 copy-start.2
  127.3 12.5 %collective-permute-start.6 = (bf16[16,4096]{1,0:T(8,128)(2,1)S(1)}, bf16[16,4096]{1,0:T(8,128)(2,1)S(1)}, u32[]{:S(2)}, u32[]{:S(2)}) collective-permute-start(bf16[16,4096]{1,0:T(8,128)(2,1)S(1)} %get-tuple-element.12), channel_id=1, source_target_pairs={{0,64},{64,128},{128,192},{192,0},{1,65},{65,129},{129,193},{193,1... | collective-permute-start | bytes 393224 | tf_op jit(solution)/shard_map/ppermute | solution.py:18
  129.6 10.2 %collective-permute-start.8 = (bf16[16,4096]{1,0:T(8,128)(2,1)S(1)}, bf16[16,4096]{1,0:T(8,128)(2,1)S(1)}, u32[]{:S(2)}, u32[]{:S(2)}) collective-permute-start(bf16[16,4096]{1,0:T(8,128)(2,1)S(1)} %get-tuple-element.13), channel_id=1, source_target_pairs={{0,192},{64,0},{128,64},{192,128},{1,193},{65,1},{129,65},{193,129... | collective-permute-start | bytes 393224 | tf_op jit(solution)/shard_map/ppermute | solution.py:18
  131.5 12.1 %collective-permute-start.7 = (bf16[16,4096]{1,0:T(8,128)(2,1)S(1)}, bf16[16,4096]{1,0:T(8,128)(2,1)S(1)}, u32[]{:S(2)}, u32[]{:S(2)}) collective-permute-start(bf16[16,4096]{1,0:T(8,128)(2,1)S(1)} %get-tuple-element.14), channel_id=1, source_target_pairs={{0,128},{64,192},{128,0},{192,64},{1,129},{65,193},{129,1},{193,65... | collective-permute-start | bytes 393224 | tf_op jit(solution)/shard_map/ppermute | solution.py:18
  143.7 11.1 %collective-permute-start.11 = (bf16[16,4096]{1,0:T(8,128)(2,1)S(1)}, bf16[16,4096]{1,0:T(8,128)(2,1)S(1)}, u32[]{:S(2)}, u32[]{:S(2)}) collective-permute-start(bf16[16,4096]{1,0:T(8,128)(2,1)S(1)} %fusion.30), channel_id=1, source_target_pairs={{0,64},{64,128},{128,192},{192,0},{1,65},{65,129},{129,193},{193,1... | collective-permute-start | bytes 393224 | tf_op jit(solution)/shard_map/ppermute | solution.py:23
  144.0 13.4 %collective-permute-start.10 = (bf16[16,4096]{1,0:T(8,128)(2,1)S(1)}, bf16[16,4096]{1,0:T(8,128)(2,1)S(1)}, u32[]{:S(2)}, u32[]{:S(2)}) collective-permute-start(bf16[16,4096]{1,0:T(8,128)(2,1)S(1)} %fusion.30), channel_id=1, source_target_pairs={{0,128},{64,192},{128,0},{192,64},{1,129},{65,193},{129,1},{193,65... | collective-permute-start | bytes 393224 | tf_op jit(solution)/shard_map/ppermute | solution.py:23
  148.7 11.9 %collective-permute-start.9 = (bf16[16,4096]{1,0:T(8,128)(2,1)S(1)}, bf16[16,4096]{1,0:T(8,128)(2,1)S(1)}, u32[]{:S(2)}, u32[]{:S(2)}) collective-permute-start(bf16[16,4096]{1,0:T(8,128)(2,1)S(1)} %fusion.30), channel_id=1, source_target_pairs={{0,192},{64,0},{128,64},{192,128},{1,193},{65,1},{129,65},{193,129... | collective-permute-start | bytes 393224 | tf_op jit(solution)/shard_map/ppermute | solution.py:23
  149.7 11.7 %copy-start.3 = (f32[64,4096]{1,0:T(8,128)S(1)}, f32[64,4096]{1,0:T(8,128)}, u32[]{:S(2)}) copy-start(f32[64,4096]{1,0:T(8,128)} %get-tuple-element.10) | copy-start | bytes 3145732

commit v3 on v2

--- a/solution.py
+++ b/solution.py
@@ -1,9 +1,13 @@
 import jax
 import jax.numpy as jnp
 from jax import lax
+from jax.experimental import pallas as pl
+from jax.experimental.pallas import tpu as pltpu
 from jax.sharding import PartitionSpec as P
 
 BLK = 128
+GROUP = 4
+INTERPRET = False
 
 
 def con_sum(part, link_type):
@@ -26,8 +30,79 @@
     return gathered.reshape(part.shape).astype(jnp.float32)
 
 
+def x_solve_kernel(s_ref, w_ref, o_ref):
+    for b in range(w_ref.shape[0]):
+        block = s_ref[:, b * BLK:(b + 1) * BLK]
+        out = lax.dot_general(w_ref[b], block, (((1,), (1,)), ((), ())), preferred_element_type=jnp.float32)
+        o_ref[b * BLK:(b + 1) * BLK, :] = out.astype(o_ref.dtype)
+
+
+def x_solve(rows, inv_x):
+    lanes, side = rows.shape
+    nblocks = inv_x.shape[0]
+    return pl.pallas_call(
+        x_solve_kernel,
+        grid=(nblocks // GROUP,),
+        in_specs=[
+            pl.BlockSpec((lanes, GROUP * BLK), lambda g: (0, g)),
+            pl.BlockSpec((GROUP, BLK, BLK), lambda g: (g, 0, 0)),
+        ],
+        out_specs=pl.BlockSpec((GROUP * BLK, lanes), lambda g: (g, 0)),
+        out_shape=jax.ShapeDtypeStruct((side, lanes), jnp.bfloat16),
+        interpret=INTERPRET,
+    )(rows, inv_x)
+
+
+def y_solve_kernel(r_ref, m_ref, w_ref, v_ref, g_ref, i_ref):
+    half = r_ref.shape[0] // (2 * w_ref.shape[0])
+    count = v_ref.shape[0]
+    lane = lax.broadcasted_iota(jnp.int32, (half, BLK), 1)
+    low = lane < half
+    for b in range(w_ref.shape[0]):
+        cols = slice(b * BLK, (b + 1) * BLK)
+        sea = m_ref[:, cols] == 1
+        weight = w_ref[b]
+        total = jnp.zeros((half, BLK), jnp.float32)
+        for q in range(count):
+            tile = slice((q // 2) * BLK, (q // 2 + 1) * BLK)
+            first = r_ref[2 * b * half:(2 * b + 1) * half, tile].astype(jnp.float32)
+            second = r_ref[(2 * b + 1) * half:(2 * b + 2) * half, tile].astype(jnp.float32)
+            if q % 2 == 0:
+                joined = jnp.where(low, first, pltpu.roll(second, half, 1))
+            else:
+                joined = jnp.where(low, pltpu.roll(first, half, 1), second)
+            joined = jnp.where(sea, joined, 0.0).astype(jnp.bfloat16)
+            out = lax.dot_general(joined, weight, (((1,), (1,)), ((), ())), preferred_element_type=jnp.float32)
+            g_ref[q, :, cols] = out
+            total = total + out * v_ref[q, :, cols].astype(jnp.float32)
+        i_ref[:, cols] = total
+
+
+def y_solve(arrived, land_mask, inv_y, vel):
+    count, rows_local, side = vel.shape
+    nblocks = inv_y.shape[0]
+    return pl.pallas_call(
+        y_solve_kernel,
+        grid=(nblocks // GROUP,),
+        in_specs=[
+            pl.BlockSpec((GROUP * 2 * rows_local, arrived.shape[1]), lambda g: (g, 0)),
+            pl.BlockSpec((rows_local, GROUP * BLK), lambda g: (0, g)),
+            pl.BlockSpec((GROUP, BLK, BLK), lambda g: (g, 0, 0)),
+            pl.BlockSpec((count, rows_local, GROUP * BLK), lambda g: (0, 0, g)),
+        ],
+        out_specs=[
+            pl.BlockSpec((count, rows_local, GROUP * BLK), lambda g: (0, 0, g)),
+            pl.BlockSpec((rows_local, GROUP * BLK), lambda g: (0, g)),
+        ],
+        out_shape=[
+            jax.ShapeDtypeStruct((count, rows_local, side), jnp.float32),
+            jax.ShapeDtypeStruct((rows_local, side), jnp.float32),
+        ],
+        interpret=INTERPRET,
+    )(arrived, land_mask, inv_y, vel)
+
+
 def local(velocity, seed_adjoint, land_mask, inv_x, inv_y, weights):
-    nblocks = inv_x.shape[0]
     con_local = velocity.shape[0]
     cols_local = seed_adjoint.shape[2]
     full_side = seed_adjoint.shape[3]
@@ -35,21 +110,13 @@
     vel_float = velocity.astype(jnp.float32)
     weight_full = weights[:, None, None, None]
     local_squares = jnp.sum(weight_full * vel_float * vel_float, axis=(0, 1))
-    sea_bool = land_mask == 1
-    sea_float = sea_bool.astype(jnp.float32)
-    sea_turned = jnp.swapaxes(sea_bool, 0, 1).astype(jnp.bfloat16)
-    blocks_x = seed_adjoint.reshape(con_local, 2, cols_local, nblocks, BLK)
-    across = jnp.einsum("cpyki,kji->cpykj", blocks_x, inv_x, preferred_element_type=jnp.float32)
-    across = across.astype(jnp.bfloat16).reshape(con_local, 2, cols_local, full_side)
+    sea_float = (land_mask == 1).astype(jnp.float32)
+    across = x_solve(seed_adjoint.reshape(con_local * 2 * cols_local, full_side), inv_x)
     across, local_squares = lax.optimization_barrier((across, local_squares))
     squares = con_sum(local_squares, jnp.bfloat16)
-    arrived = lax.all_to_all(across, "grid", split_axis=3, concat_axis=2, tiled=True)
-    count = arrived.shape[0]
-    masked = arrived * sea_turned[None, None]
-    blocks_y = masked.reshape(count, 2, nblocks, BLK, rows_local)
-    solved = jnp.einsum("cpkiu,kji->cpukj", blocks_y, inv_y, preferred_element_type=jnp.float32)
-    rhs_adjoint = solved.reshape(count, 2, rows_local, nblocks * BLK)
-    local_inner = jnp.sum(rhs_adjoint * vel_float, axis=(0, 1))
+    arrived = lax.all_to_all(across, "grid", split_axis=0, concat_axis=0, tiled=True)
+    solved, local_inner = y_solve(arrived, land_mask, inv_y, velocity.reshape(con_local * 2, rows_local, full_side))
+    rhs_adjoint = solved.reshape(con_local, 2, rows_local, full_side)
     inner = con_sum(local_inner, jnp.bfloat16)
     speed = jnp.sqrt(0.25 + squares)
     first = -0.5 * sea_float * speed * rhs_adjoint

time: 167 us -> 135 us (0.81)
  the two profiles are of different devices: /device:TPU:48 before, /device:TPU:8 now
where the time goes in v3:
time: 135 us; the launch traced here: 134 us
  waiting for transfers between devices  56.1 us (42%)
  starting transfers between devices  46.7 us (35%)
  Pallas kernels  15.5 us (11%)
  other arithmetic  11.8 us (9%)
  local copies, waits for them, and re-layouts  3.91 us (3%)
    ppermute x6, waiting for transfers between devices, con_sum(): lax.ppermute(piece.astype(link_type), 'con', pairs).astype(jnp.float32)  34 us
    ppermute x6, waiting for transfers between devices, con_sum(): pieces.append(lax.ppermute(mine, 'con', pairs))  22 us
    ppermute x6, starting transfers between devices, con_sum(): lax.ppermute(piece.astype(link_type), 'con', pairs).astype(jnp.float32)  19.3 us
    ppermute x6, starting transfers between devices, con_sum(): pieces.append(lax.ppermute(mine, 'con', pairs))  18.1 us
    all_to_all x1, starting transfers between devices, local(): lax.all_to_all(across, 'grid', split_axis=0, concat_axis=0, tiled=True)  9.3 us
    pallas_call x1, Pallas kernels, y_solve(): pl.pallas_call(y_solve_kernel, grid=(nblocks // GROUP,), in_specs=[pl.Blo...  8.87 us
    pallas_call x1, Pallas kernels, x_solve(): pl.pallas_call(x_solve_kernel, grid=(nblocks // GROUP,), in_specs=[pl.Blo...  6.59 us
    add x1, other arithmetic, local(): return first + second  3.14 us
  transfers between devices with their start and end apart: 13, of which 9 were waited for; matrix products, arithmetic and copies ran while one was open for 4% of the time, Pallas kernels for 0%

profile of v3, /device:TPU:8, one launch (start us, length us, event | category | flops | bytes accessed | tf_op | source)
XLA Modules:
  0.0 134.1 jit_solution(2890369400375272906)
XLA Ops:
  0.0 2.4 %fusion.3 = f32[64,4096]{1,0:T(8,128)S(1)} fusion(bf16[2,2,64,4096]{3,2,1,0:T(8,128)(2,1)} %param.8, f32[2]{0:T(128)} %param.13), kind=kLoop, calls=%fused_computation.5 | loop fusion | flops 3932160 | bytes 3145736 | tf_op jit(solution)/shard_map/reduce_sum | solution.py:112
  2.4 6.6 %shard_map.64 = bf16[4096,256]{1,0:T(8,128)(2,1)} custom-call(bf16[256,4096]{1,0:T(8,128)(2,1)} %bitcast.55, bf16[32,128,128]{2,1,0:T(8,128)(2,1)} %w_ref.2), custom_call_target="tpu_custom_call" | custom-call | tf_op jit(solution)/shard_map/pallas_call | solution.py:43
  9.0 9.3 %all-to-all-start = ((bf16[64,64,256]{2,1,0:T(8,128)(2,1)}), bf16[64,64,256]{2,1,0:T(8,128)(2,1)S(1)}, u32[]{:S(2)}, u32[]{:S(2)}) async-start(bf16[64,64,256]{2,1,0:T(8,128)(2,1)} %bitcast.51), calls=%async_computation | async-start | bytes 4194304 | tf_op jit(solution)/shard_map/all_to_all | solution.py:117
  19.1 3.3 %collective-permute-start = (bf16[16,4096]{1,0:T(8,128)(2,1)}, bf16[16,4096]{1,0:T(8,128)(2,1)S(1)}, u32[]{:S(2)}, u32[]{:S(2)}) collective-permute-start(bf16[16,4096]{1,0:T(8,128)(2,1)} %get-tuple-element.19), channel_id=1, source_target_pairs={{0,64},{64,128},{128,192},{192,0},{1,65},{65,129},{129,193},{193,1... | collective-permute-start | bytes 393224 | tf_op jit(solution)/shard_map/ppermute | solution.py:22
  22.3 2.1 %collective-permute-start.2 = (bf16[16,4096]{1,0:T(8,128)(2,1)}, bf16[16,4096]{1,0:T(8,128)(2,1)S(1)}, u32[]{:S(2)}, u32[]{:S(2)}) collective-permute-start(bf16[16,4096]{1,0:T(8,128)(2,1)} %get-tuple-element.20), channel_id=1, source_target_pairs={{0,192},{64,0},{128,64},{192,128},{1,193},{65,1},{129,65},{193,129... | collective-permute-start | bytes 393224 | tf_op jit(solution)/shard_map/ppermute | solution.py:22
  24.5 5.0 %collective-permute-start.1 = (bf16[16,4096]{1,0:T(8,128)(2,1)S(1)}, bf16[16,4096]{1,0:T(8,128)(2,1)}, u32[]{:S(2)}, u32[]{:S(2)}) collective-permute-start(bf16[16,4096]{1,0:T(8,128)(2,1)S(1)} %get-tuple-element.21), channel_id=1, source_target_pairs={{0,128},{64,192},{128,0},{192,64},{1,129},{65,193},{129,1},{193,65... | collective-permute-start | bytes 393224 | tf_op jit(solution)/shard_map/ppermute | solution.py:22
  29.5 29.7 %collective-permute-done = bf16[16,4096]{1,0:T(8,128)(2,1)S(1)} collective-permute-done((bf16[16,4096]{1,0:T(8,128)(2,1)}, bf16[16,4096]{1,0:T(8,128)(2,1)S(1)}, u32[]{:S(2)}, u32[]{:S(2)}) %collective-permute-start) | collective-permute-done | bytes 131104 | tf_op jit(solution)/shard_map/ppermute | solution.py:22
  60.2 4.8 %collective-permute-start.5 = (bf16[16,4096]{1,0:T(8,128)(2,1)S(1)}, bf16[16,4096]{1,0:T(8,128)(2,1)S(1)}, u32[]{:S(2)}, u32[]{:S(2)}) collective-permute-start(bf16[16,4096]{1,0:T(8,128)(2,1)S(1)} %fusion.23), channel_id=1, source_target_pairs={{0,64},{64,128},{128,192},{192,0},{1,65},{65,129},{129,193},{193,1... | collective-permute-start | bytes 393224 | tf_op jit(solution)/shard_map/ppermute | solution.py:27
  66.4 2.2 %collective-permute-start.3 = (bf16[16,4096]{1,0:T(8,128)(2,1)S(1)}, bf16[16,4096]{1,0:T(8,128)(2,1)S(1)}, u32[]{:S(2)}, u32[]{:S(2)}) collective-permute-start(bf16[16,4096]{1,0:T(8,128)(2,1)S(1)} %fusion.23), channel_id=1, source_target_pairs={{0,192},{64,0},{128,64},{192,128},{1,193},{65,1},{129,65},{193,129... | collective-permute-start | bytes 393224 | tf_op jit(solution)/shard_map/ppermute | solution.py:27
  68.6 3.1 %collective-permute-done.5 = bf16[16,4096]{1,0:T(8,128)(2,1)S(1)} collective-permute-done((bf16[16,4096]{1,0:T(8,128)(2,1)S(1)}, bf16[16,4096]{1,0:T(8,128)(2,1)S(1)}, u32[]{:S(2)}, u32[]{:S(2)}) %collective-permute-start.5) | collective-permute-done | bytes 131104 | tf_op jit(solution)/shard_map/ppermute | solution.py:27
  71.7 7.0 %collective-permute-done.4 = bf16[16,4096]{1,0:T(8,128)(2,1)S(1)} collective-permute-done((bf16[16,4096]{1,0:T(8,128)(2,1)S(1)}, bf16[16,4096]{1,0:T(8,128)(2,1)S(1)}, u32[]{:S(2)}, u32[]{:S(2)}) %collective-permute-start.4) | collective-permute-done | bytes 131104 | tf_op jit(solution)/shard_map/ppermute | solution.py:27
  79.5 1.9 %add_sqrt_fusion = f32[4,16,4096]{2,1,0:T(8,128)S(1)} fusion(s32[]{:T(128)S(6)} %select_n.57, bf16[1,16,4096]{2,1,0:T(8,128)(2,1)S(1)} %bitcast.56, bf16[1,16,4096]{2,1,0:T(8,128)(2,1)} %bitcast.62, bf16[1,16,4096]{2,1,0:T(8,128)(2,1)S(1)} %bitcast.61, bf16[1,16,4096]{2,1,0:T(8,128)(2,1)S(1)} %bitcast.60), kind=kLoop, calls=%fused_computation.23 | loop fusion | flops 2359296 | bytes 1572868 | tf_op jit(solution)/shard_map/sqrt | solution.py:121
  82.7 8.9 %shard_map.65 = (f32[4,64,4096]{2,1,0:T(8,128)}, f32[64,4096]{1,0:T(8,128)}) custom-call(bf16[4096,256]{1,0:T(8,128)(2,1)} %bitcast.50, s32[64,4096]{1,0:T(8,128)} %m_ref.1, bf16[32,128,128]{2,1,0:T(8,128)(2,1)} %w_ref.3, bf16[4,64,4096]{2,1,0:T(8,128)(2,1)} %bitcast.48), custom_call_target="tpu_custom_call" | custom-call | tf_op jit(solution)/shard_map/pallas_call | solution.py:84
  92.7 2.7 %collective-permute-start.6 = (bf16[16,4096]{1,0:T(8,128)(2,1)S(1)}, bf16[16,4096]{1,0:T(8,128)(2,1)S(1)}, u32[]{:S(2)}, u32[]{:S(2)}) collective-permute-start(bf16[16,4096]{1,0:T(8,128)(2,1)S(1)} %get-tuple-element.16), channel_id=1, source_target_pairs={{0,64},{64,128},{128,192},{192,0},{1,65},{65,129},{129,193},{193,1... | collective-permute-start | bytes 393224 | tf_op jit(solution)/shard_map/ppermute | solution.py:22
  96.9 4.7 %collective-permute-start.7 = (bf16[16,4096]{1,0:T(8,128)(2,1)S(1)}, bf16[16,4096]{1,0:T(8,128)(2,1)S(1)}, u32[]{:S(2)}, u32[]{:S(2)}) collective-permute-start(bf16[16,4096]{1,0:T(8,128)(2,1)S(1)} %get-tuple-element.18), channel_id=1, source_target_pairs={{0,128},{64,192},{128,0},{192,64},{1,129},{65,193},{129,1},{193,65... | collective-permute-start | bytes 393224 | tf_op jit(solution)/shard_map/ppermute | solution.py:22
  103.1 1.6 %collective-permute-done.8 = bf16[16,4096]{1,0:T(8,128)(2,1)S(1)} collective-permute-done((bf16[16,4096]{1,0:T(8,128)(2,1)S(1)}, bf16[16,4096]{1,0:T(8,128)(2,1)S(1)}, u32[]{:S(2)}, u32[]{:S(2)}) %collective-permute-start.8) | collective-permute-done | bytes 131104 | tf_op jit(solution)/shard_map/ppermute | solution.py:22
  104.7 2.7 %collective-permute-done.7 = bf16[16,4096]{1,0:T(8,128)(2,1)S(1)} collective-permute-done((bf16[16,4096]{1,0:T(8,128)(2,1)S(1)}, bf16[16,4096]{1,0:T(8,128)(2,1)S(1)}, u32[]{:S(2)}, u32[]{:S(2)}) %collective-permute-start.7) | collective-permute-done | bytes 131104 | tf_op jit(solution)/shard_map/ppermute | solution.py:22
  108.4 6.0 %collective-permute-start.11 = (bf16[16,4096]{1,0:T(8,128)(2,1)S(1)}, bf16[16,4096]{1,0:T(8,128)(2,1)S(1)}, u32[]{:S(2)}, u32[]{:S(2)}) collective-permute-start(bf16[16,4096]{1,0:T(8,128)(2,1)S(1)} %fusion.20), channel_id=1, source_target_pairs={{0,64},{64,128},{128,192},{192,0},{1,65},{65,129},{129,193},{193,1... | collective-permute-start | bytes 393224 | tf_op jit(solution)/shard_map/ppermute | solution.py:27
  114.4 1.9 %collective-permute-start.10 = (bf16[16,4096]{1,0:T(8,128)(2,1)S(1)}, bf16[16,4096]{1,0:T(8,128)(2,1)S(1)}, u32[]{:S(2)}, u32[]{:S(2)}) collective-permute-start(bf16[16,4096]{1,0:T(8,128)(2,1)S(1)} %fusion.20), channel_id=1, source_target_pairs={{0,128},{64,192},{128,0},{192,64},{1,129},{65,193},{129,1},{193,65... | collective-permute-start | bytes 393224 | tf_op jit(solution)/shard_map/ppermute | solution.py:27
  116.3 1.8 %collective-permute-start.9 = (bf16[16,4096]{1,0:T(8,128)(2,1)S(1)}, bf16[16,4096]{1,0:T(8,128)(2,1)S(1)}, u32[]{:S(2)}, u32[]{:S(2)}) collective-permute-start(bf16[16,4096]{1,0:T(8,128)(2,1)S(1)} %fusion.20), channel_id=1, source_target_pairs={{0,192},{64,0},{128,64},{192,128},{1,193},{65,1},{129,65},{193,129... | collective-permute-start | bytes 393224 | tf_op jit(solution)/shard_map/ppermute | solution.py:27
  118.4 2.3 %collective-permute-done.11 = bf16[16,4096]{1,0:T(8,128)(2,1)S(1)} collective-permute-done((bf16[16,4096]{1,0:T(8,128)(2,1)S(1)}, bf16[16,4096]{1,0:T(8,128)(2,1)S(1)}, u32[]{:S(2)}, u32[]{:S(2)}) %collective-permute-start.11) | collective-permute-done | bytes 131104 | tf_op jit(solution)/shard_map/ppermute | solution.py:27
  120.7 7.3 %collective-permute-done.10 = bf16[16,4096]{1,0:T(8,128)(2,1)S(1)} collective-permute-done((bf16[16,4096]{1,0:T(8,128)(2,1)S(1)}, bf16[16,4096]{1,0:T(8,128)(2,1)S(1)}, u32[]{:S(2)}, u32[]{:S(2)}) %collective-permute-start.10) | collective-permute-done | bytes 131104 | tf_op jit(solution)/shard_map/ppermute | solution.py:27
  127.9 2.2 %collective-permute-done.9 = bf16[16,4096]{1,0:T(8,128)(2,1)S(1)} collective-permute-done((bf16[16,4096]{1,0:T(8,128)(2,1)S(1)}, bf16[16,4096]{1,0:T(8,128)(2,1)S(1)}, u32[]{:S(2)}, u32[]{:S(2)}) %collective-permute-start.9) | collective-permute-done | bytes 131104 | tf_op jit(solution)/shard_map/ppermute | solution.py:27
  130.9 3.1 %fusion.2 = f32[2,2,64,4096]{3,2,1,0:T(8,128)} fusion(bf16[2,2,64,4096]{3,2,1,0:T(8,128)(2,1)S(1)} %copy-done, f32[2,2,64,4096]{3,2,1,0:T(8,128)S(1)} %bitcast.52, f32[64,4096]{1,0:T(8,128)S(1)} %bitcast.49, f32[64,4096]{1,0:T(8,128)S(1)} %bitcast_convert_fusion, f32[2,64,4096]{2,1,0:T(8,128)S(1)} %broadcast_multiply_fusion, f32[64,4096]{1,0:T(8,128)S(1)} %get-tuple-element.14), kind=kLoop, calls=%fused_computation.4 | loop fusion | flops 6291456 | bytes 15728640 | tf_op jit(solution)/shard_map/add | solution.py:124
  (25 shorter events, 11.3 us)
Async XLA Ops:
  9.0 72.4 %all-to-all-start = ((bf16[64,64,256]{2,1,0:T(8,128)(2,1)}), bf16[64,64,256]{2,1,0:T(8,128)(2,1)S(1)}, u32[]{:S(2)}, u32[]{:S(2)}) async-start(bf16[64,64,256]{2,1,0:T(8,128)(2,1)} %bitcast.51), calls=%async_computation | async-start | bytes 4194304 | tf_op jit(solution)/shard_map/all_to_all | solution.py:117
  19.1 40.1 %collective-permute-start = (bf16[16,4096]{1,0:T(8,128)(2,1)}, bf16[16,4096]{1,0:T(8,128)(2,1)S(1)}, u32[]{:S(2)}, u32[]{:S(2)}) collective-permute-start(bf16[16,4096]{1,0:T(8,128)(2,1)} %get-tuple-element.19), channel_id=1, source_target_pairs={{0,64},{64,128},{128,192},{192,0},{1,65},{65,129},{129,193},{193,1... | collective-permute-start | bytes 393224 | tf_op jit(solution)/shard_map/ppermute | solution.py:22
  22.3 36.9 %collective-permute-start.2 = (bf16[16,4096]{1,0:T(8,128)(2,1)}, bf16[16,4096]{1,0:T(8,128)(2,1)S(1)}, u32[]{:S(2)}, u32[]{:S(2)}) collective-permute-start(bf16[16,4096]{1,0:T(8,128)(2,1)} %get-tuple-element.20), channel_id=1, source_target_pairs={{0,192},{64,0},{128,64},{192,128},{1,193},{65,1},{129,65},{193,129... | collective-permute-start | bytes 393224 | tf_op jit(solution)/shard_map/ppermute | solution.py:22
  24.5 34.7 %collective-permute-start.1 = (bf16[16,4096]{1,0:T(8,128)(2,1)S(1)}, bf16[16,4096]{1,0:T(8,128)(2,1)}, u32[]{:S(2)}, u32[]{:S(2)}) collective-permute-start(bf16[16,4096]{1,0:T(8,128)(2,1)S(1)} %get-tuple-element.21), channel_id=1, source_target_pairs={{0,128},{64,192},{128,0},{192,64},{1,129},{65,193},{129,1},{193,65... | collective-permute-start | bytes 393224 | tf_op jit(solution)/shard_map/ppermute | solution.py:22
  60.2 11.6 %collective-permute-start.5 = (bf16[16,4096]{1,0:T(8,128)(2,1)S(1)}, bf16[16,4096]{1,0:T(8,128)(2,1)S(1)}, u32[]{:S(2)}, u32[]{:S(2)}) collective-permute-start(bf16[16,4096]{1,0:T(8,128)(2,1)S(1)} %fusion.23), channel_id=1, source_target_pairs={{0,64},{64,128},{128,192},{192,0},{1,65},{65,129},{129,193},{193,1... | collective-permute-start | bytes 393224 | tf_op jit(solution)/shard_map/ppermute | solution.py:27
  64.9 13.8 %collective-permute-start.4 = (bf16[16,4096]{1,0:T(8,128)(2,1)S(1)}, bf16[16,4096]{1,0:T(8,128)(2,1)S(1)}, u32[]{:S(2)}, u32[]{:S(2)}) collective-permute-start(bf16[16,4096]{1,0:T(8,128)(2,1)S(1)} %fusion.23), channel_id=1, source_target_pairs={{0,128},{64,192},{128,0},{192,64},{1,129},{65,193},{129,1},{193,65... | collective-permute-start | bytes 393224 | tf_op jit(solution)/shard_map/ppermute | solution.py:27
  66.4 12.5 %collective-permute-start.3 = (bf16[16,4096]{1,0:T(8,128)(2,1)S(1)}, bf16[16,4096]{1,0:T(8,128)(2,1)S(1)}, u32[]{:S(2)}, u32[]{:S(2)}) collective-permute-start(bf16[16,4096]{1,0:T(8,128)(2,1)S(1)} %fusion.23), channel_id=1, source_target_pairs={{0,192},{64,0},{128,64},{192,128},{1,193},{65,1},{129,65},{193,129... | collective-permute-start | bytes 393224 | tf_op jit(solution)/shard_map/ppermute | solution.py:27
  78.8 0.6 copy-start.3
  81.3 1.3 copy-start.1
  91.6 26.5 %copy-start.4 = (f32[2]{0:T(128)S(1)}, f32[2]{0:T(128)}, u32[]{:S(2)}) copy-start(f32[2]{0:T(128)} %param.13) | copy-start | bytes 28
  92.7 10.3 %collective-permute-start.6 = (bf16[16,4096]{1,0:T(8,128)(2,1)S(1)}, bf16[16,4096]{1,0:T(8,128)(2,1)S(1)}, u32[]{:S(2)}, u32[]{:S(2)}) collective-permute-start(bf16[16,4096]{1,0:T(8,128)(2,1)S(1)} %get-tuple-element.16), channel_id=1, source_target_pairs={{0,64},{64,128},{128,192},{192,0},{1,65},{65,129},{129,193},{193,1... | collective-permute-start | bytes 393224 | tf_op jit(solution)/shard_map/ppermute | solution.py:22
  95.5 9.2 %collective-permute-start.8 = (bf16[16,4096]{1,0:T(8,128)(2,1)S(1)}, bf16[16,4096]{1,0:T(8,128)(2,1)S(1)}, u32[]{:S(2)}, u32[]{:S(2)}) collective-permute-start(bf16[16,4096]{1,0:T(8,128)(2,1)S(1)} %get-tuple-element.17), channel_id=1, source_target_pairs={{0,192},{64,0},{128,64},{192,128},{1,193},{65,1},{129,65},{193,129... | collective-permute-start | bytes 393224 | tf_op jit(solution)/shard_map/ppermute | solution.py:22
  96.9 10.5 %collective-permute-start.7 = (bf16[16,4096]{1,0:T(8,128)(2,1)S(1)}, bf16[16,4096]{1,0:T(8,128)(2,1)S(1)}, u32[]{:S(2)}, u32[]{:S(2)}) collective-permute-start(bf16[16,4096]{1,0:T(8,128)(2,1)S(1)} %get-tuple-element.18), channel_id=1, source_target_pairs={{0,128},{64,192},{128,0},{192,64},{1,129},{65,193},{129,1},{193,65... | collective-permute-start | bytes 393224 | tf_op jit(solution)/shard_map/ppermute | solution.py:22
  103.0 27.9 %copy-start = (bf16[2,2,64,4096]{3,2,1,0:T(8,128)(2,1)S(1)}, bf16[2,2,64,4096]{3,2,1,0:T(8,128)(2,1)}, u32[]{:S(2)}) copy-start(bf16[2,2,64,4096]{3,2,1,0:T(8,128)(2,1)} %param.8) | copy-start | bytes 6291460
  103.0 27.9 %copy-start.2 = (f32[4,64,4096]{2,1,0:T(8,128)S(1)}, f32[4,64,4096]{2,1,0:T(8,128)}, u32[]{:S(2)}) copy-start(f32[4,64,4096]{2,1,0:T(8,128)} %get-tuple-element.12) | copy-start | bytes 12582916
  108.4 12.2 %collective-permute-start.11 = (bf16[16,4096]{1,0:T(8,128)(2,1)S(1)}, bf16[16,4096]{1,0:T(8,128)(2,1)S(1)}, u32[]{:S(2)}, u32[]{:S(2)}) collective-permute-start(bf16[16,4096]{1,0:T(8,128)(2,1)S(1)} %fusion.20), channel_id=1, source_target_pairs={{0,64},{64,128},{128,192},{192,0},{1,65},{65,129},{129,193},{193,1... | collective-permute-start | bytes 393224 | tf_op jit(solution)/shard_map/ppermute | solution.py:27
  114.4 13.5 %collective-permute-start.10 = (bf16[16,4096]{1,0:T(8,128)(2,1)S(1)}, bf16[16,4096]{1,0:T(8,128)(2,1)S(1)}, u32[]{:S(2)}, u32[]{:S(2)}) collective-permute-start(bf16[16,4096]{1,0:T(8,128)(2,1)S(1)} %fusion.20), channel_id=1, source_target_pairs={{0,128},{64,192},{128,0},{192,64},{1,129},{65,193},{129,1},{193,65... | collective-permute-start | bytes 393224 | tf_op jit(solution)/shard_map/ppermute | solution.py:27
  116.3 13.8 %collective-permute-start.9 = (bf16[16,4096]{1,0:T(8,128)(2,1)S(1)}, bf16[16,4096]{1,0:T(8,128)(2,1)S(1)}, u32[]{:S(2)}, u32[]{:S(2)}) collective-permute-start(bf16[16,4096]{1,0:T(8,128)(2,1)S(1)} %fusion.20), channel_id=1, source_target_pairs={{0,192},{64,0},{128,64},{192,128},{1,193},{65,1},{129,65},{193,129... | collective-permute-start | bytes 393224 | tf_op jit(solution)/shard_map/ppermute | solution.py:27

commit v4 on v3

--- a/solution.py
+++ b/solution.py
@@ -12,21 +12,12 @@
 
 def con_sum(part, link_type):
     count = lax.axis_size("con")
-    me = lax.axis_index("con")
     rows = part.shape[0]
-    quarters = part.reshape((count, rows // count) + part.shape[1:])
-    total = lax.dynamic_index_in_dim(quarters, me, 0, keepdims=False).astype(jnp.float32)
-    for shift in range(1, count):
-        pairs = [(i, (i + shift) % count) for i in range(count)]
-        piece = lax.dynamic_index_in_dim(quarters, (me + shift) % count, 0, keepdims=False)
-        total = total + lax.ppermute(piece.astype(link_type), "con", pairs).astype(jnp.float32)
-    mine = total.astype(link_type)
-    pieces = [mine]
-    for shift in range(1, count):
-        pairs = [(i, (i + shift) % count) for i in range(count)]
-        pieces.append(lax.ppermute(mine, "con", pairs))
-    ordered = jnp.stack([pieces[(-t) % count] for t in range(count)])
-    gathered = jnp.roll(ordered, me, axis=0)
+    quarters = part.astype(link_type).reshape((count, rows // count) + part.shape[1:])
+    arrived = lax.all_to_all(quarters, "con", 0, 0, tiled=True)
+    mine = jnp.sum(arrived.astype(jnp.float32), axis=0).astype(link_type)
+    spread = jnp.broadcast_to(mine[None], (count,) + mine.shape)
+    gathered = lax.all_to_all(spread, "con", 0, 0, tiled=True)
     return gathered.reshape(part.shape).astype(jnp.float32)
 
 

time: 135 us -> 152 us (1.13)
  the two profiles are of different devices: /device:TPU:8 before, /device:TPU:36 now
where the time goes in v4:
time: 152 us; the launch traced here: 151 us
  waiting for transfers between devices  53 us (35%)
  blocking collectives  41.1 us (27%)
  other arithmetic  20 us (13%)
  starting transfers between devices  18.8 us (12%)
  Pallas kernels  15.5 us (10%)
  local copies, waits for them, and re-layouts  2.24 us (1%)
    all_to_all x1, waiting for transfers between devices, local(): lax.all_to_all(across, 'grid', split_axis=0, concat_axis=0, tiled=True)  26.1 us
    all_to_all x1, blocking collectives, con_sum(): arrived = lax.all_to_all(quarters, 'con', 0, 0, tiled=True)  24.1 us
    all_to_all x1, blocking collectives, con_sum(): gathered = lax.all_to_all(spread, 'con', 0, 0, tiled=True)  17 us
    all_to_all x1, waiting for transfers between devices, con_sum(): arrived = lax.all_to_all(quarters, 'con', 0, 0, tiled=True)  14.4 us
    all_to_all x1, waiting for transfers between devices, con_sum(): gathered = lax.all_to_all(spread, 'con', 0, 0, tiled=True)  12.5 us
    all_to_all x1, starting transfers between devices, local(): lax.all_to_all(across, 'grid', split_axis=0, concat_axis=0, tiled=True)  10.4 us
    pallas_call x1, Pallas kernels, y_solve(): pl.pallas_call(y_solve_kernel, grid=(nblocks // GROUP,), in_specs=[pl.Blo...  8.87 us
    pallas_call x1, Pallas kernels, x_solve(): pl.pallas_call(x_solve_kernel, grid=(nblocks // GROUP,), in_specs=[pl.Blo...  6.59 us
  transfers between devices with their start and end apart: 3, of which 3 were waited for; matrix products, arithmetic and copies ran while one was open for 5% of the time, Pallas kernels for 0%

profile of v4, /device:TPU:36, one launch (start us, length us, event | category | flops | bytes accessed | tf_op | source)
XLA Modules:
  0.0 150.6 jit_solution(3545023605842176476)
XLA Ops:
  0.0 2.3 %fusion.3 = bf16[64,4096]{1,0:T(8,128)(2,1)S(1)} fusion(bf16[2,2,64,4096]{3,2,1,0:T(8,128)(2,1)} %param.6, f32[2]{0:T(128)} %param.11), kind=kLoop, calls=%fused_computation.5 | loop fusion | flops 3932160 | bytes 2621448 | tf_op jit(solution)/shard_map/reduce_sum | solution.py:103
  2.3 6.6 %shard_map.64 = bf16[4096,256]{1,0:T(8,128)(2,1)} custom-call(bf16[256,4096]{1,0:T(8,128)(2,1)} %bitcast.17, bf16[32,128,128]{2,1,0:T(8,128)(2,1)} %w_ref.2), custom_call_target="tpu_custom_call" | custom-call | tf_op jit(solution)/shard_map/pallas_call | solution.py:34
  8.9 24.1 %all_to_all.31 = bf16[4,16,4096]{2,1,0:T(8,128)(2,1)S(1)} all-to-all(bf16[4,16,4096]{2,1,0:T(8,128)(2,1)S(1)} %bitcast.18), channel_id=1, replica_groups=mesh['con'=4,'grid'=64] {'con'}, dimensions={0} | all-to-all | bytes 1048576 | tf_op jit(solution)/shard_map/all_to_all | solution.py:17
  32.9 0.1 reduce_sum.34
  33.0 17.0 %all_to_all.32 = bf16[4,16,4096]{2,1,0:T(8,128)(2,1)} all-to-all(bf16[4,16,4096]{2,1,0:T(8,128)(2,1)S(1)} %broadcast_in_dim.4), channel_id=1, replica_groups=mesh['con'=4,'grid'=64] {'con'}, dimensions={0} | all-to-all | bytes 1048576 | tf_op jit(solution)/shard_map/all_to_all | solution.py:20
  50.1 10.4 %all-to-all-start.2 = ((bf16[64,64,256]{2,1,0:T(8,128)(2,1)}), bf16[64,64,256]{2,1,0:T(8,128)(2,1)S(1)}, u32[]{:S(2)}, u32[]{:S(2)}) async-start(bf16[64,64,256]{2,1,0:T(8,128)(2,1)} %bitcast.15), calls=%async_computation.2 | async-start | bytes 4194304 | tf_op jit(solution)/shard_map/all_to_all | solution.py:108
  60.4 1.4 add_sqrt_fusion
  61.8 26.1 %all-to-all-done.2 = bf16[64,64,256]{2,1,0:T(8,128)(2,1)S(1)} async-done(((bf16[64,64,256]{2,1,0:T(8,128)(2,1)}), bf16[64,64,256]{2,1,0:T(8,128)(2,1)S(1)}, u32[]{:S(2)}, u32[]{:S(2)}) %all-to-all-start.2) | async-done | bytes 2097184 | tf_op jit(solution)/shard_map/all_to_all | solution.py:108
  87.8 0.0 copy-start.1
  87.9 1.3 copy-done.1
  89.2 8.9 %shard_map.65 = (f32[4,64,4096]{2,1,0:T(8,128)}, f32[64,4096]{1,0:T(8,128)}) custom-call(bf16[4096,256]{1,0:T(8,128)(2,1)} %bitcast.14, s32[64,4096]{1,0:T(8,128)} %m_ref.1, bf16[32,128,128]{2,1,0:T(8,128)(2,1)} %w_ref.3, bf16[4,64,4096]{2,1,0:T(8,128)(2,1)} %bitcast.12), custom_call_target="tpu_custom_call" | custom-call | tf_op jit(solution)/shard_map/pallas_call | solution.py:75
  98.1 2.1 %convert_element_type.35 = bf16[64,4096]{1,0:T(8,128)(2,1)} convert(f32[64,4096]{1,0:T(8,128)} %get-tuple-element.12) | non-fusion elementwise | flops 262144 | bytes 1572864 | tf_op jit(solution)/shard_map/convert_element_type | solution.py:16
  100.1 4.3 %all-to-all-start.3 = ((bf16[4,16,4096]{2,1,0:T(8,128)(2,1)}), bf16[4,16,4096]{2,1,0:T(8,128)(2,1)}, u32[]{:S(2)}, u32[]{:S(2)}) async-start(bf16[4,16,4096]{2,1,0:T(8,128)(2,1)} %bitcast.7), calls=%async_computation.3 | async-start | bytes 1048576 | tf_op jit(solution)/shard_map/all_to_all | solution.py:17
  104.4 2.8 %bitcast_multiply_fusion = (f32[64,4096]{1,0:T(8,128)}, f32[64,4096]{1,0:T(8,128)}) fusion(f32[4,16,4096]{2,1,0:T(8,128)S(1)} %add_sqrt_fusion, s32[64,4096]{1,0:T(8,128)} %m_ref.1), kind=kLoop, calls=%fused_computation.10 | loop fusion | flops 786432 | bytes 4194304 | tf_op jit(solution)/shard_map/mul | solution.py:113
  107.2 14.4 %all-to-all-done.3 = bf16[4,16,4096]{2,1,0:T(8,128)(2,1)} async-done(((bf16[4,16,4096]{2,1,0:T(8,128)(2,1)}), bf16[4,16,4096]{2,1,0:T(8,128)(2,1)}, u32[]{:S(2)}, u32[]{:S(2)}) %all-to-all-start.3) | async-done | bytes 524320 | tf_op jit(solution)/shard_map/all_to_all | solution.py:17
  121.6 1.1 reduce_sum.35
  122.7 0.9 broadcast_in_dim.5
  123.6 4.1 %all-to-all-start.4 = ((bf16[4,16,4096]{2,1,0:T(8,128)(2,1)}), bf16[4,16,4096]{2,1,0:T(8,128)(2,1)}, u32[]{:S(2)}, u32[]{:S(2)}) async-start(bf16[4,16,4096]{2,1,0:T(8,128)(2,1)} %broadcast_in_dim.5), calls=%async_computation.4 | async-start | bytes 1048576 | tf_op jit(solution)/shard_map/all_to_all | solution.py:20
  127.7 0.0 copy-done.2
  127.8 2.8 %broadcast_multiply_fusion = f32[2,64,4096]{2,1,0:T(8,128)} fusion(f32[2]{0:T(128)S(1)} %copy-done.2, f32[64,4096]{1,0:T(8,128)} %get-tuple-element.14), kind=kLoop, calls=%fused_computation.6 | loop fusion | flops 524288 | bytes 3145736 | tf_op jit(solution)/shard_map/mul | solution.py:114
  130.6 12.5 %all-to-all-done.4 = bf16[4,16,4096]{2,1,0:T(8,128)(2,1)} async-done(((bf16[4,16,4096]{2,1,0:T(8,128)(2,1)}), bf16[4,16,4096]{2,1,0:T(8,128)(2,1)}, u32[]{:S(2)}, u32[]{:S(2)}) %all-to-all-start.4) | async-done | bytes 524320 | tf_op jit(solution)/shard_map/all_to_all | solution.py:20
  143.1 1.1 bitcast_convert_fusion
  144.2 0.0 copy-done
  144.2 6.4 %fusion.2 = f32[2,2,64,4096]{3,2,1,0:T(8,128)} fusion(bf16[2,2,64,4096]{3,2,1,0:T(8,128)(2,1)S(1)} %copy-done, f32[2,2,64,4096]{3,2,1,0:T(8,128)} %bitcast.16, f32[64,4096]{1,0:T(8,128)S(1)} %bitcast.13, f32[64,4096]{1,0:T(8,128)S(1)} %bitcast_convert_fusion, f32[2,64,4096]{2,1,0:T(8,128)} %broadcast_multiply_fusion, f32[64,4096]{1,0:T(8,128)} %get-tuple-element.13), kind=kLoop, calls=%fused_computation.4 | loop fusion | flops 6291456 | bytes 15728640 | tf_op jit(solution)/shard_map/add | solution.py:115
  (3 shorter events, 0.0 us)
Async XLA Ops:
  50.1 37.8 %all-to-all-start.2 = ((bf16[64,64,256]{2,1,0:T(8,128)(2,1)}), bf16[64,64,256]{2,1,0:T(8,128)(2,1)S(1)}, u32[]{:S(2)}, u32[]{:S(2)}) async-start(bf16[64,64,256]{2,1,0:T(8,128)(2,1)} %bitcast.15), calls=%async_computation.2 | async-start | bytes 4194304 | tf_op jit(solution)/shard_map/all_to_all | solution.py:108
  87.8 1.3 copy-start.1
  100.1 27.6 %copy-start.2 = (f32[2]{0:T(128)S(1)}, f32[2]{0:T(128)}, u32[]{:S(2)}) copy-start(f32[2]{0:T(128)} %param.11) | copy-start | bytes 28
  100.1 21.5 %all-to-all-start.3 = ((bf16[4,16,4096]{2,1,0:T(8,128)(2,1)}), bf16[4,16,4096]{2,1,0:T(8,128)(2,1)}, u32[]{:S(2)}, u32[]{:S(2)}) async-start(bf16[4,16,4096]{2,1,0:T(8,128)(2,1)} %bitcast.7), calls=%async_computation.3 | async-start | bytes 1048576 | tf_op jit(solution)/shard_map/all_to_all | solution.py:17
  107.2 37.0 %copy-start = (bf16[2,2,64,4096]{3,2,1,0:T(8,128)(2,1)S(1)}, bf16[2,2,64,4096]{3,2,1,0:T(8,128)(2,1)}, u32[]{:S(2)}) copy-start(bf16[2,2,64,4096]{3,2,1,0:T(8,128)(2,1)} %param.6) | copy-start | bytes 6291460
  123.6 19.5 %all-to-all-start.4 = ((bf16[4,16,4096]{2,1,0:T(8,128)(2,1)}), bf16[4,16,4096]{2,1,0:T(8,128)(2,1)}, u32[]{:S(2)}, u32[]{:S(2)}) async-start(bf16[4,16,4096]{2,1,0:T(8,128)(2,1)} %broadcast_in_dim.5), calls=%async_computation.4 | async-start | bytes 1048576 | tf_op jit(solution)/shard_map/all_to_all | solution.py:20

commit v5 on v3

--- a/solution.py
+++ b/solution.py
@@ -112,12 +112,11 @@
     local_squares = jnp.sum(weight_full * vel_float * vel_float, axis=(0, 1))
     sea_float = (land_mask == 1).astype(jnp.float32)
     across = x_solve(seed_adjoint.reshape(con_local * 2 * cols_local, full_side), inv_x)
-    across, local_squares = lax.optimization_barrier((across, local_squares))
-    squares = con_sum(local_squares, jnp.bfloat16)
     arrived = lax.all_to_all(across, "grid", split_axis=0, concat_axis=0, tiled=True)
     solved, local_inner = y_solve(arrived, land_mask, inv_y, velocity.reshape(con_local * 2, rows_local, full_side))
     rhs_adjoint = solved.reshape(con_local, 2, rows_local, full_side)
-    inner = con_sum(local_inner, jnp.bfloat16)
+    both = con_sum(jnp.concatenate([local_squares, local_inner], axis=0), jnp.bfloat16)
+    squares, inner = both[:rows_local], both[rows_local:]
     speed = jnp.sqrt(0.25 + squares)
     first = -0.5 * sea_float * speed * rhs_adjoint
     second = -0.5 * sea_float * weight_full * vel_float * inner / speed

time: 135 us -> 129 us (0.956)
  the two profiles are of different devices: /device:TPU:8 before, /device:TPU:70 now
where the time goes in v5:
time: 129 us; the launch traced here: 128 us
  waiting for transfers between devices  71.6 us (56%)
  starting transfers between devices  23.1 us (18%)
  Pallas kernels  15.5 us (12%)
  other arithmetic  9.06 us (7%)
  local copies, waits for them, and re-layouts  8.59 us (7%)
    all_to_all x1, waiting for transfers between devices, local(): lax.all_to_all(across, 'grid', split_axis=0, concat_axis=0, tiled=True)  26.7 us
    ppermute x3, waiting for transfers between devices, con_sum(): lax.ppermute(piece.astype(link_type), 'con', pairs).astype(jnp.float32)  23.4 us
    ppermute x3, waiting for transfers between devices, con_sum(): pieces.append(lax.ppermute(mine, 'con', pairs))  21.5 us
    all_to_all x1, starting transfers between devices, local(): lax.all_to_all(across, 'grid', split_axis=0, concat_axis=0, tiled=True)  9.65 us
    pallas_call x1, Pallas kernels, y_solve(): pl.pallas_call(y_solve_kernel, grid=(nblocks // GROUP,), in_specs=[pl.Blo...  8.9 us
    unnamed x16, local copies, waits for them, and re-layouts  7.75 us
    ppermute x3, starting transfers between devices, con_sum(): lax.ppermute(piece.astype(link_type), 'con', pairs).astype(jnp.float32)  7.49 us
    pallas_call x1, Pallas kernels, x_solve(): pl.pallas_call(x_solve_kernel, grid=(nblocks // GROUP,), in_specs=[pl.Blo...  6.58 us
  transfers between devices with their start and end apart: 7, of which 5 were waited for; matrix products, arithmetic and copies ran while one was open for 2% of the time, Pallas kernels for 0%

profile of v5, /device:TPU:70, one launch (start us, length us, event | category | flops | bytes accessed | tf_op | source)
XLA Modules:
  0.0 128.1 jit_solution(18405008917174377000)
XLA Ops:
  0.0 6.6 %shard_map.64 = bf16[4096,256]{1,0:T(8,128)(2,1)} custom-call(bf16[256,4096]{1,0:T(8,128)(2,1)} %bitcast.43, bf16[32,128,128]{2,1,0:T(8,128)(2,1)} %w_ref.2), custom_call_target="tpu_custom_call" | custom-call | tf_op jit(solution)/shard_map/pallas_call | solution.py:43
  6.6 9.7 %all-to-all-start = ((bf16[64,64,256]{2,1,0:T(8,128)(2,1)}), bf16[64,64,256]{2,1,0:T(8,128)(2,1)}, u32[]{:S(2)}, u32[]{:S(2)}) async-start(bf16[64,64,256]{2,1,0:T(8,128)(2,1)} %bitcast.38), calls=%async_computation | async-start | bytes 4194304 | tf_op jit(solution)/shard_map/all_to_all | solution.py:115
  17.0 26.7 %all-to-all-done = bf16[64,64,256]{2,1,0:T(8,128)(2,1)} async-done(((bf16[64,64,256]{2,1,0:T(8,128)(2,1)}), bf16[64,64,256]{2,1,0:T(8,128)(2,1)}, u32[]{:S(2)}, u32[]{:S(2)}) %all-to-all-start) | async-done | bytes 2097184 | tf_op jit(solution)/shard_map/all_to_all | solution.py:115
  43.7 8.9 %shard_map.65 = (f32[4,64,4096]{2,1,0:T(8,128)}, f32[64,4096]{1,0:T(8,128)}) custom-call(bf16[4096,256]{1,0:T(8,128)(2,1)} %bitcast.2.r_ref, s32[64,4096]{1,0:T(8,128)} %m_ref.1, bf16[32,128,128]{2,1,0:T(8,128)(2,1)} %w_ref.3, bf16[4,64,4096]{2,1,0:T(8,128)(2,1)} %bitcast.36), custom_call_target="tpu_custom_call" | custom-call | tf_op jit(solution)/shard_map/pallas_call | solution.py:84
  52.6 1.4 %pad_maximum_fusion = f32[128,4096]{1,0:T(8,128)S(1)} fusion(f32[64,4096]{1,0:T(8,128)} %get-tuple-element.7, f32[64,4096]{1,0:T(8,128)S(1)} %fusion.3), kind=kLoop, calls=%fused_computation.6 | loop fusion | flops 524288 | bytes 4194304 | tf_op jit(solution)/shard_map/concatenate | solution.py:118
  54.1 3.7 %collective-permute-start = (bf16[32,4096]{1,0:T(8,128)(2,1)S(1)}, bf16[32,4096]{1,0:T(8,128)(2,1)S(1)}, u32[]{:S(2)}, u32[]{:S(2)}) collective-permute-start(bf16[32,4096]{1,0:T(8,128)(2,1)S(1)} %get-tuple-element.13), channel_id=1, source_target_pairs={{0,64},{64,128},{128,192},{192,0},{1,65},{65,129},{129,193},{193,1... | collective-permute-start | bytes 786440 | tf_op jit(solution)/shard_map/ppermute | solution.py:22
  57.8 3.8 %collective-permute-start.1 = (bf16[32,4096]{1,0:T(8,128)(2,1)S(1)}, bf16[32,4096]{1,0:T(8,128)(2,1)}, u32[]{:S(2)}, u32[]{:S(2)}) collective-permute-start(bf16[32,4096]{1,0:T(8,128)(2,1)S(1)} %get-tuple-element.15), channel_id=1, source_target_pairs={{0,128},{64,192},{128,0},{192,64},{1,129},{65,193},{129,1},{193,65... | collective-permute-start | bytes 786440 | tf_op jit(solution)/shard_map/ppermute | solution.py:22
  61.6 6.1 %collective-permute-done = bf16[32,4096]{1,0:T(8,128)(2,1)S(1)} collective-permute-done((bf16[32,4096]{1,0:T(8,128)(2,1)S(1)}, bf16[32,4096]{1,0:T(8,128)(2,1)S(1)}, u32[]{:S(2)}, u32[]{:S(2)}) %collective-permute-start) | collective-permute-done | bytes 262176 | tf_op jit(solution)/shard_map/ppermute | solution.py:22
  67.7 17.3 %collective-permute-done.2 = bf16[32,4096]{1,0:T(8,128)(2,1)S(1)} collective-permute-done((bf16[32,4096]{1,0:T(8,128)(2,1)S(1)}, bf16[32,4096]{1,0:T(8,128)(2,1)S(1)}, u32[]{:S(2)}, u32[]{:S(2)}) %collective-permute-start.2) | collective-permute-done | bytes 262176 | tf_op jit(solution)/shard_map/ppermute | solution.py:22
  85.0 1.8 %bitcast_dynamic-update-slice_fusion.6 = (bf16[8,32,4096]{2,1,0:T(8,128)(2,1)}, bf16[32,4096]{1,0:T(8,128)(2,1)S(1)}) fusion(bf16[32,4096]{1,0:T(8,128)(2,1)S(1)} %collective-permute-done.2, bf16[32,4096]{1,0:T(8,128)(2,1)} %collective-permute-done.1, bf16[32,4096]{1,0:T(8,128)(2,1)S(1)} %collective-permute-done, f32[4,32,4096]{2,1,0:T(8,128)S(1)} %bitcast.40, ...), kind=kLoop, calls=%fused_computation.28 | loop fusion | flops 917503 | bytes 1835012
  86.8 4.1 %collective-permute-start.5 = (bf16[32,4096]{1,0:T(8,128)(2,1)S(1)}, bf16[32,4096]{1,0:T(8,128)(2,1)S(1)}, u32[]{:S(2)}, u32[]{:S(2)}) collective-permute-start(bf16[32,4096]{1,0:T(8,128)(2,1)S(1)} %get-tuple-element.10), channel_id=1, source_target_pairs={{0,64},{64,128},{128,192},{192,0},{1,65},{65,129},{129,193},{193,1... | collective-permute-start | bytes 786440 | tf_op jit(solution)/shard_map/ppermute | solution.py:27
  90.9 1.9 %collective-permute-start.4 = (bf16[32,4096]{1,0:T(8,128)(2,1)S(1)}, bf16[32,4096]{1,0:T(8,128)(2,1)S(1)}, u32[]{:S(2)}, u32[]{:S(2)}) collective-permute-start(bf16[32,4096]{1,0:T(8,128)(2,1)S(1)} %get-tuple-element.10), channel_id=1, source_target_pairs={{0,128},{64,192},{128,0},{192,64},{1,129},{65,193},{129,1},{193,65... | collective-permute-start | bytes 786440 | tf_op jit(solution)/shard_map/ppermute | solution.py:27
  92.8 3.3 %collective-permute-done.3 = bf16[32,4096]{1,0:T(8,128)(2,1)S(1)} collective-permute-done((bf16[32,4096]{1,0:T(8,128)(2,1)S(1)}, bf16[32,4096]{1,0:T(8,128)(2,1)S(1)}, u32[]{:S(2)}, u32[]{:S(2)}) %collective-permute-start.3) | collective-permute-done | bytes 262176 | tf_op jit(solution)/shard_map/ppermute | solution.py:27
  96.8 18.2 %collective-permute-done.4 = bf16[32,4096]{1,0:T(8,128)(2,1)S(1)} collective-permute-done((bf16[32,4096]{1,0:T(8,128)(2,1)S(1)}, bf16[32,4096]{1,0:T(8,128)(2,1)S(1)}, u32[]{:S(2)}, u32[]{:S(2)}) %collective-permute-start.4) | collective-permute-done | bytes 262176 | tf_op jit(solution)/shard_map/ppermute | solution.py:27
  115.0 0.7 bitcast_dynamic-update-slice_fusion.2
  115.7 0.7 bitcast_dynamic-update-slice_fusion
  116.5 0.7 bitcast_dynamic-update-slice_fusion.7
  117.9 0.7 bitcast_dynamic-update-slice_fusion.3
  118.6 0.7 bitcast_dynamic-update-slice_fusion.1
  119.4 1.4 %dynamic-slice_convert_fusion = f32[4,32,4096]{2,1,0:T(8,128)S(1)} fusion(bf16[8,32,4096]{2,1,0:T(8,128)(2,1)} %bitcast_dynamic-update-slice_fusion.1, s32[]{:T(128)S(6)} %select_n.48), kind=kLoop, calls=%fused_computation.10 | loop fusion | flops 524288 | bytes 3145732 | tf_op jit(solution)/shard_map/convert_element_type | solution.py:30
  121.1 0.9 copy-done.3
  122.5 1.7 %copy-done.2 = f32[4,64,4096]{2,1,0:T(8,128)S(1)} copy-done((f32[4,64,4096]{2,1,0:T(8,128)S(1)}, f32[4,64,4096]{2,1,0:T(8,128)}, u32[]{:S(2)}) %copy-start.2) | copy-done | bytes 4194328
  124.2 0.7 copy-done.1
  125.0 3.1 %fusion.2 = f32[2,2,64,4096]{3,2,1,0:T(8,128)} fusion(bf16[2,2,64,4096]{3,2,1,0:T(8,128)(2,1)S(1)} %copy-done.1, f32[2,2,64,4096]{3,2,1,0:T(8,128)S(1)} %bitcast.41, f32[64,4096]{1,0:T(8,128)S(1)} %bitcast.37, f32[64,4096]{1,0:T(8,128)S(1)} %bitcast.42, f32[2,64,4096]{2,1,0:T(8,128)S(1)} %broadcast_multiply_fusion, f32[64,4096]{1,0:T(8,128)S(1)} %get-tuple-element.16), kind=kLoop, calls=%fused_computation.4 | loop fusion | flops 6291456 | bytes 15728640 | tf_op jit(solution)/shard_map/add | solution.py:123
  (18 shorter events, 3.0 us)
Async XLA Ops:
  6.6 9.7 %copy-start = (bf16[2,2,64,4096]{3,2,1,0:T(8,128)(2,1)S(1)}, bf16[2,2,64,4096]{3,2,1,0:T(8,128)(2,1)}, u32[]{:S(2)}) copy-start(bf16[2,2,64,4096]{3,2,1,0:T(8,128)(2,1)} %param.6) | copy-start | bytes 6291460
  6.6 9.7 %copy-start.4 = (f32[2]{0:T(128)S(1)}, f32[2]{0:T(128)}, u32[]{:S(2)}) copy-start(f32[2]{0:T(128)} %param.11) | copy-start | bytes 28
  6.6 37.1 %all-to-all-start = ((bf16[64,64,256]{2,1,0:T(8,128)(2,1)}), bf16[64,64,256]{2,1,0:T(8,128)(2,1)}, u32[]{:S(2)}, u32[]{:S(2)}) async-start(bf16[64,64,256]{2,1,0:T(8,128)(2,1)} %bitcast.38), calls=%async_computation | async-start | bytes 4194304 | tf_op jit(solution)/shard_map/all_to_all | solution.py:115
  54.1 13.6 %collective-permute-start = (bf16[32,4096]{1,0:T(8,128)(2,1)S(1)}, bf16[32,4096]{1,0:T(8,128)(2,1)S(1)}, u32[]{:S(2)}, u32[]{:S(2)}) collective-permute-start(bf16[32,4096]{1,0:T(8,128)(2,1)S(1)} %get-tuple-element.13), channel_id=1, source_target_pairs={{0,64},{64,128},{128,192},{192,0},{1,65},{65,129},{129,193},{193,1... | collective-permute-start | bytes 786440 | tf_op jit(solution)/shard_map/ppermute | solution.py:22
  57.8 27.2 %collective-permute-start.2 = (bf16[32,4096]{1,0:T(8,128)(2,1)S(1)}, bf16[32,4096]{1,0:T(8,128)(2,1)S(1)}, u32[]{:S(2)}, u32[]{:S(2)}) collective-permute-start(bf16[32,4096]{1,0:T(8,128)(2,1)S(1)} %get-tuple-element.14), channel_id=1, source_target_pairs={{0,192},{64,0},{128,64},{192,128},{1,193},{65,1},{129,65},{193,129... | collective-permute-start | bytes 786440 | tf_op jit(solution)/shard_map/ppermute | solution.py:22
  57.8 27.2 %collective-permute-start.1 = (bf16[32,4096]{1,0:T(8,128)(2,1)S(1)}, bf16[32,4096]{1,0:T(8,128)(2,1)}, u32[]{:S(2)}, u32[]{:S(2)}) collective-permute-start(bf16[32,4096]{1,0:T(8,128)(2,1)S(1)} %get-tuple-element.15), channel_id=1, source_target_pairs={{0,128},{64,192},{128,0},{192,64},{1,129},{65,193},{129,1},{193,65... | collective-permute-start | bytes 786440 | tf_op jit(solution)/shard_map/ppermute | solution.py:22
  86.8 9.3 %collective-permute-start.3 = (bf16[32,4096]{1,0:T(8,128)(2,1)S(1)}, bf16[32,4096]{1,0:T(8,128)(2,1)S(1)}, u32[]{:S(2)}, u32[]{:S(2)}) collective-permute-start(bf16[32,4096]{1,0:T(8,128)(2,1)S(1)} %get-tuple-element.10), channel_id=1, source_target_pairs={{0,192},{64,0},{128,64},{192,128},{1,193},{65,1},{129,65},{193,129... | collective-permute-start | bytes 786440 | tf_op jit(solution)/shard_map/ppermute | solution.py:27
  86.8 29.0 %collective-permute-start.5 = (bf16[32,4096]{1,0:T(8,128)(2,1)S(1)}, bf16[32,4096]{1,0:T(8,128)(2,1)S(1)}, u32[]{:S(2)}, u32[]{:S(2)}) collective-permute-start(bf16[32,4096]{1,0:T(8,128)(2,1)S(1)} %get-tuple-element.10), channel_id=1, source_target_pairs={{0,64},{64,128},{128,192},{192,0},{1,65},{65,129},{129,193},{193,1... | collective-permute-start | bytes 786440 | tf_op jit(solution)/shard_map/ppermute | solution.py:27
  90.9 24.1 %collective-permute-start.4 = (bf16[32,4096]{1,0:T(8,128)(2,1)S(1)}, bf16[32,4096]{1,0:T(8,128)(2,1)S(1)}, u32[]{:S(2)}, u32[]{:S(2)}) collective-permute-start(bf16[32,4096]{1,0:T(8,128)(2,1)S(1)} %get-tuple-element.10), channel_id=1, source_target_pairs={{0,128},{64,192},{128,0},{192,64},{1,129},{65,193},{129,1},{193,65... | collective-permute-start | bytes 786440 | tf_op jit(solution)/shard_map/ppermute | solution.py:27
  120.8 1.2 copy-start.3
  122.0 2.2 %copy-start.2 = (f32[4,64,4096]{2,1,0:T(8,128)S(1)}, f32[4,64,4096]{2,1,0:T(8,128)}, u32[]{:S(2)}) copy-start(f32[4,64,4096]{2,1,0:T(8,128)} %get-tuple-element.8) | copy-start | bytes 12582916
  122.2 2.7 %copy-start.1 = (bf16[2,2,64,4096]{3,2,1,0:T(8,128)(2,1)S(1)}, bf16[2,2,64,4096]{3,2,1,0:T(8,128)(2,1)}, u32[]{:S(2)}) copy-start(bf16[2,2,64,4096]{3,2,1,0:T(8,128)(2,1)} %param.6) | copy-start | bytes 6291460

commit v6 on v3

--- a/solution.py
+++ b/solution.py
@@ -25,9 +25,14 @@
     for shift in range(1, count):
         pairs = [(i, (i + shift) % count) for i in range(count)]
         pieces.append(lax.ppermute(mine, "con", pairs))
-    ordered = jnp.stack([pieces[(-t) % count] for t in range(count)])
-    gathered = jnp.roll(ordered, me, axis=0)
-    return gathered.reshape(part.shape).astype(jnp.float32)
+    slots = []
+    for q in range(count):
+        source = (me - q) % count
+        slot = pieces[0]
+        for shift in range(1, count):
+            slot = jnp.where(source == shift, pieces[shift], slot)
+        slots.append(slot)
+    return jnp.concatenate(slots, axis=0).astype(jnp.float32)
 
 
 def x_solve_kernel(s_ref, w_ref, o_ref):
@@ -112,9 +117,9 @@
     local_squares = jnp.sum(weight_full * vel_float * vel_float, axis=(0, 1))
     sea_float = (land_mask == 1).astype(jnp.float32)
     across = x_solve(seed_adjoint.reshape(con_local * 2 * cols_local, full_side), inv_x)
-    across, local_squares = lax.optimization_barrier((across, local_squares))
+    arrived = lax.all_to_all(across, "grid", split_axis=0, concat_axis=0, tiled=True)
+    arrived, local_squares = lax.optimization_barrier((arrived, local_squares))
     squares = con_sum(local_squares, jnp.bfloat16)
-    arrived = lax.all_to_all(across, "grid", split_axis=0, concat_axis=0, tiled=True)
     solved, local_inner = y_solve(arrived, land_mask, inv_y, velocity.reshape(con_local * 2, rows_local, full_side))
     rhs_adjoint = solved.reshape(con_local, 2, rows_local, full_side)
     inner = con_sum(local_inner, jnp.bfloat16)

time: 135 us -> 113 us (0.84)
  the two profiles are of different devices: /device:TPU:8 before, /device:TPU:48 now
where the time goes in v6:
time: 113 us; the launch traced here: 112 us
  waiting for transfers between devices  51.4 us (45%)
  starting transfers between devices  36.6 us (32%)
  Pallas kernels  15.7 us (14%)
  other arithmetic  6.84 us (6%)
  local copies, waits for them, and re-layouts  1.22 us (1%)
    all_to_all x1, waiting for transfers between devices, local(): lax.all_to_all(across, 'grid', split_axis=0, concat_axis=0, tiled=True)  24.6 us
    ppermute x6, waiting for transfers between devices, con_sum(): lax.ppermute(piece.astype(link_type), 'con', pairs).astype(jnp.float32)  21.4 us
    ppermute x6, starting transfers between devices, con_sum(): lax.ppermute(piece.astype(link_type), 'con', pairs).astype(jnp.float32)  15.7 us
    ppermute x6, starting transfers between devices, con_sum(): pieces.append(lax.ppermute(mine, 'con', pairs))  11.8 us
    all_to_all x1, starting transfers between devices, local(): lax.all_to_all(across, 'grid', split_axis=0, concat_axis=0, tiled=True)  9.13 us
    pallas_call x1, Pallas kernels, y_solve(): pl.pallas_call(y_solve_kernel, grid=(nblocks // GROUP,), in_specs=[pl.Blo...  8.98 us
    pallas_call x1, Pallas kernels, x_solve(): pl.pallas_call(x_solve_kernel, grid=(nblocks // GROUP,), in_specs=[pl.Blo...  6.73 us
    ppermute x6, waiting for transfers between devices, con_sum(): pieces.append(lax.ppermute(mine, 'con', pairs))  5.51 us
  transfers between devices with their start and end apart: 13, of which 3 were waited for; matrix products, arithmetic and copies ran while one was open for 4% of the time, Pallas kernels for 8%

profile of v6, /device:TPU:48, one launch (start us, length us, event | category | flops | bytes accessed | tf_op | source)
XLA Modules:
  0.0 112.1 jit_solution(14304067265802833757)
XLA Ops:
  0.0 6.7 %shard_map.64 = bf16[4096,256]{1,0:T(8,128)(2,1)} custom-call(bf16[256,4096]{1,0:T(8,128)(2,1)} %bitcast.40, bf16[32,128,128]{2,1,0:T(8,128)(2,1)} %w_ref.2), custom_call_target="tpu_custom_call" | custom-call | tf_op jit(solution)/shard_map/pallas_call | solution.py:48
  6.7 9.1 %all-to-all-start = ((bf16[64,64,256]{2,1,0:T(8,128)(2,1)}), bf16[64,64,256]{2,1,0:T(8,128)(2,1)}, u32[]{:S(2)}, u32[]{:S(2)}) async-start(bf16[64,64,256]{2,1,0:T(8,128)(2,1)} %bitcast.36), calls=%async_computation | async-start | bytes 4194304 | tf_op jit(solution)/shard_map/all_to_all | solution.py:120
  16.0 0.7 fusion.3
  16.7 24.6 %all-to-all-done = bf16[64,64,256]{2,1,0:T(8,128)(2,1)} async-done(((bf16[64,64,256]{2,1,0:T(8,128)(2,1)}), bf16[64,64,256]{2,1,0:T(8,128)(2,1)}, u32[]{:S(2)}, u32[]{:S(2)}) %all-to-all-start) | async-done | bytes 2097184 | tf_op jit(solution)/shard_map/all_to_all | solution.py:120
  41.3 3.3 %collective-permute-start = (bf16[16,4096]{1,0:T(8,128)(2,1)S(1)}, bf16[16,4096]{1,0:T(8,128)(2,1)S(1)}, u32[]{:S(2)}, u32[]{:S(2)}) collective-permute-start(bf16[16,4096]{1,0:T(8,128)(2,1)S(1)} %get-tuple-element.18), channel_id=1, source_target_pairs={{0,64},{64,128},{128,192},{192,0},{1,65},{65,129},{129,193},{193,1... | collective-permute-start | bytes 393224 | tf_op jit(solution)/shard_map/ppermute | solution.py:22
  44.7 2.2 %collective-permute-start.2 = (bf16[16,4096]{1,0:T(8,128)(2,1)S(1)}, bf16[16,4096]{1,0:T(8,128)(2,1)S(1)}, u32[]{:S(2)}, u32[]{:S(2)}) collective-permute-start(bf16[16,4096]{1,0:T(8,128)(2,1)S(1)} %get-tuple-element.19), channel_id=1, source_target_pairs={{0,192},{64,0},{128,64},{192,128},{1,193},{65,1},{129,65},{193,129... | collective-permute-start | bytes 393224 | tf_op jit(solution)/shard_map/ppermute | solution.py:22
  46.9 4.9 %collective-permute-start.1 = (bf16[16,4096]{1,0:T(8,128)(2,1)S(1)}, bf16[16,4096]{1,0:T(8,128)(2,1)S(1)}, u32[]{:S(2)}, u32[]{:S(2)}) collective-permute-start(bf16[16,4096]{1,0:T(8,128)(2,1)S(1)} %get-tuple-element.20), channel_id=1, source_target_pairs={{0,128},{64,192},{128,0},{192,64},{1,129},{65,193},{129,1},{193,65... | collective-permute-start | bytes 393224 | tf_op jit(solution)/shard_map/ppermute | solution.py:22
  51.8 9.0 %shard_map.65 = (f32[4,64,4096]{2,1,0:T(8,128)}, f32[64,4096]{1,0:T(8,128)}) custom-call(bf16[4096,256]{1,0:T(8,128)(2,1)} %bitcast.2.r_ref, s32[64,4096]{1,0:T(8,128)} %m_ref.1, bf16[32,128,128]{2,1,0:T(8,128)(2,1)} %w_ref.3, bf16[4,64,4096]{2,1,0:T(8,128)(2,1)} %bitcast.35), custom_call_target="tpu_custom_call" | custom-call | tf_op jit(solution)/shard_map/pallas_call | solution.py:89
  60.8 1.1 %fusion.13 = (bf16[16,4096]{1,0:T(8,128)(2,1)S(1)}, bf16[16,4096]{1,0:T(8,128)(2,1)S(1)}, bf16[16,4096]{1,0:T(8,128)(2,1)S(1)}) fusion(f32[4,16,4096]{2,1,0:T(8,128)} %bitcast.41, s32[]{:T(128)S(6)} %select_n.188, s32[]{:T(128)S(6)} %select_n.192, s32[]{:T(128)S(6)} %select_n.190), kind=kLoop, calls=%fused_computation.27 | loop fusion | bytes 786444 | tf_op jit(solution)/shard_map/convert_element_type | solution.py:22
  62.0 0.3 collective-permute-start.6
  62.3 3.9 %collective-permute-start.8 = (bf16[16,4096]{1,0:T(8,128)(2,1)S(1)}, bf16[16,4096]{1,0:T(8,128)(2,1)S(1)}, u32[]{:S(2)}, u32[]{:S(2)}) collective-permute-start(bf16[16,4096]{1,0:T(8,128)(2,1)S(1)} %get-tuple-element.16), channel_id=1, source_target_pairs={{0,192},{64,0},{128,64},{192,128},{1,193},{65,1},{129,65},{193,129... | collective-permute-start | bytes 393224 | tf_op jit(solution)/shard_map/ppermute | solution.py:22
  66.2 1.0 collective-permute-start.7
  67.2 1.0 fusion.9
  68.2 1.5 %collective-permute-start.5 = (bf16[16,4096]{1,0:T(8,128)(2,1)S(1)}, bf16[16,4096]{1,0:T(8,128)(2,1)S(1)}, u32[]{:S(2)}, u32[]{:S(2)}) collective-permute-start(bf16[16,4096]{1,0:T(8,128)(2,1)S(1)} %fusion.9), channel_id=1, source_target_pairs={{0,64},{64,128},{128,192},{192,0},{1,65},{65,129},{129,193},{193,1... | collective-permute-start | bytes 393224 | tf_op jit(solution)/shard_map/ppermute | solution.py:27
  69.6 3.7 %collective-permute-start.4 = (bf16[16,4096]{1,0:T(8,128)(2,1)S(1)}, bf16[16,4096]{1,0:T(8,128)(2,1)S(1)}, u32[]{:S(2)}, u32[]{:S(2)}) collective-permute-start(bf16[16,4096]{1,0:T(8,128)(2,1)S(1)} %fusion.9), channel_id=1, source_target_pairs={{0,128},{64,192},{128,0},{192,64},{1,129},{65,193},{129,1},{193,65... | collective-permute-start | bytes 393224 | tf_op jit(solution)/shard_map/ppermute | solution.py:27
  73.3 21.3 %collective-permute-done.6 = bf16[16,4096]{1,0:T(8,128)(2,1)S(1)} collective-permute-done((bf16[16,4096]{1,0:T(8,128)(2,1)S(1)}, bf16[16,4096]{1,0:T(8,128)(2,1)S(1)}, u32[]{:S(2)}, u32[]{:S(2)}) %collective-permute-start.6) | collective-permute-done | bytes 131104 | tf_op jit(solution)/shard_map/ppermute | solution.py:22
  94.7 1.0 fusion.6
  95.7 3.0 %collective-permute-start.11 = (bf16[16,4096]{1,0:T(8,128)(2,1)S(1)}, bf16[16,4096]{1,0:T(8,128)(2,1)S(1)}, u32[]{:S(2)}, u32[]{:S(2)}) collective-permute-start(bf16[16,4096]{1,0:T(8,128)(2,1)S(1)} %fusion.6), channel_id=1, source_target_pairs={{0,64},{64,128},{128,192},{192,0},{1,65},{65,129},{129,193},{193,1... | collective-permute-start | bytes 393224 | tf_op jit(solution)/shard_map/ppermute | solution.py:27
  98.7 3.7 %collective-permute-start.9 = (bf16[16,4096]{1,0:T(8,128)(2,1)S(1)}, bf16[16,4096]{1,0:T(8,128)(2,1)S(1)}, u32[]{:S(2)}, u32[]{:S(2)}) collective-permute-start(bf16[16,4096]{1,0:T(8,128)(2,1)S(1)} %fusion.6), channel_id=1, source_target_pairs={{0,192},{64,0},{128,64},{192,128},{1,193},{65,1},{129,65},{193,129... | collective-permute-start | bytes 393224 | tf_op jit(solution)/shard_map/ppermute | solution.py:27
  102.5 0.4 fusion.16
  102.9 0.3 broadcast_multiply_fusion
  103.2 5.5 %collective-permute-done.10 = bf16[16,4096]{1,0:T(8,128)(2,1)S(1)} collective-permute-done((bf16[16,4096]{1,0:T(8,128)(2,1)S(1)}, bf16[16,4096]{1,0:T(8,128)(2,1)S(1)}, u32[]{:S(2)}, u32[]{:S(2)}) %collective-permute-start.10) | collective-permute-done | bytes 131104 | tf_op jit(solution)/shard_map/ppermute | solution.py:27
  108.8 0.1 maximum_convert_fusion
  108.9 3.2 %fusion.2 = f32[2,2,64,4096]{3,2,1,0:T(8,128)} fusion(bf16[2,2,64,4096]{3,2,1,0:T(8,128)(2,1)S(1)} %copy-done.1, f32[2,2,64,4096]{3,2,1,0:T(8,128)S(1)} %bitcast.37, f32[64,4096]{1,0:T(8,128)S(1)} %get-tuple-element.21, f32[64,4096]{1,0:T(8,128)S(1)} %maximum_convert_fusion, f32[2,64,4096]{2,1,0:T(8,128)S(1)} %broadcast_multiply_fusion, ...), kind=kLoop, calls=%fused_computation.4 | loop fusion | flops 6291456 | bytes 15728640 | tf_op jit(solution)/shard_map/add | solution.py:129
  (27 shorter events, 0.2 us)
Async XLA Ops:
  0.0 16.0 %copy-start = (bf16[2,2,64,4096]{3,2,1,0:T(8,128)(2,1)S(1)}, bf16[2,2,64,4096]{3,2,1,0:T(8,128)(2,1)}, u32[]{:S(2)}) copy-start(bf16[2,2,64,4096]{3,2,1,0:T(8,128)(2,1)} %param.6) | copy-start | bytes 6291460
  0.0 16.0 %copy-start.5 = (f32[2]{0:T(128)S(1)}, f32[2]{0:T(128)}, u32[]{:S(2)}) copy-start(f32[2]{0:T(128)} %param.11) | copy-start | bytes 28
  6.7 34.5 %all-to-all-start = ((bf16[64,64,256]{2,1,0:T(8,128)(2,1)}), bf16[64,64,256]{2,1,0:T(8,128)(2,1)}, u32[]{:S(2)}, u32[]{:S(2)}) async-start(bf16[64,64,256]{2,1,0:T(8,128)(2,1)} %bitcast.36), calls=%async_computation | async-start | bytes 4194304 | tf_op jit(solution)/shard_map/all_to_all | solution.py:120
  16.7 35.1 %copy-start.4 = (f32[64,4096]{1,0:T(8,128)}, f32[64,4096]{1,0:T(8,128)S(1)}, u32[]{:S(2)}) copy-start(f32[64,4096]{1,0:T(8,128)S(1)} %fusion.3) | copy-start | bytes 3145732
  41.3 24.9 %collective-permute-start = (bf16[16,4096]{1,0:T(8,128)(2,1)S(1)}, bf16[16,4096]{1,0:T(8,128)(2,1)S(1)}, u32[]{:S(2)}, u32[]{:S(2)}) collective-permute-start(bf16[16,4096]{1,0:T(8,128)(2,1)S(1)} %get-tuple-element.18), channel_id=1, source_target_pairs={{0,64},{64,128},{128,192},{192,0},{1,65},{65,129},{129,193},{193,1... | collective-permute-start | bytes 393224 | tf_op jit(solution)/shard_map/ppermute | solution.py:22
  44.7 22.5 %collective-permute-start.2 = (bf16[16,4096]{1,0:T(8,128)(2,1)S(1)}, bf16[16,4096]{1,0:T(8,128)(2,1)S(1)}, u32[]{:S(2)}, u32[]{:S(2)}) collective-permute-start(bf16[16,4096]{1,0:T(8,128)(2,1)S(1)} %get-tuple-element.19), channel_id=1, source_target_pairs={{0,192},{64,0},{128,64},{192,128},{1,193},{65,1},{129,65},{193,129... | collective-permute-start | bytes 393224 | tf_op jit(solution)/shard_map/ppermute | solution.py:22
  46.9 20.3 %collective-permute-start.1 = (bf16[16,4096]{1,0:T(8,128)(2,1)S(1)}, bf16[16,4096]{1,0:T(8,128)(2,1)S(1)}, u32[]{:S(2)}, u32[]{:S(2)}) collective-permute-start(bf16[16,4096]{1,0:T(8,128)(2,1)S(1)} %get-tuple-element.20), channel_id=1, source_target_pairs={{0,128},{64,192},{128,0},{192,64},{1,129},{65,193},{129,1},{193,65... | collective-permute-start | bytes 393224 | tf_op jit(solution)/shard_map/ppermute | solution.py:22
  51.8 50.6 %copy-start.3 = (s32[64,4096]{1,0:T(8,128)S(1)}, s32[64,4096]{1,0:T(8,128)}, u32[]{:S(2)}) copy-start(s32[64,4096]{1,0:T(8,128)} %m_ref.1) | copy-start | bytes 3145732
  62.0 32.7 %collective-permute-start.6 = (bf16[16,4096]{1,0:T(8,128)(2,1)S(1)}, bf16[16,4096]{1,0:T(8,128)(2,1)S(1)}, u32[]{:S(2)}, u32[]{:S(2)}) collective-permute-start(bf16[16,4096]{1,0:T(8,128)(2,1)S(1)} %get-tuple-element.15), channel_id=1, source_target_pairs={{0,64},{64,128},{128,192},{192,0},{1,65},{65,129},{129,193},{193,1... | collective-permute-start | bytes 393224 | tf_op jit(solution)/shard_map/ppermute | solution.py:22
  62.3 32.4 %collective-permute-start.8 = (bf16[16,4096]{1,0:T(8,128)(2,1)S(1)}, bf16[16,4096]{1,0:T(8,128)(2,1)S(1)}, u32[]{:S(2)}, u32[]{:S(2)}) collective-permute-start(bf16[16,4096]{1,0:T(8,128)(2,1)S(1)} %get-tuple-element.16), channel_id=1, source_target_pairs={{0,192},{64,0},{128,64},{192,128},{1,193},{65,1},{129,65},{193,129... | collective-permute-start | bytes 393224 | tf_op jit(solution)/shard_map/ppermute | solution.py:22
  66.2 28.5 %collective-permute-start.7 = (bf16[16,4096]{1,0:T(8,128)(2,1)S(1)}, bf16[16,4096]{1,0:T(8,128)(2,1)S(1)}, u32[]{:S(2)}, u32[]{:S(2)}) collective-permute-start(bf16[16,4096]{1,0:T(8,128)(2,1)S(1)} %get-tuple-element.17), channel_id=1, source_target_pairs={{0,128},{64,192},{128,0},{192,64},{1,129},{65,193},{129,1},{193,65... | collective-permute-start | bytes 393224 | tf_op jit(solution)/shard_map/ppermute | solution.py:22
  68.2 30.5 %collective-permute-start.5 = (bf16[16,4096]{1,0:T(8,128)(2,1)S(1)}, bf16[16,4096]{1,0:T(8,128)(2,1)S(1)}, u32[]{:S(2)}, u32[]{:S(2)}) collective-permute-start(bf16[16,4096]{1,0:T(8,128)(2,1)S(1)} %fusion.9), channel_id=1, source_target_pairs={{0,64},{64,128},{128,192},{192,0},{1,65},{65,129},{129,193},{193,1... | collective-permute-start | bytes 393224 | tf_op jit(solution)/shard_map/ppermute | solution.py:27
  69.6 32.7 %collective-permute-start.4 = (bf16[16,4096]{1,0:T(8,128)(2,1)S(1)}, bf16[16,4096]{1,0:T(8,128)(2,1)S(1)}, u32[]{:S(2)}, u32[]{:S(2)}) collective-permute-start(bf16[16,4096]{1,0:T(8,128)(2,1)S(1)} %fusion.9), channel_id=1, source_target_pairs={{0,128},{64,192},{128,0},{192,64},{1,129},{65,193},{129,1},{193,65... | collective-permute-start | bytes 393224 | tf_op jit(solution)/shard_map/ppermute | solution.py:27
  94.7 7.7 %collective-permute-start.3 = (bf16[16,4096]{1,0:T(8,128)(2,1)S(1)}, bf16[16,4096]{1,0:T(8,128)(2,1)S(1)}, u32[]{:S(2)}, u32[]{:S(2)}) collective-permute-start(bf16[16,4096]{1,0:T(8,128)(2,1)S(1)} %fusion.9), channel_id=1, source_target_pairs={{0,192},{64,0},{128,64},{192,128},{1,193},{65,1},{129,65},{193,129... | collective-permute-start | bytes 393224 | tf_op jit(solution)/shard_map/ppermute | solution.py:27
  95.7 7.5 %collective-permute-start.11 = (bf16[16,4096]{1,0:T(8,128)(2,1)S(1)}, bf16[16,4096]{1,0:T(8,128)(2,1)S(1)}, u32[]{:S(2)}, u32[]{:S(2)}) collective-permute-start(bf16[16,4096]{1,0:T(8,128)(2,1)S(1)} %fusion.6), channel_id=1, source_target_pairs={{0,64},{64,128},{128,192},{192,0},{1,65},{65,129},{129,193},{193,1... | collective-permute-start | bytes 393224 | tf_op jit(solution)/shard_map/ppermute | solution.py:27
  98.7 10.0 %collective-permute-start.10 = (bf16[16,4096]{1,0:T(8,128)(2,1)S(1)}, bf16[16,4096]{1,0:T(8,128)(2,1)S(1)}, u32[]{:S(2)}, u32[]{:S(2)}) collective-permute-start(bf16[16,4096]{1,0:T(8,128)(2,1)S(1)} %fusion.6), channel_id=1, source_target_pairs={{0,128},{64,192},{128,0},{192,64},{1,129},{65,193},{129,1},{193,65... | collective-permute-start | bytes 393224 | tf_op jit(solution)/shard_map/ppermute | solution.py:27
  98.7 10.0 %collective-permute-start.9 = (bf16[16,4096]{1,0:T(8,128)(2,1)S(1)}, bf16[16,4096]{1,0:T(8,128)(2,1)S(1)}, u32[]{:S(2)}, u32[]{:S(2)}) collective-permute-start(bf16[16,4096]{1,0:T(8,128)(2,1)S(1)} %fusion.6), channel_id=1, source_target_pairs={{0,192},{64,0},{128,64},{192,128},{1,193},{65,1},{129,65},{193,129... | collective-permute-start | bytes 393224 | tf_op jit(solution)/shard_map/ppermute | solution.py:27
  102.5 6.4 %copy-start.1 = (bf16[2,2,64,4096]{3,2,1,0:T(8,128)(2,1)S(1)}, bf16[2,2,64,4096]{3,2,1,0:T(8,128)(2,1)}, u32[]{:S(2)}) copy-start(bf16[2,2,64,4096]{3,2,1,0:T(8,128)(2,1)} %param.6) | copy-start | bytes 6291460
  102.5 6.4 %copy-start.2 = (f32[4,64,4096]{2,1,0:T(8,128)S(1)}, f32[4,64,4096]{2,1,0:T(8,128)}, u32[]{:S(2)}) copy-start(f32[4,64,4096]{2,1,0:T(8,128)} %get-tuple-element.11) | copy-start | bytes 12582916

commit v7 on v6

--- a/solution.py
+++ b/solution.py
@@ -116,12 +116,21 @@
     weight_full = weights[:, None, None, None]
     local_squares = jnp.sum(weight_full * vel_float * vel_float, axis=(0, 1))
     sea_float = (land_mask == 1).astype(jnp.float32)
-    across = x_solve(seed_adjoint.reshape(con_local * 2 * cols_local, full_side), inv_x)
-    arrived = lax.all_to_all(across, "grid", split_axis=0, concat_axis=0, tiled=True)
-    arrived, local_squares = lax.optimization_barrier((arrived, local_squares))
+    seed_rows = seed_adjoint.reshape(con_local, 2 * cols_local, full_side)
+    vel_rows = velocity.reshape(con_local, 2, rows_local, full_side)
+    landed = []
+    for c in range(con_local):
+        across = x_solve(seed_rows[c], inv_x)
+        landed.append(lax.all_to_all(across, "grid", split_axis=0, concat_axis=0, tiled=True))
+    landed[-1], local_squares = lax.optimization_barrier((landed[-1], local_squares))
     squares = con_sum(local_squares, jnp.bfloat16)
-    solved, local_inner = y_solve(arrived, land_mask, inv_y, velocity.reshape(con_local * 2, rows_local, full_side))
-    rhs_adjoint = solved.reshape(con_local, 2, rows_local, full_side)
+    solved_parts = []
+    local_inner = None
+    for c in range(con_local):
+        part, part_inner = y_solve(landed[c], land_mask, inv_y, vel_rows[c])
+        solved_parts.append(part)
+        local_inner = part_inner if local_inner is None else local_inner + part_inner
+    rhs_adjoint = jnp.stack(solved_parts, axis=0)
     inner = con_sum(local_inner, jnp.bfloat16)
     speed = jnp.sqrt(0.25 + squares)
     first = -0.5 * sea_float * speed * rhs_adjoint

time: 113 us -> 130 us (1.15)
  starting transfers between devices: 36.6 us -> 58.9 us
  waiting for transfers between devices: 51.4 us -> 29.5 us
  Pallas kernels: 15.7 us -> 27.7 us
  local copies, waits for them, and re-layouts: 1.22 us -> 5.61 us
    all_to_all x1 -> x2, waiting for transfers between devices: 24.6 us -> 12 us  [local(): lax.all_to_all(across, 'grid', split_axis=0, concat_axis=0, tiled=True)]
    ppermute x6, waiting for transfers between devices: 21.4 us -> 10.9 us  [con_sum(): lax.ppermute(piece.astype(link_type), 'con', pairs).astype(jnp.float32)]
    ppermute x6, starting transfers between devices: 11.8 us -> 21.1 us  [con_sum(): pieces.append(lax.ppermute(mine, 'con', pairs))]
    all_to_all x1 -> x2, starting transfers between devices: 9.13 us -> 16.8 us  [local(): lax.all_to_all(across, 'grid', split_axis=0, concat_axis=0, tiled=True)]
    pallas_call x1 -> x2, Pallas kernels: 8.98 us -> 15.2 us  [y_solve(): pl.pallas_call(y_solve_kernel, grid=(nblocks // GROUP,), in_specs=[pl.Blo...]
    pallas_call x1 -> x2, Pallas kernels: 6.73 us -> 12.5 us  [x_solve(): pl.pallas_call(x_solve_kernel, grid=(nblocks // GROUP,), in_specs=[pl.Blo...]
    ppermute x6, starting transfers between devices: 15.7 us -> 21 us  [con_sum(): lax.ppermute(piece.astype(link_type), 'con', pairs).astype(jnp.float32)]
    slice x0 -> x1, local copies, waits for them, and re-layouts: none -> 3.09 us  [local(): across = x_solve(seed_rows[c], inv_x)]
  transfers between devices with their start and end apart: 13 -> 14, of which waited for: 3 -> 5; matrix products, arithmetic and copies ran while one was open for 4% -> 5% of each run, Pallas kernels for 8% -> 17%
where the time goes in v7:
time: 130 us; the launch traced here: 129 us
  starting transfers between devices  58.9 us (45%)
  waiting for transfers between devices  29.5 us (23%)
  Pallas kernels  27.7 us (21%)
  other arithmetic  6.64 us (5%)
  local copies, waits for them, and re-layouts  5.61 us (4%)
    ppermute x6, starting transfers between devices, con_sum(): pieces.append(lax.ppermute(mine, 'con', pairs))  21.1 us
    ppermute x6, starting transfers between devices, con_sum(): lax.ppermute(piece.astype(link_type), 'con', pairs).astype(jnp.float32)  21 us
    all_to_all x2, starting transfers between devices, local(): lax.all_to_all(across, 'grid', split_axis=0, concat_axis=0, tiled=True)  16.8 us
    pallas_call x2, Pallas kernels, y_solve(): pl.pallas_call(y_solve_kernel, grid=(nblocks // GROUP,), in_specs=[pl.Blo...  15.2 us
    pallas_call x2, Pallas kernels, x_solve(): pl.pallas_call(x_solve_kernel, grid=(nblocks // GROUP,), in_specs=[pl.Blo...  12.5 us
    all_to_all x2, waiting for transfers between devices, local(): lax.all_to_all(across, 'grid', split_axis=0, concat_axis=0, tiled=True)  12 us
    ppermute x6, waiting for transfers between devices, con_sum(): lax.ppermute(piece.astype(link_type), 'con', pairs).astype(jnp.float32)  10.9 us
    ppermute x6, waiting for transfers between devices, con_sum(): pieces.append(lax.ppermute(mine, 'con', pairs))  6.68 us
  transfers between devices with their start and end apart: 14, of which 5 were waited for; matrix products, arithmetic and copies ran while one was open for 5% of the time, Pallas kernels for 17%

profile of v7, /device:TPU:48, one launch (start us, length us, event | category | flops | bytes accessed | tf_op | source)
XLA Modules:
  0.0 128.7 jit_solution(9942030854939216892)
XLA Ops:
  0.0 3.1 %fusion.17 = (bf16[1,2,64,4096]{3,2,1,0:T(8,128)(2,1)}, bf16[1,2,64,4096]{3,2,1,0:T(8,128)(2,1)}) fusion(bf16[2,2,64,4096]{3,2,1,0:T(8,128)(2,1)} %param.7), kind=kLoop, calls=%fused_computation.42 | loop fusion | bytes 4194304 | tf_op jit(solution)/shard_map/slice | solution.py:123
  3.1 6.2 %shard_map.64 = bf16[4096,128]{1,0:T(8,128)(2,1)} custom-call(bf16[128,4096]{1,0:T(8,128)(2,1)} %bitcast.45, bf16[32,128,128]{2,1,0:T(8,128)(2,1)} %w_ref.5), custom_call_target="tpu_custom_call" | custom-call | tf_op jit(solution)/shard_map/pallas_call | solution.py:48
  9.3 9.0 %all-to-all-start = ((bf16[64,64,128]{2,1,0:T(8,128)(2,1)}), bf16[64,64,128]{2,1,0:T(8,128)(2,1)S(1)}, u32[]{:S(2)}, u32[]{:S(2)}) async-start(bf16[64,64,128]{2,1,0:T(8,128)(2,1)} %bitcast.43), calls=%async_computation | async-start | bytes 2097152 | tf_op jit(solution)/shard_map/all_to_all | solution.py:124
  18.4 6.3 %shard_map.65 = bf16[4096,128]{1,0:T(8,128)(2,1)} custom-call(bf16[128,4096]{1,0:T(8,128)(2,1)} %bitcast.44, bf16[32,128,128]{2,1,0:T(8,128)(2,1)} %w_ref.5), custom_call_target="tpu_custom_call" | custom-call | tf_op jit(solution)/shard_map/pallas_call | solution.py:48
  24.6 8.3 %all-to-all-done = bf16[64,64,128]{2,1,0:T(8,128)(2,1)S(1)} async-done(((bf16[64,64,128]{2,1,0:T(8,128)(2,1)}), bf16[64,64,128]{2,1,0:T(8,128)(2,1)S(1)}, u32[]{:S(2)}, u32[]{:S(2)}) %all-to-all-start) | async-done | bytes 1048608 | tf_op jit(solution)/shard_map/all_to_all | solution.py:124
  33.0 7.8 %all-to-all-start.1 = ((bf16[64,64,128]{2,1,0:T(8,128)(2,1)}), bf16[64,64,128]{2,1,0:T(8,128)(2,1)}, u32[]{:S(2)}, u32[]{:S(2)}) async-start(bf16[64,64,128]{2,1,0:T(8,128)(2,1)} %bitcast.42), calls=%async_computation.1 | async-start | bytes 2097152 | tf_op jit(solution)/shard_map/all_to_all | solution.py:124
  41.6 1.7 %slice_bitcast_fusion.1 = (bf16[2,64,4096]{2,1,0:T(8,128)(2,1)}, bf16[2,64,4096]{2,1,0:T(8,128)(2,1)}) fusion(bf16[2,2,64,4096]{3,2,1,0:T(8,128)(2,1)S(1)} %copy-done), kind=kLoop, calls=%fused_computation.9 | loop fusion | bytes 4194304 | tf_op jit(solution)/shard_map/squeeze | solution.py:130
  44.0 3.3 %collective-permute-start = (bf16[16,4096]{1,0:T(8,128)(2,1)}, bf16[16,4096]{1,0:T(8,128)(2,1)S(1)}, u32[]{:S(2)}, u32[]{:S(2)}) collective-permute-start(bf16[16,4096]{1,0:T(8,128)(2,1)} %get-tuple-element.26), channel_id=1, source_target_pairs={{0,64},{64,128},{128,192},{192,0},{1,65},{65,129},{129,193},{193,1... | collective-permute-start | bytes 393224 | tf_op jit(solution)/shard_map/ppermute | solution.py:22
  47.3 2.1 %collective-permute-start.2 = (bf16[16,4096]{1,0:T(8,128)(2,1)}, bf16[16,4096]{1,0:T(8,128)(2,1)S(1)}, u32[]{:S(2)}, u32[]{:S(2)}) collective-permute-start(bf16[16,4096]{1,0:T(8,128)(2,1)} %get-tuple-element.27), channel_id=1, source_target_pairs={{0,192},{64,0},{128,64},{192,128},{1,193},{65,1},{129,65},{193,129... | collective-permute-start | bytes 393224 | tf_op jit(solution)/shard_map/ppermute | solution.py:22
  49.4 5.0 %collective-permute-start.1 = (bf16[16,4096]{1,0:T(8,128)(2,1)S(1)}, bf16[16,4096]{1,0:T(8,128)(2,1)}, u32[]{:S(2)}, u32[]{:S(2)}) collective-permute-start(bf16[16,4096]{1,0:T(8,128)(2,1)S(1)} %get-tuple-element.28), channel_id=1, source_target_pairs={{0,128},{64,192},{128,0},{192,64},{1,129},{65,193},{129,1},{193,65... | collective-permute-start | bytes 393224 | tf_op jit(solution)/shard_map/ppermute | solution.py:22
  54.5 3.7 %all-to-all-done.1 = bf16[64,64,128]{2,1,0:T(8,128)(2,1)} async-done(((bf16[64,64,128]{2,1,0:T(8,128)(2,1)}), bf16[64,64,128]{2,1,0:T(8,128)(2,1)}, u32[]{:S(2)}, u32[]{:S(2)}) %all-to-all-start.1) | async-done | bytes 1048608 | tf_op jit(solution)/shard_map/all_to_all | solution.py:124
  58.1 7.6 %shard_map.66 = (f32[2,64,4096]{2,1,0:T(8,128)}, f32[64,4096]{1,0:T(8,128)}) custom-call(bf16[4096,128]{1,0:T(8,128)(2,1)} %bitcast.10.r_ref, s32[64,4096]{1,0:T(8,128)} %m_ref.3, bf16[32,128,128]{2,1,0:T(8,128)(2,1)} %w_ref.7, bf16[2,64,4096]{2,1,0:T(8,128)(2,1)} %get-tuple-element.17.v_ref), custom_call_target="tpu_custom_call" | custom-call | tf_op jit(solution)/shard_map/pallas_call | solution.py:89
  65.7 7.6 %shard_map.67 = (f32[2,64,4096]{2,1,0:T(8,128)}, f32[64,4096]{1,0:T(8,128)}) custom-call(bf16[4096,128]{1,0:T(8,128)(2,1)} %bitcast.46, s32[64,4096]{1,0:T(8,128)} %m_ref.3, bf16[32,128,128]{2,1,0:T(8,128)(2,1)} %w_ref.7, bf16[2,64,4096]{2,1,0:T(8,128)(2,1)} %get-tuple-element.18.v_ref), custom_call_target="tpu_custom_call" | custom-call | tf_op jit(solution)/shard_map/pallas_call | solution.py:89
  74.9 3.3 %collective-permute-start.6 = (bf16[16,4096]{1,0:T(8,128)(2,1)S(1)}, bf16[16,4096]{1,0:T(8,128)(2,1)S(1)}, u32[]{:S(2)}, u32[]{:S(2)}) collective-permute-start(bf16[16,4096]{1,0:T(8,128)(2,1)S(1)} %get-tuple-element.23), channel_id=1, source_target_pairs={{0,64},{64,128},{128,192},{192,0},{1,65},{65,129},{129,193},{193,1... | collective-permute-start | bytes 393224 | tf_op jit(solution)/shard_map/ppermute | solution.py:22
  78.2 2.2 %collective-permute-start.8 = (bf16[16,4096]{1,0:T(8,128)(2,1)S(1)}, bf16[16,4096]{1,0:T(8,128)(2,1)S(1)}, u32[]{:S(2)}, u32[]{:S(2)}) collective-permute-start(bf16[16,4096]{1,0:T(8,128)(2,1)S(1)} %get-tuple-element.24), channel_id=1, source_target_pairs={{0,192},{64,0},{128,64},{192,128},{1,193},{65,1},{129,65},{193,129... | collective-permute-start | bytes 393224 | tf_op jit(solution)/shard_map/ppermute | solution.py:22
  80.4 4.9 %collective-permute-start.7 = (bf16[16,4096]{1,0:T(8,128)(2,1)S(1)}, bf16[16,4096]{1,0:T(8,128)(2,1)S(1)}, u32[]{:S(2)}, u32[]{:S(2)}) collective-permute-start(bf16[16,4096]{1,0:T(8,128)(2,1)S(1)} %get-tuple-element.25), channel_id=1, source_target_pairs={{0,128},{64,192},{128,0},{192,64},{1,129},{65,193},{129,1},{193,65... | collective-permute-start | bytes 393224 | tf_op jit(solution)/shard_map/ppermute | solution.py:22
  86.8 2.1 %collective-permute-start.4 = (bf16[16,4096]{1,0:T(8,128)(2,1)S(1)}, bf16[16,4096]{1,0:T(8,128)(2,1)S(1)}, u32[]{:S(2)}, u32[]{:S(2)}) collective-permute-start(bf16[16,4096]{1,0:T(8,128)(2,1)S(1)} %fusion.9), channel_id=1, source_target_pairs={{0,128},{64,192},{128,0},{192,64},{1,129},{65,193},{129,1},{193,65... | collective-permute-start | bytes 393224 | tf_op jit(solution)/shard_map/ppermute | solution.py:27
  88.9 2.8 %collective-permute-start.3 = (bf16[16,4096]{1,0:T(8,128)(2,1)S(1)}, bf16[16,4096]{1,0:T(8,128)(2,1)S(1)}, u32[]{:S(2)}, u32[]{:S(2)}) collective-permute-start(bf16[16,4096]{1,0:T(8,128)(2,1)S(1)} %fusion.9), channel_id=1, source_target_pairs={{0,192},{64,0},{128,64},{192,128},{1,193},{65,1},{129,65},{193,129... | collective-permute-start | bytes 393224 | tf_op jit(solution)/shard_map/ppermute | solution.py:27
  91.7 10.8 %collective-permute-done.7 = bf16[16,4096]{1,0:T(8,128)(2,1)S(1)} collective-permute-done((bf16[16,4096]{1,0:T(8,128)(2,1)S(1)}, bf16[16,4096]{1,0:T(8,128)(2,1)S(1)}, u32[]{:S(2)}, u32[]{:S(2)}) %collective-permute-start.7) | collective-permute-done | bytes 131104 | tf_op jit(solution)/shard_map/ppermute | solution.py:22
  102.6 7.6 %collective-permute-start.11 = (bf16[16,4096]{1,0:T(8,128)(2,1)S(1)}, bf16[16,4096]{1,0:T(8,128)(2,1)S(1)}, u32[]{:S(2)}, u32[]{:S(2)}) collective-permute-start(bf16[16,4096]{1,0:T(8,128)(2,1)S(1)} %fusion.6), channel_id=1, source_target_pairs={{0,64},{64,128},{128,192},{192,0},{1,65},{65,129},{129,193},{193,1... | collective-permute-start | bytes 393224 | tf_op jit(solution)/shard_map/ppermute | solution.py:27
  110.1 7.1 %collective-permute-start.10 = (bf16[16,4096]{1,0:T(8,128)(2,1)S(1)}, bf16[16,4096]{1,0:T(8,128)(2,1)S(1)}, u32[]{:S(2)}, u32[]{:S(2)}) collective-permute-start(bf16[16,4096]{1,0:T(8,128)(2,1)S(1)} %fusion.6), channel_id=1, source_target_pairs={{0,128},{64,192},{128,0},{192,64},{1,129},{65,193},{129,1},{193,65... | collective-permute-start | bytes 393224 | tf_op jit(solution)/shard_map/ppermute | solution.py:27
  119.3 4.3 %collective-permute-done.10 = bf16[16,4096]{1,0:T(8,128)(2,1)S(1)} collective-permute-done((bf16[16,4096]{1,0:T(8,128)(2,1)S(1)}, bf16[16,4096]{1,0:T(8,128)(2,1)S(1)}, u32[]{:S(2)}, u32[]{:S(2)}) %collective-permute-start.10) | collective-permute-done | bytes 131104 | tf_op jit(solution)/shard_map/ppermute | solution.py:27
  123.6 2.4 %collective-permute-done.9 = bf16[16,4096]{1,0:T(8,128)(2,1)S(1)} collective-permute-done((bf16[16,4096]{1,0:T(8,128)(2,1)S(1)}, bf16[16,4096]{1,0:T(8,128)(2,1)S(1)}, u32[]{:S(2)}, u32[]{:S(2)}) %collective-permute-start.9) | collective-permute-done | bytes 131104 | tf_op jit(solution)/shard_map/ppermute | solution.py:27
  126.2 2.5 %fusion.2 = f32[2,2,64,4096]{3,2,1,0:T(8,128)} fusion(bf16[2,2,64,4096]{3,2,1,0:T(8,128)(2,1)S(1)} %copy-done, f32[1,2,64,4096]{3,2,1,0:T(8,128)S(1)} %bitcast.52, f32[1,2,64,4096]{3,2,1,0:T(8,128)S(1)} %bitcast.51, f32[64,4096]{1,0:T(8,128)S(1)} %get-tuple-element.29, f32[64,4096]{1,0:T(8,128)S(1)} %maximum_convert_fusion, ...), kind=kLoop, calls=%fused_computation.4 | loop fusion | flops 7340032 | bytes 15728640 | tf_op jit(solution)/shard_map/add | solution.py:138
  (38 shorter events, 6.5 us)
Async XLA Ops:
  9.3 31.5 %copy-start = (bf16[2,2,64,4096]{3,2,1,0:T(8,128)(2,1)S(1)}, bf16[2,2,64,4096]{3,2,1,0:T(8,128)(2,1)}, u32[]{:S(2)}) copy-start(bf16[2,2,64,4096]{3,2,1,0:T(8,128)(2,1)} %param.6) | copy-start | bytes 6291460
  9.3 31.5 %copy-start.7 = (f32[2]{0:T(128)S(1)}, f32[2]{0:T(128)}, u32[]{:S(2)}) copy-start(f32[2]{0:T(128)} %param.11) | copy-start | bytes 28
  9.3 23.6 %all-to-all-start = ((bf16[64,64,128]{2,1,0:T(8,128)(2,1)}), bf16[64,64,128]{2,1,0:T(8,128)(2,1)S(1)}, u32[]{:S(2)}, u32[]{:S(2)}) async-start(bf16[64,64,128]{2,1,0:T(8,128)(2,1)} %bitcast.43), calls=%async_computation | async-start | bytes 2097152 | tf_op jit(solution)/shard_map/all_to_all | solution.py:124
  33.0 10.3 %copy-start.2 = (bf16[64,64,128]{2,1,0:T(8,128)(2,1)}, bf16[64,64,128]{2,1,0:T(8,128)(2,1)S(1)}, u32[]{:S(2)}) copy-start(bf16[64,64,128]{2,1,0:T(8,128)(2,1)S(1)} %all-to-all-done) | copy-start | bytes 3145732
  33.0 25.2 %all-to-all-start.1 = ((bf16[64,64,128]{2,1,0:T(8,128)(2,1)}), bf16[64,64,128]{2,1,0:T(8,128)(2,1)}, u32[]{:S(2)}, u32[]{:S(2)}) async-start(bf16[64,64,128]{2,1,0:T(8,128)(2,1)} %bitcast.42), calls=%async_computation.1 | async-start | bytes 2097152 | tf_op jit(solution)/shard_map/all_to_all | solution.py:124
  41.6 1.7 %copy-start.3 = (f32[64,4096]{1,0:T(8,128)}, f32[64,4096]{1,0:T(8,128)S(1)}, u32[]{:S(2)}) copy-start(f32[64,4096]{1,0:T(8,128)S(1)} %fusion.3) | copy-start | bytes 3145732
  44.0 36.4 %collective-permute-start = (bf16[16,4096]{1,0:T(8,128)(2,1)}, bf16[16,4096]{1,0:T(8,128)(2,1)S(1)}, u32[]{:S(2)}, u32[]{:S(2)}) collective-permute-start(bf16[16,4096]{1,0:T(8,128)(2,1)} %get-tuple-element.26), channel_id=1, source_target_pairs={{0,64},{64,128},{128,192},{192,0},{1,65},{65,129},{129,193},{193,1... | collective-permute-start | bytes 393224 | tf_op jit(solution)/shard_map/ppermute | solution.py:22
  47.3 38.1 %collective-permute-start.2 = (bf16[16,4096]{1,0:T(8,128)(2,1)}, bf16[16,4096]{1,0:T(8,128)(2,1)S(1)}, u32[]{:S(2)}, u32[]{:S(2)}) collective-permute-start(bf16[16,4096]{1,0:T(8,128)(2,1)} %get-tuple-element.27), channel_id=1, source_target_pairs={{0,192},{64,0},{128,64},{192,128},{1,193},{65,1},{129,65},{193,129... | collective-permute-start | bytes 393224 | tf_op jit(solution)/shard_map/ppermute | solution.py:22
  49.4 35.9 %collective-permute-start.1 = (bf16[16,4096]{1,0:T(8,128)(2,1)S(1)}, bf16[16,4096]{1,0:T(8,128)(2,1)}, u32[]{:S(2)}, u32[]{:S(2)}) collective-permute-start(bf16[16,4096]{1,0:T(8,128)(2,1)S(1)} %get-tuple-element.28), channel_id=1, source_target_pairs={{0,128},{64,192},{128,0},{192,64},{1,129},{65,193},{129,1},{193,65... | collective-permute-start | bytes 393224 | tf_op jit(solution)/shard_map/ppermute | solution.py:22
  65.7 7.6 %copy-start.6 = (f32[64,4096]{1,0:T(8,128)S(1)}, f32[64,4096]{1,0:T(8,128)}, u32[]{:S(2)}) copy-start(f32[64,4096]{1,0:T(8,128)} %get-tuple-element.15) | copy-start | bytes 3145732
  73.4 45.2 %copy-start.1 = (s32[64,4096]{1,0:T(8,128)S(1)}, s32[64,4096]{1,0:T(8,128)}, u32[]{:S(2)}) copy-start(s32[64,4096]{1,0:T(8,128)} %m_ref.3) | copy-start | bytes 3145732
  74.9 14.1 %collective-permute-start.6 = (bf16[16,4096]{1,0:T(8,128)(2,1)S(1)}, bf16[16,4096]{1,0:T(8,128)(2,1)S(1)}, u32[]{:S(2)}, u32[]{:S(2)}) collective-permute-start(bf16[16,4096]{1,0:T(8,128)(2,1)S(1)} %get-tuple-element.23), channel_id=1, source_target_pairs={{0,64},{64,128},{128,192},{192,0},{1,65},{65,129},{129,193},{193,1... | collective-permute-start | bytes 393224 | tf_op jit(solution)/shard_map/ppermute | solution.py:22
  78.2 13.5 %collective-permute-start.8 = (bf16[16,4096]{1,0:T(8,128)(2,1)S(1)}, bf16[16,4096]{1,0:T(8,128)(2,1)S(1)}, u32[]{:S(2)}, u32[]{:S(2)}) collective-permute-start(bf16[16,4096]{1,0:T(8,128)(2,1)S(1)} %get-tuple-element.24), channel_id=1, source_target_pairs={{0,192},{64,0},{128,64},{192,128},{1,193},{65,1},{129,65},{193,129... | collective-permute-start | bytes 393224 | tf_op jit(solution)/shard_map/ppermute | solution.py:22
  80.4 22.1 %collective-permute-start.7 = (bf16[16,4096]{1,0:T(8,128)(2,1)S(1)}, bf16[16,4096]{1,0:T(8,128)(2,1)S(1)}, u32[]{:S(2)}, u32[]{:S(2)}) collective-permute-start(bf16[16,4096]{1,0:T(8,128)(2,1)S(1)} %get-tuple-element.25), channel_id=1, source_target_pairs={{0,128},{64,192},{128,0},{192,64},{1,129},{65,193},{129,1},{193,65... | collective-permute-start | bytes 393224 | tf_op jit(solution)/shard_map/ppermute | solution.py:22
  86.5 30.8 %collective-permute-start.5 = (bf16[16,4096]{1,0:T(8,128)(2,1)S(1)}, bf16[16,4096]{1,0:T(8,128)(2,1)S(1)}, u32[]{:S(2)}, u32[]{:S(2)}) collective-permute-start(bf16[16,4096]{1,0:T(8,128)(2,1)S(1)} %fusion.9), channel_id=1, source_target_pairs={{0,64},{64,128},{128,192},{192,0},{1,65},{65,129},{129,193},{193,1... | collective-permute-start | bytes 393224 | tf_op jit(solution)/shard_map/ppermute | solution.py:27
  86.8 31.7 %collective-permute-start.4 = (bf16[16,4096]{1,0:T(8,128)(2,1)S(1)}, bf16[16,4096]{1,0:T(8,128)(2,1)S(1)}, u32[]{:S(2)}, u32[]{:S(2)}) collective-permute-start(bf16[16,4096]{1,0:T(8,128)(2,1)S(1)} %fusion.9), channel_id=1, source_target_pairs={{0,128},{64,192},{128,0},{192,64},{1,129},{65,193},{129,1},{193,65... | collective-permute-start | bytes 393224 | tf_op jit(solution)/shard_map/ppermute | solution.py:27
  88.9 29.6 %collective-permute-start.3 = (bf16[16,4096]{1,0:T(8,128)(2,1)S(1)}, bf16[16,4096]{1,0:T(8,128)(2,1)S(1)}, u32[]{:S(2)}, u32[]{:S(2)}) collective-permute-start(bf16[16,4096]{1,0:T(8,128)(2,1)S(1)} %fusion.9), channel_id=1, source_target_pairs={{0,192},{64,0},{128,64},{192,128},{1,193},{65,1},{129,65},{193,129... | collective-permute-start | bytes 393224 | tf_op jit(solution)/shard_map/ppermute | solution.py:27
  102.6 16.7 %collective-permute-start.11 = (bf16[16,4096]{1,0:T(8,128)(2,1)S(1)}, bf16[16,4096]{1,0:T(8,128)(2,1)S(1)}, u32[]{:S(2)}, u32[]{:S(2)}) collective-permute-start(bf16[16,4096]{1,0:T(8,128)(2,1)S(1)} %fusion.6), channel_id=1, source_target_pairs={{0,64},{64,128},{128,192},{192,0},{1,65},{65,129},{129,193},{193,1... | collective-permute-start | bytes 393224 | tf_op jit(solution)/shard_map/ppermute | solution.py:27
  110.1 13.5 %collective-permute-start.10 = (bf16[16,4096]{1,0:T(8,128)(2,1)S(1)}, bf16[16,4096]{1,0:T(8,128)(2,1)S(1)}, u32[]{:S(2)}, u32[]{:S(2)}) collective-permute-start(bf16[16,4096]{1,0:T(8,128)(2,1)S(1)} %fusion.6), channel_id=1, source_target_pairs={{0,128},{64,192},{128,0},{192,64},{1,129},{65,193},{129,1},{193,65... | collective-permute-start | bytes 393224 | tf_op jit(solution)/shard_map/ppermute | solution.py:27
  117.3 8.7 %collective-permute-start.9 = (bf16[16,4096]{1,0:T(8,128)(2,1)S(1)}, bf16[16,4096]{1,0:T(8,128)(2,1)S(1)}, u32[]{:S(2)}, u32[]{:S(2)}) collective-permute-start(bf16[16,4096]{1,0:T(8,128)(2,1)S(1)} %fusion.6), channel_id=1, source_target_pairs={{0,192},{64,0},{128,64},{192,128},{1,193},{65,1},{129,65},{193,129... | collective-permute-start | bytes 393224 | tf_op jit(solution)/shard_map/ppermute | solution.py:27
  118.6 7.6 %copy-start.4 = (f32[2,64,4096]{2,1,0:T(8,128)S(1)}, f32[2,64,4096]{2,1,0:T(8,128)}, u32[]{:S(2)}) copy-start(f32[2,64,4096]{2,1,0:T(8,128)} %get-tuple-element.12) | copy-start | bytes 6291460
  118.6 7.6 %copy-start.5 = (f32[2,64,4096]{2,1,0:T(8,128)S(1)}, f32[2,64,4096]{2,1,0:T(8,128)}, u32[]{:S(2)}) copy-start(f32[2,64,4096]{2,1,0:T(8,128)} %get-tuple-element.14) | copy-start | bytes 6291460

commit v8 on v6

--- a/solution.py
+++ b/solution.py
@@ -6,7 +6,7 @@
 from jax.sharding import PartitionSpec as P
 
 BLK = 128
-GROUP = 4
+GROUP = 8
 INTERPRET = False
 
 
@@ -70,13 +70,13 @@
         total = jnp.zeros((half, BLK), jnp.float32)
         for q in range(count):
             tile = slice((q // 2) * BLK, (q // 2 + 1) * BLK)
-            first = r_ref[2 * b * half:(2 * b + 1) * half, tile].astype(jnp.float32)
-            second = r_ref[(2 * b + 1) * half:(2 * b + 2) * half, tile].astype(jnp.float32)
+            first = r_ref[2 * b * half:(2 * b + 1) * half, tile]
+            second = r_ref[(2 * b + 1) * half:(2 * b + 2) * half, tile]
             if q % 2 == 0:
                 joined = jnp.where(low, first, pltpu.roll(second, half, 1))
             else:
                 joined = jnp.where(low, pltpu.roll(first, half, 1), second)
-            joined = jnp.where(sea, joined, 0.0).astype(jnp.bfloat16)
+            joined = jnp.where(sea, joined, jnp.zeros_like(joined))
             out = lax.dot_general(joined, weight, (((1,), (1,)), ((), ())), preferred_element_type=jnp.float32)
             g_ref[q, :, cols] = out
             total = total + out * v_ref[q, :, cols].astype(jnp.float32)

time: 113 us -> 109 us (0.965)
  Pallas kernels: 15.7 us -> 11.8 us
    pallas_call x1, Pallas kernels: 6.73 us -> 4.62 us  [x_solve(): pl.pallas_call(x_solve_kernel, grid=(nblocks // GROUP,), in_specs=[pl.Blo...]
    pallas_call x1, Pallas kernels: 8.98 us -> 7.18 us  [y_solve(): pl.pallas_call(y_solve_kernel, grid=(nblocks // GROUP,), in_specs=[pl.Blo...]
  transfers between devices with their start and end apart: 13 -> 13, of which waited for: 3 -> 3; matrix products, arithmetic and copies ran while one was open for 4% -> 4% of each run, Pallas kernels for 8% -> 7%
where the time goes in v8:
time: 109 us; the launch traced here: 108 us
  waiting for transfers between devices  51.4 us (47%)
  starting transfers between devices  36.6 us (34%)
  Pallas kernels  11.8 us (11%)
  other arithmetic  6.84 us (6%)
  local copies, waits for them, and re-layouts  1.22 us (1%)
    all_to_all x1, waiting for transfers between devices, local(): lax.all_to_all(across, 'grid', split_axis=0, concat_axis=0, tiled=True)  24.6 us
    ppermute x6, waiting for transfers between devices, con_sum(): lax.ppermute(piece.astype(link_type), 'con', pairs).astype(jnp.float32)  21.3 us
    ppermute x6, starting transfers between devices, con_sum(): lax.ppermute(piece.astype(link_type), 'con', pairs).astype(jnp.float32)  15.7 us
    ppermute x6, starting transfers between devices, con_sum(): pieces.append(lax.ppermute(mine, 'con', pairs))  11.8 us
    all_to_all x1, starting transfers between devices, local(): lax.all_to_all(across, 'grid', split_axis=0, concat_axis=0, tiled=True)  9.12 us
    pallas_call x1, Pallas kernels, y_solve(): pl.pallas_call(y_solve_kernel, grid=(nblocks // GROUP,), in_specs=[pl.Blo...  7.18 us
    ppermute x6, waiting for transfers between devices, con_sum(): pieces.append(lax.ppermute(mine, 'con', pairs))  5.51 us
    pallas_call x1, Pallas kernels, x_solve(): pl.pallas_call(x_solve_kernel, grid=(nblocks // GROUP,), in_specs=[pl.Blo...  4.62 us
  transfers between devices with their start and end apart: 13, of which 3 were waited for; matrix products, arithmetic and copies ran while one was open for 4% of the time, Pallas kernels for 7%

profile of v8, /device:TPU:48, one launch (start us, length us, event | category | flops | bytes accessed | tf_op | source)
XLA Modules:
  0.0 108.2 jit_solution(10121771507828003238)
XLA Ops:
  0.0 4.6 %shard_map.64 = bf16[4096,256]{1,0:T(8,128)(2,1)} custom-call(bf16[256,4096]{1,0:T(8,128)(2,1)} %bitcast.40, bf16[32,128,128]{2,1,0:T(8,128)(2,1)} %w_ref.2), custom_call_target="tpu_custom_call" | custom-call | tf_op jit(solution)/shard_map/pallas_call | solution.py:48
  4.6 9.1 %all-to-all-start = ((bf16[64,64,256]{2,1,0:T(8,128)(2,1)}), bf16[64,64,256]{2,1,0:T(8,128)(2,1)}, u32[]{:S(2)}, u32[]{:S(2)}) async-start(bf16[64,64,256]{2,1,0:T(8,128)(2,1)} %bitcast.36), calls=%async_computation | async-start | bytes 4194304 | tf_op jit(solution)/shard_map/all_to_all | solution.py:120
  13.9 0.7 fusion.3
  14.6 24.6 %all-to-all-done = bf16[64,64,256]{2,1,0:T(8,128)(2,1)} async-done(((bf16[64,64,256]{2,1,0:T(8,128)(2,1)}), bf16[64,64,256]{2,1,0:T(8,128)(2,1)}, u32[]{:S(2)}, u32[]{:S(2)}) %all-to-all-start) | async-done | bytes 2097184 | tf_op jit(solution)/shard_map/all_to_all | solution.py:120
  39.2 3.3 %collective-permute-start = (bf16[16,4096]{1,0:T(8,128)(2,1)S(1)}, bf16[16,4096]{1,0:T(8,128)(2,1)S(1)}, u32[]{:S(2)}, u32[]{:S(2)}) collective-permute-start(bf16[16,4096]{1,0:T(8,128)(2,1)S(1)} %get-tuple-element.18), channel_id=1, source_target_pairs={{0,64},{64,128},{128,192},{192,0},{1,65},{65,129},{129,193},{193,1... | collective-permute-start | bytes 393224 | tf_op jit(solution)/shard_map/ppermute | solution.py:22
  42.6 2.2 %collective-permute-start.2 = (bf16[16,4096]{1,0:T(8,128)(2,1)S(1)}, bf16[16,4096]{1,0:T(8,128)(2,1)S(1)}, u32[]{:S(2)}, u32[]{:S(2)}) collective-permute-start(bf16[16,4096]{1,0:T(8,128)(2,1)S(1)} %get-tuple-element.19), channel_id=1, source_target_pairs={{0,192},{64,0},{128,64},{192,128},{1,193},{65,1},{129,65},{193,129... | collective-permute-start | bytes 393224 | tf_op jit(solution)/shard_map/ppermute | solution.py:22
  44.8 4.9 %collective-permute-start.1 = (bf16[16,4096]{1,0:T(8,128)(2,1)S(1)}, bf16[16,4096]{1,0:T(8,128)(2,1)S(1)}, u32[]{:S(2)}, u32[]{:S(2)}) collective-permute-start(bf16[16,4096]{1,0:T(8,128)(2,1)S(1)} %get-tuple-element.20), channel_id=1, source_target_pairs={{0,128},{64,192},{128,0},{192,64},{1,129},{65,193},{129,1},{193,65... | collective-permute-start | bytes 393224 | tf_op jit(solution)/shard_map/ppermute | solution.py:22
  49.7 7.2 %shard_map.65 = (f32[4,64,4096]{2,1,0:T(8,128)}, f32[64,4096]{1,0:T(8,128)}) custom-call(bf16[4096,256]{1,0:T(8,128)(2,1)} %bitcast.2.r_ref, s32[64,4096]{1,0:T(8,128)} %m_ref.1, bf16[32,128,128]{2,1,0:T(8,128)(2,1)} %w_ref.3, bf16[4,64,4096]{2,1,0:T(8,128)(2,1)} %bitcast.35), custom_call_target="tpu_custom_call" | custom-call | tf_op jit(solution)/shard_map/pallas_call | solution.py:89
  56.9 1.1 %fusion.13 = (bf16[16,4096]{1,0:T(8,128)(2,1)S(1)}, bf16[16,4096]{1,0:T(8,128)(2,1)S(1)}, bf16[16,4096]{1,0:T(8,128)(2,1)S(1)}) fusion(f32[4,16,4096]{2,1,0:T(8,128)} %bitcast.41, s32[]{:T(128)S(6)} %select_n.188, s32[]{:T(128)S(6)} %select_n.192, s32[]{:T(128)S(6)} %select_n.190), kind=kLoop, calls=%fused_computation.27 | loop fusion | bytes 786444 | tf_op jit(solution)/shard_map/convert_element_type | solution.py:22
  58.0 0.3 collective-permute-start.6
  58.4 3.9 %collective-permute-start.8 = (bf16[16,4096]{1,0:T(8,128)(2,1)S(1)}, bf16[16,4096]{1,0:T(8,128)(2,1)S(1)}, u32[]{:S(2)}, u32[]{:S(2)}) collective-permute-start(bf16[16,4096]{1,0:T(8,128)(2,1)S(1)} %get-tuple-element.16), channel_id=1, source_target_pairs={{0,192},{64,0},{128,64},{192,128},{1,193},{65,1},{129,65},{193,129... | collective-permute-start | bytes 393224 | tf_op jit(solution)/shard_map/ppermute | solution.py:22
  62.3 1.0 collective-permute-start.7
  63.3 1.0 fusion.9
  64.3 1.4 %collective-permute-start.5 = (bf16[16,4096]{1,0:T(8,128)(2,1)S(1)}, bf16[16,4096]{1,0:T(8,128)(2,1)S(1)}, u32[]{:S(2)}, u32[]{:S(2)}) collective-permute-start(bf16[16,4096]{1,0:T(8,128)(2,1)S(1)} %fusion.9), channel_id=1, source_target_pairs={{0,64},{64,128},{128,192},{192,0},{1,65},{65,129},{129,193},{193,1... | collective-permute-start | bytes 393224 | tf_op jit(solution)/shard_map/ppermute | solution.py:27
  65.7 3.7 %collective-permute-start.4 = (bf16[16,4096]{1,0:T(8,128)(2,1)S(1)}, bf16[16,4096]{1,0:T(8,128)(2,1)S(1)}, u32[]{:S(2)}, u32[]{:S(2)}) collective-permute-start(bf16[16,4096]{1,0:T(8,128)(2,1)S(1)} %fusion.9), channel_id=1, source_target_pairs={{0,128},{64,192},{128,0},{192,64},{1,129},{65,193},{129,1},{193,65... | collective-permute-start | bytes 393224 | tf_op jit(solution)/shard_map/ppermute | solution.py:27
  69.4 21.3 %collective-permute-done.6 = bf16[16,4096]{1,0:T(8,128)(2,1)S(1)} collective-permute-done((bf16[16,4096]{1,0:T(8,128)(2,1)S(1)}, bf16[16,4096]{1,0:T(8,128)(2,1)S(1)}, u32[]{:S(2)}, u32[]{:S(2)}) %collective-permute-start.6) | collective-permute-done | bytes 131104 | tf_op jit(solution)/shard_map/ppermute | solution.py:22
  90.7 1.0 fusion.6
  91.8 3.0 %collective-permute-start.11 = (bf16[16,4096]{1,0:T(8,128)(2,1)S(1)}, bf16[16,4096]{1,0:T(8,128)(2,1)S(1)}, u32[]{:S(2)}, u32[]{:S(2)}) collective-permute-start(bf16[16,4096]{1,0:T(8,128)(2,1)S(1)} %fusion.6), channel_id=1, source_target_pairs={{0,64},{64,128},{128,192},{192,0},{1,65},{65,129},{129,193},{193,1... | collective-permute-start | bytes 393224 | tf_op jit(solution)/shard_map/ppermute | solution.py:27
  94.8 3.7 %collective-permute-start.9 = (bf16[16,4096]{1,0:T(8,128)(2,1)S(1)}, bf16[16,4096]{1,0:T(8,128)(2,1)S(1)}, u32[]{:S(2)}, u32[]{:S(2)}) collective-permute-start(bf16[16,4096]{1,0:T(8,128)(2,1)S(1)} %fusion.6), channel_id=1, source_target_pairs={{0,192},{64,0},{128,64},{192,128},{1,193},{65,1},{129,65},{193,129... | collective-permute-start | bytes 393224 | tf_op jit(solution)/shard_map/ppermute | solution.py:27
  98.5 0.4 fusion.16
  99.0 0.3 broadcast_multiply_fusion
  99.3 5.5 %collective-permute-done.10 = bf16[16,4096]{1,0:T(8,128)(2,1)S(1)} collective-permute-done((bf16[16,4096]{1,0:T(8,128)(2,1)S(1)}, bf16[16,4096]{1,0:T(8,128)(2,1)S(1)}, u32[]{:S(2)}, u32[]{:S(2)}) %collective-permute-start.10) | collective-permute-done | bytes 131104 | tf_op jit(solution)/shard_map/ppermute | solution.py:27
  104.9 0.1 maximum_convert_fusion
  105.0 3.2 %fusion.2 = f32[2,2,64,4096]{3,2,1,0:T(8,128)} fusion(bf16[2,2,64,4096]{3,2,1,0:T(8,128)(2,1)S(1)} %copy-done.1, f32[2,2,64,4096]{3,2,1,0:T(8,128)S(1)} %bitcast.37, f32[64,4096]{1,0:T(8,128)S(1)} %get-tuple-element.21, f32[64,4096]{1,0:T(8,128)S(1)} %maximum_convert_fusion, f32[2,64,4096]{2,1,0:T(8,128)S(1)} %broadcast_multiply_fusion, ...), kind=kLoop, calls=%fused_computation.4 | loop fusion | flops 6291456 | bytes 15728640 | tf_op jit(solution)/shard_map/add | solution.py:129
  (27 shorter events, 0.2 us)
Async XLA Ops:
  0.0 13.9 %copy-start = (bf16[2,2,64,4096]{3,2,1,0:T(8,128)(2,1)S(1)}, bf16[2,2,64,4096]{3,2,1,0:T(8,128)(2,1)}, u32[]{:S(2)}) copy-start(bf16[2,2,64,4096]{3,2,1,0:T(8,128)(2,1)} %param.6) | copy-start | bytes 6291460
  0.0 13.9 %copy-start.5 = (f32[2]{0:T(128)S(1)}, f32[2]{0:T(128)}, u32[]{:S(2)}) copy-start(f32[2]{0:T(128)} %param.11) | copy-start | bytes 28
  4.6 34.5 %all-to-all-start = ((bf16[64,64,256]{2,1,0:T(8,128)(2,1)}), bf16[64,64,256]{2,1,0:T(8,128)(2,1)}, u32[]{:S(2)}, u32[]{:S(2)}) async-start(bf16[64,64,256]{2,1,0:T(8,128)(2,1)} %bitcast.36), calls=%async_computation | async-start | bytes 4194304 | tf_op jit(solution)/shard_map/all_to_all | solution.py:120
  14.6 35.1 %copy-start.4 = (f32[64,4096]{1,0:T(8,128)}, f32[64,4096]{1,0:T(8,128)S(1)}, u32[]{:S(2)}) copy-start(f32[64,4096]{1,0:T(8,128)S(1)} %fusion.3) | copy-start | bytes 3145732
  39.2 23.1 %collective-permute-start = (bf16[16,4096]{1,0:T(8,128)(2,1)S(1)}, bf16[16,4096]{1,0:T(8,128)(2,1)S(1)}, u32[]{:S(2)}, u32[]{:S(2)}) collective-permute-start(bf16[16,4096]{1,0:T(8,128)(2,1)S(1)} %get-tuple-element.18), channel_id=1, source_target_pairs={{0,64},{64,128},{128,192},{192,0},{1,65},{65,129},{129,193},{193,1... | collective-permute-start | bytes 393224 | tf_op jit(solution)/shard_map/ppermute | solution.py:22
  42.6 20.7 %collective-permute-start.2 = (bf16[16,4096]{1,0:T(8,128)(2,1)S(1)}, bf16[16,4096]{1,0:T(8,128)(2,1)S(1)}, u32[]{:S(2)}, u32[]{:S(2)}) collective-permute-start(bf16[16,4096]{1,0:T(8,128)(2,1)S(1)} %get-tuple-element.19), channel_id=1, source_target_pairs={{0,192},{64,0},{128,64},{192,128},{1,193},{65,1},{129,65},{193,129... | collective-permute-start | bytes 393224 | tf_op jit(solution)/shard_map/ppermute | solution.py:22
  44.8 18.5 %collective-permute-start.1 = (bf16[16,4096]{1,0:T(8,128)(2,1)S(1)}, bf16[16,4096]{1,0:T(8,128)(2,1)S(1)}, u32[]{:S(2)}, u32[]{:S(2)}) collective-permute-start(bf16[16,4096]{1,0:T(8,128)(2,1)S(1)} %get-tuple-element.20), channel_id=1, source_target_pairs={{0,128},{64,192},{128,0},{192,64},{1,129},{65,193},{129,1},{193,65... | collective-permute-start | bytes 393224 | tf_op jit(solution)/shard_map/ppermute | solution.py:22
  49.7 48.8 %copy-start.3 = (s32[64,4096]{1,0:T(8,128)S(1)}, s32[64,4096]{1,0:T(8,128)}, u32[]{:S(2)}) copy-start(s32[64,4096]{1,0:T(8,128)} %m_ref.1) | copy-start | bytes 3145732
  58.0 32.7 %collective-permute-start.6 = (bf16[16,4096]{1,0:T(8,128)(2,1)S(1)}, bf16[16,4096]{1,0:T(8,128)(2,1)S(1)}, u32[]{:S(2)}, u32[]{:S(2)}) collective-permute-start(bf16[16,4096]{1,0:T(8,128)(2,1)S(1)} %get-tuple-element.15), channel_id=1, source_target_pairs={{0,64},{64,128},{128,192},{192,0},{1,65},{65,129},{129,193},{193,1... | collective-permute-start | bytes 393224 | tf_op jit(solution)/shard_map/ppermute | solution.py:22
  58.4 32.3 %collective-permute-start.8 = (bf16[16,4096]{1,0:T(8,128)(2,1)S(1)}, bf16[16,4096]{1,0:T(8,128)(2,1)S(1)}, u32[]{:S(2)}, u32[]{:S(2)}) collective-permute-start(bf16[16,4096]{1,0:T(8,128)(2,1)S(1)} %get-tuple-element.16), channel_id=1, source_target_pairs={{0,192},{64,0},{128,64},{192,128},{1,193},{65,1},{129,65},{193,129... | collective-permute-start | bytes 393224 | tf_op jit(solution)/shard_map/ppermute | solution.py:22
  62.3 28.5 %collective-permute-start.7 = (bf16[16,4096]{1,0:T(8,128)(2,1)S(1)}, bf16[16,4096]{1,0:T(8,128)(2,1)S(1)}, u32[]{:S(2)}, u32[]{:S(2)}) collective-permute-start(bf16[16,4096]{1,0:T(8,128)(2,1)S(1)} %get-tuple-element.17), channel_id=1, source_target_pairs={{0,128},{64,192},{128,0},{192,64},{1,129},{65,193},{129,1},{193,65... | collective-permute-start | bytes 393224 | tf_op jit(solution)/shard_map/ppermute | solution.py:22
  64.3 30.5 %collective-permute-start.5 = (bf16[16,4096]{1,0:T(8,128)(2,1)S(1)}, bf16[16,4096]{1,0:T(8,128)(2,1)S(1)}, u32[]{:S(2)}, u32[]{:S(2)}) collective-permute-start(bf16[16,4096]{1,0:T(8,128)(2,1)S(1)} %fusion.9), channel_id=1, source_target_pairs={{0,64},{64,128},{128,192},{192,0},{1,65},{65,129},{129,193},{193,1... | collective-permute-start | bytes 393224 | tf_op jit(solution)/shard_map/ppermute | solution.py:27
  65.7 32.7 %collective-permute-start.4 = (bf16[16,4096]{1,0:T(8,128)(2,1)S(1)}, bf16[16,4096]{1,0:T(8,128)(2,1)S(1)}, u32[]{:S(2)}, u32[]{:S(2)}) collective-permute-start(bf16[16,4096]{1,0:T(8,128)(2,1)S(1)} %fusion.9), channel_id=1, source_target_pairs={{0,128},{64,192},{128,0},{192,64},{1,129},{65,193},{129,1},{193,65... | collective-permute-start | bytes 393224 | tf_op jit(solution)/shard_map/ppermute | solution.py:27
  90.7 7.7 %collective-permute-start.3 = (bf16[16,4096]{1,0:T(8,128)(2,1)S(1)}, bf16[16,4096]{1,0:T(8,128)(2,1)S(1)}, u32[]{:S(2)}, u32[]{:S(2)}) collective-permute-start(bf16[16,4096]{1,0:T(8,128)(2,1)S(1)} %fusion.9), channel_id=1, source_target_pairs={{0,192},{64,0},{128,64},{192,128},{1,193},{65,1},{129,65},{193,129... | collective-permute-start | bytes 393224 | tf_op jit(solution)/shard_map/ppermute | solution.py:27
  91.8 7.5 %collective-permute-start.11 = (bf16[16,4096]{1,0:T(8,128)(2,1)S(1)}, bf16[16,4096]{1,0:T(8,128)(2,1)S(1)}, u32[]{:S(2)}, u32[]{:S(2)}) collective-permute-start(bf16[16,4096]{1,0:T(8,128)(2,1)S(1)} %fusion.6), channel_id=1, source_target_pairs={{0,64},{64,128},{128,192},{192,0},{1,65},{65,129},{129,193},{193,1... | collective-permute-start | bytes 393224 | tf_op jit(solution)/shard_map/ppermute | solution.py:27
  94.8 10.0 %collective-permute-start.10 = (bf16[16,4096]{1,0:T(8,128)(2,1)S(1)}, bf16[16,4096]{1,0:T(8,128)(2,1)S(1)}, u32[]{:S(2)}, u32[]{:S(2)}) collective-permute-start(bf16[16,4096]{1,0:T(8,128)(2,1)S(1)} %fusion.6), channel_id=1, source_target_pairs={{0,128},{64,192},{128,0},{192,64},{1,129},{65,193},{129,1},{193,65... | collective-permute-start | bytes 393224 | tf_op jit(solution)/shard_map/ppermute | solution.py:27
  94.8 10.0 %collective-permute-start.9 = (bf16[16,4096]{1,0:T(8,128)(2,1)S(1)}, bf16[16,4096]{1,0:T(8,128)(2,1)S(1)}, u32[]{:S(2)}, u32[]{:S(2)}) collective-permute-start(bf16[16,4096]{1,0:T(8,128)(2,1)S(1)} %fusion.6), channel_id=1, source_target_pairs={{0,192},{64,0},{128,64},{192,128},{1,193},{65,1},{129,65},{193,129... | collective-permute-start | bytes 393224 | tf_op jit(solution)/shard_map/ppermute | solution.py:27
  98.5 6.4 %copy-start.1 = (bf16[2,2,64,4096]{3,2,1,0:T(8,128)(2,1)S(1)}, bf16[2,2,64,4096]{3,2,1,0:T(8,128)(2,1)}, u32[]{:S(2)}) copy-start(bf16[2,2,64,4096]{3,2,1,0:T(8,128)(2,1)} %param.6) | copy-start | bytes 6291460
  98.5 6.4 %copy-start.2 = (f32[4,64,4096]{2,1,0:T(8,128)S(1)}, f32[4,64,4096]{2,1,0:T(8,128)}, u32[]{:S(2)}) copy-start(f32[4,64,4096]{2,1,0:T(8,128)} %get-tuple-element.11) | copy-start | bytes 12582916

commit v9 on v8

--- a/solution.py
+++ b/solution.py
@@ -6,7 +6,7 @@
 from jax.sharding import PartitionSpec as P
 
 BLK = 128
-GROUP = 8
+GROUP = 16
 INTERPRET = False
 
 

time: 109 us -> 107 us (0.982)
  Pallas kernels: 11.8 us -> 10.1 us
    pallas_call x1, Pallas kernels: 4.62 us -> 3.4 us  [x_solve(): pl.pallas_call(x_solve_kernel, grid=(nblocks // GROUP,), in_specs=[pl.Blo...]
  transfers between devices with their start and end apart: 13 -> 13, of which waited for: 3 -> 3; matrix products, arithmetic and copies ran while one was open for 4% -> 4% of each run, Pallas kernels for 7% -> 6%
where the time goes in v9:
time: 107 us; the launch traced here: 106 us
  waiting for transfers between devices  51.4 us (48%)
  starting transfers between devices  36.6 us (34%)
  Pallas kernels  10.1 us (9%)
  other arithmetic  6.84 us (6%)
  local copies, waits for them, and re-layouts  1.22 us (1%)
    all_to_all x1, waiting for transfers between devices, local(): lax.all_to_all(across, 'grid', split_axis=0, concat_axis=0, tiled=True)  24.6 us
    ppermute x6, waiting for transfers between devices, con_sum(): lax.ppermute(piece.astype(link_type), 'con', pairs).astype(jnp.float32)  21.4 us
    ppermute x6, starting transfers between devices, con_sum(): lax.ppermute(piece.astype(link_type), 'con', pairs).astype(jnp.float32)  15.7 us
    ppermute x6, starting transfers between devices, con_sum(): pieces.append(lax.ppermute(mine, 'con', pairs))  11.8 us
    all_to_all x1, starting transfers between devices, local(): lax.all_to_all(across, 'grid', split_axis=0, concat_axis=0, tiled=True)  9.12 us
    pallas_call x1, Pallas kernels, y_solve(): pl.pallas_call(y_solve_kernel, grid=(nblocks // GROUP,), in_specs=[pl.Blo...  6.71 us
    ppermute x6, waiting for transfers between devices, con_sum(): pieces.append(lax.ppermute(mine, 'con', pairs))  5.51 us
    pallas_call x1, Pallas kernels, x_solve(): pl.pallas_call(x_solve_kernel, grid=(nblocks // GROUP,), in_specs=[pl.Blo...  3.4 us
  transfers between devices with their start and end apart: 13, of which 3 were waited for; matrix products, arithmetic and copies ran while one was open for 4% of the time, Pallas kernels for 6%

profile of v9, /device:TPU:48, one launch (start us, length us, event | category | flops | bytes accessed | tf_op | source)
XLA Modules:
  0.0 106.5 jit_solution(11022462380740861997)
XLA Ops:
  0.0 3.4 %shard_map.64 = bf16[4096,256]{1,0:T(8,128)(2,1)} custom-call(bf16[256,4096]{1,0:T(8,128)(2,1)} %bitcast.40, bf16[32,128,128]{2,1,0:T(8,128)(2,1)} %w_ref.2), custom_call_target="tpu_custom_call" | custom-call | tf_op jit(solution)/shard_map/pallas_call | solution.py:48
  3.4 9.1 %all-to-all-start = ((bf16[64,64,256]{2,1,0:T(8,128)(2,1)}), bf16[64,64,256]{2,1,0:T(8,128)(2,1)}, u32[]{:S(2)}, u32[]{:S(2)}) async-start(bf16[64,64,256]{2,1,0:T(8,128)(2,1)} %bitcast.36), calls=%async_computation | async-start | bytes 4194304 | tf_op jit(solution)/shard_map/all_to_all | solution.py:120
  12.7 0.7 fusion.3
  13.4 24.6 %all-to-all-done = bf16[64,64,256]{2,1,0:T(8,128)(2,1)} async-done(((bf16[64,64,256]{2,1,0:T(8,128)(2,1)}), bf16[64,64,256]{2,1,0:T(8,128)(2,1)}, u32[]{:S(2)}, u32[]{:S(2)}) %all-to-all-start) | async-done | bytes 2097184 | tf_op jit(solution)/shard_map/all_to_all | solution.py:120
  38.0 3.3 %collective-permute-start = (bf16[16,4096]{1,0:T(8,128)(2,1)S(1)}, bf16[16,4096]{1,0:T(8,128)(2,1)S(1)}, u32[]{:S(2)}, u32[]{:S(2)}) collective-permute-start(bf16[16,4096]{1,0:T(8,128)(2,1)S(1)} %get-tuple-element.18), channel_id=1, source_target_pairs={{0,64},{64,128},{128,192},{192,0},{1,65},{65,129},{129,193},{193,1... | collective-permute-start | bytes 393224 | tf_op jit(solution)/shard_map/ppermute | solution.py:22
  41.3 2.2 %collective-permute-start.2 = (bf16[16,4096]{1,0:T(8,128)(2,1)S(1)}, bf16[16,4096]{1,0:T(8,128)(2,1)S(1)}, u32[]{:S(2)}, u32[]{:S(2)}) collective-permute-start(bf16[16,4096]{1,0:T(8,128)(2,1)S(1)} %get-tuple-element.19), channel_id=1, source_target_pairs={{0,192},{64,0},{128,64},{192,128},{1,193},{65,1},{129,65},{193,129... | collective-permute-start | bytes 393224 | tf_op jit(solution)/shard_map/ppermute | solution.py:22
  43.6 4.9 %collective-permute-start.1 = (bf16[16,4096]{1,0:T(8,128)(2,1)S(1)}, bf16[16,4096]{1,0:T(8,128)(2,1)S(1)}, u32[]{:S(2)}, u32[]{:S(2)}) collective-permute-start(bf16[16,4096]{1,0:T(8,128)(2,1)S(1)} %get-tuple-element.20), channel_id=1, source_target_pairs={{0,128},{64,192},{128,0},{192,64},{1,129},{65,193},{129,1},{193,65... | collective-permute-start | bytes 393224 | tf_op jit(solution)/shard_map/ppermute | solution.py:22
  48.5 6.7 %shard_map.65 = (f32[4,64,4096]{2,1,0:T(8,128)}, f32[64,4096]{1,0:T(8,128)}) custom-call(bf16[4096,256]{1,0:T(8,128)(2,1)} %bitcast.2.r_ref, s32[64,4096]{1,0:T(8,128)} %m_ref.1, bf16[32,128,128]{2,1,0:T(8,128)(2,1)} %w_ref.3, bf16[4,64,4096]{2,1,0:T(8,128)(2,1)} %bitcast.35), custom_call_target="tpu_custom_call" | custom-call | tf_op jit(solution)/shard_map/pallas_call | solution.py:89
  55.2 1.1 %fusion.13 = (bf16[16,4096]{1,0:T(8,128)(2,1)S(1)}, bf16[16,4096]{1,0:T(8,128)(2,1)S(1)}, bf16[16,4096]{1,0:T(8,128)(2,1)S(1)}) fusion(f32[4,16,4096]{2,1,0:T(8,128)} %bitcast.41, s32[]{:T(128)S(6)} %select_n.188, s32[]{:T(128)S(6)} %select_n.192, s32[]{:T(128)S(6)} %select_n.190), kind=kLoop, calls=%fused_computation.27 | loop fusion | bytes 786444 | tf_op jit(solution)/shard_map/convert_element_type | solution.py:22
  56.4 0.3 collective-permute-start.6
  56.7 3.9 %collective-permute-start.8 = (bf16[16,4096]{1,0:T(8,128)(2,1)S(1)}, bf16[16,4096]{1,0:T(8,128)(2,1)S(1)}, u32[]{:S(2)}, u32[]{:S(2)}) collective-permute-start(bf16[16,4096]{1,0:T(8,128)(2,1)S(1)} %get-tuple-element.16), channel_id=1, source_target_pairs={{0,192},{64,0},{128,64},{192,128},{1,193},{65,1},{129,65},{193,129... | collective-permute-start | bytes 393224 | tf_op jit(solution)/shard_map/ppermute | solution.py:22
  60.6 1.0 collective-permute-start.7
  61.6 1.0 fusion.9
  62.6 1.4 %collective-permute-start.5 = (bf16[16,4096]{1,0:T(8,128)(2,1)S(1)}, bf16[16,4096]{1,0:T(8,128)(2,1)S(1)}, u32[]{:S(2)}, u32[]{:S(2)}) collective-permute-start(bf16[16,4096]{1,0:T(8,128)(2,1)S(1)} %fusion.9), channel_id=1, source_target_pairs={{0,64},{64,128},{128,192},{192,0},{1,65},{65,129},{129,193},{193,1... | collective-permute-start | bytes 393224 | tf_op jit(solution)/shard_map/ppermute | solution.py:27
  64.0 3.7 %collective-permute-start.4 = (bf16[16,4096]{1,0:T(8,128)(2,1)S(1)}, bf16[16,4096]{1,0:T(8,128)(2,1)S(1)}, u32[]{:S(2)}, u32[]{:S(2)}) collective-permute-start(bf16[16,4096]{1,0:T(8,128)(2,1)S(1)} %fusion.9), channel_id=1, source_target_pairs={{0,128},{64,192},{128,0},{192,64},{1,129},{65,193},{129,1},{193,65... | collective-permute-start | bytes 393224 | tf_op jit(solution)/shard_map/ppermute | solution.py:27
  67.7 21.3 %collective-permute-done.6 = bf16[16,4096]{1,0:T(8,128)(2,1)S(1)} collective-permute-done((bf16[16,4096]{1,0:T(8,128)(2,1)S(1)}, bf16[16,4096]{1,0:T(8,128)(2,1)S(1)}, u32[]{:S(2)}, u32[]{:S(2)}) %collective-permute-start.6) | collective-permute-done | bytes 131104 | tf_op jit(solution)/shard_map/ppermute | solution.py:22
  89.1 1.0 fusion.6
  90.1 3.0 %collective-permute-start.11 = (bf16[16,4096]{1,0:T(8,128)(2,1)S(1)}, bf16[16,4096]{1,0:T(8,128)(2,1)S(1)}, u32[]{:S(2)}, u32[]{:S(2)}) collective-permute-start(bf16[16,4096]{1,0:T(8,128)(2,1)S(1)} %fusion.6), channel_id=1, source_target_pairs={{0,64},{64,128},{128,192},{192,0},{1,65},{65,129},{129,193},{193,1... | collective-permute-start | bytes 393224 | tf_op jit(solution)/shard_map/ppermute | solution.py:27
  93.1 3.7 %collective-permute-start.9 = (bf16[16,4096]{1,0:T(8,128)(2,1)S(1)}, bf16[16,4096]{1,0:T(8,128)(2,1)S(1)}, u32[]{:S(2)}, u32[]{:S(2)}) collective-permute-start(bf16[16,4096]{1,0:T(8,128)(2,1)S(1)} %fusion.6), channel_id=1, source_target_pairs={{0,192},{64,0},{128,64},{192,128},{1,193},{65,1},{129,65},{193,129... | collective-permute-start | bytes 393224 | tf_op jit(solution)/shard_map/ppermute | solution.py:27
  96.9 0.4 fusion.16
  97.3 0.3 broadcast_multiply_fusion
  97.6 5.5 %collective-permute-done.10 = bf16[16,4096]{1,0:T(8,128)(2,1)S(1)} collective-permute-done((bf16[16,4096]{1,0:T(8,128)(2,1)S(1)}, bf16[16,4096]{1,0:T(8,128)(2,1)S(1)}, u32[]{:S(2)}, u32[]{:S(2)}) %collective-permute-start.10) | collective-permute-done | bytes 131104 | tf_op jit(solution)/shard_map/ppermute | solution.py:27
  103.2 0.1 maximum_convert_fusion
  103.3 3.2 %fusion.2 = f32[2,2,64,4096]{3,2,1,0:T(8,128)} fusion(bf16[2,2,64,4096]{3,2,1,0:T(8,128)(2,1)S(1)} %copy-done.1, f32[2,2,64,4096]{3,2,1,0:T(8,128)S(1)} %bitcast.37, f32[64,4096]{1,0:T(8,128)S(1)} %get-tuple-element.21, f32[64,4096]{1,0:T(8,128)S(1)} %maximum_convert_fusion, f32[2,64,4096]{2,1,0:T(8,128)S(1)} %broadcast_multiply_fusion, ...), kind=kLoop, calls=%fused_computation.4 | loop fusion | flops 6291456 | bytes 15728640 | tf_op jit(solution)/shard_map/add | solution.py:129
  (27 shorter events, 0.2 us)
Async XLA Ops:
  0.0 12.7 %copy-start = (bf16[2,2,64,4096]{3,2,1,0:T(8,128)(2,1)S(1)}, bf16[2,2,64,4096]{3,2,1,0:T(8,128)(2,1)}, u32[]{:S(2)}) copy-start(bf16[2,2,64,4096]{3,2,1,0:T(8,128)(2,1)} %param.6) | copy-start | bytes 6291460
  0.0 12.7 %copy-start.5 = (f32[2]{0:T(128)S(1)}, f32[2]{0:T(128)}, u32[]{:S(2)}) copy-start(f32[2]{0:T(128)} %param.11) | copy-start | bytes 28
  3.4 34.5 %all-to-all-start = ((bf16[64,64,256]{2,1,0:T(8,128)(2,1)}), bf16[64,64,256]{2,1,0:T(8,128)(2,1)}, u32[]{:S(2)}, u32[]{:S(2)}) async-start(bf16[64,64,256]{2,1,0:T(8,128)(2,1)} %bitcast.36), calls=%async_computation | async-start | bytes 4194304 | tf_op jit(solution)/shard_map/all_to_all | solution.py:120
  13.4 35.1 %copy-start.4 = (f32[64,4096]{1,0:T(8,128)}, f32[64,4096]{1,0:T(8,128)S(1)}, u32[]{:S(2)}) copy-start(f32[64,4096]{1,0:T(8,128)S(1)} %fusion.3) | copy-start | bytes 3145732
  38.0 22.6 %collective-permute-start = (bf16[16,4096]{1,0:T(8,128)(2,1)S(1)}, bf16[16,4096]{1,0:T(8,128)(2,1)S(1)}, u32[]{:S(2)}, u32[]{:S(2)}) collective-permute-start(bf16[16,4096]{1,0:T(8,128)(2,1)S(1)} %get-tuple-element.18), channel_id=1, source_target_pairs={{0,64},{64,128},{128,192},{192,0},{1,65},{65,129},{129,193},{193,1... | collective-permute-start | bytes 393224 | tf_op jit(solution)/shard_map/ppermute | solution.py:22
  41.3 20.2 %collective-permute-start.2 = (bf16[16,4096]{1,0:T(8,128)(2,1)S(1)}, bf16[16,4096]{1,0:T(8,128)(2,1)S(1)}, u32[]{:S(2)}, u32[]{:S(2)}) collective-permute-start(bf16[16,4096]{1,0:T(8,128)(2,1)S(1)} %get-tuple-element.19), channel_id=1, source_target_pairs={{0,192},{64,0},{128,64},{192,128},{1,193},{65,1},{129,65},{193,129... | collective-permute-start | bytes 393224 | tf_op jit(solution)/shard_map/ppermute | solution.py:22
  43.6 18.0 %collective-permute-start.1 = (bf16[16,4096]{1,0:T(8,128)(2,1)S(1)}, bf16[16,4096]{1,0:T(8,128)(2,1)S(1)}, u32[]{:S(2)}, u32[]{:S(2)}) collective-permute-start(bf16[16,4096]{1,0:T(8,128)(2,1)S(1)} %get-tuple-element.20), channel_id=1, source_target_pairs={{0,128},{64,192},{128,0},{192,64},{1,129},{65,193},{129,1},{193,65... | collective-permute-start | bytes 393224 | tf_op jit(solution)/shard_map/ppermute | solution.py:22
  48.5 48.3 %copy-start.3 = (s32[64,4096]{1,0:T(8,128)S(1)}, s32[64,4096]{1,0:T(8,128)}, u32[]{:S(2)}) copy-start(s32[64,4096]{1,0:T(8,128)} %m_ref.1) | copy-start | bytes 3145732
  56.4 32.7 %collective-permute-start.6 = (bf16[16,4096]{1,0:T(8,128)(2,1)S(1)}, bf16[16,4096]{1,0:T(8,128)(2,1)S(1)}, u32[]{:S(2)}, u32[]{:S(2)}) collective-permute-start(bf16[16,4096]{1,0:T(8,128)(2,1)S(1)} %get-tuple-element.15), channel_id=1, source_target_pairs={{0,64},{64,128},{128,192},{192,0},{1,65},{65,129},{129,193},{193,1... | collective-permute-start | bytes 393224 | tf_op jit(solution)/shard_map/ppermute | solution.py:22
  56.7 32.4 %collective-permute-start.8 = (bf16[16,4096]{1,0:T(8,128)(2,1)S(1)}, bf16[16,4096]{1,0:T(8,128)(2,1)S(1)}, u32[]{:S(2)}, u32[]{:S(2)}) collective-permute-start(bf16[16,4096]{1,0:T(8,128)(2,1)S(1)} %get-tuple-element.16), channel_id=1, source_target_pairs={{0,192},{64,0},{128,64},{192,128},{1,193},{65,1},{129,65},{193,129... | collective-permute-start | bytes 393224 | tf_op jit(solution)/shard_map/ppermute | solution.py:22
  60.6 28.5 %collective-permute-start.7 = (bf16[16,4096]{1,0:T(8,128)(2,1)S(1)}, bf16[16,4096]{1,0:T(8,128)(2,1)S(1)}, u32[]{:S(2)}, u32[]{:S(2)}) collective-permute-start(bf16[16,4096]{1,0:T(8,128)(2,1)S(1)} %get-tuple-element.17), channel_id=1, source_target_pairs={{0,128},{64,192},{128,0},{192,64},{1,129},{65,193},{129,1},{193,65... | collective-permute-start | bytes 393224 | tf_op jit(solution)/shard_map/ppermute | solution.py:22
  62.6 30.5 %collective-permute-start.5 = (bf16[16,4096]{1,0:T(8,128)(2,1)S(1)}, bf16[16,4096]{1,0:T(8,128)(2,1)S(1)}, u32[]{:S(2)}, u32[]{:S(2)}) collective-permute-start(bf16[16,4096]{1,0:T(8,128)(2,1)S(1)} %fusion.9), channel_id=1, source_target_pairs={{0,64},{64,128},{128,192},{192,0},{1,65},{65,129},{129,193},{193,1... | collective-permute-start | bytes 393224 | tf_op jit(solution)/shard_map/ppermute | solution.py:27
  64.0 32.7 %collective-permute-start.4 = (bf16[16,4096]{1,0:T(8,128)(2,1)S(1)}, bf16[16,4096]{1,0:T(8,128)(2,1)S(1)}, u32[]{:S(2)}, u32[]{:S(2)}) collective-permute-start(bf16[16,4096]{1,0:T(8,128)(2,1)S(1)} %fusion.9), channel_id=1, source_target_pairs={{0,128},{64,192},{128,0},{192,64},{1,129},{65,193},{129,1},{193,65... | collective-permute-start | bytes 393224 | tf_op jit(solution)/shard_map/ppermute | solution.py:27
  89.0 7.7 %collective-permute-start.3 = (bf16[16,4096]{1,0:T(8,128)(2,1)S(1)}, bf16[16,4096]{1,0:T(8,128)(2,1)S(1)}, u32[]{:S(2)}, u32[]{:S(2)}) collective-permute-start(bf16[16,4096]{1,0:T(8,128)(2,1)S(1)} %fusion.9), channel_id=1, source_target_pairs={{0,192},{64,0},{128,64},{192,128},{1,193},{65,1},{129,65},{193,129... | collective-permute-start | bytes 393224 | tf_op jit(solution)/shard_map/ppermute | solution.py:27
  90.1 7.5 %collective-permute-start.11 = (bf16[16,4096]{1,0:T(8,128)(2,1)S(1)}, bf16[16,4096]{1,0:T(8,128)(2,1)S(1)}, u32[]{:S(2)}, u32[]{:S(2)}) collective-permute-start(bf16[16,4096]{1,0:T(8,128)(2,1)S(1)} %fusion.6), channel_id=1, source_target_pairs={{0,64},{64,128},{128,192},{192,0},{1,65},{65,129},{129,193},{193,1... | collective-permute-start | bytes 393224 | tf_op jit(solution)/shard_map/ppermute | solution.py:27
  93.1 10.0 %collective-permute-start.10 = (bf16[16,4096]{1,0:T(8,128)(2,1)S(1)}, bf16[16,4096]{1,0:T(8,128)(2,1)S(1)}, u32[]{:S(2)}, u32[]{:S(2)}) collective-permute-start(bf16[16,4096]{1,0:T(8,128)(2,1)S(1)} %fusion.6), channel_id=1, source_target_pairs={{0,128},{64,192},{128,0},{192,64},{1,129},{65,193},{129,1},{193,65... | collective-permute-start | bytes 393224 | tf_op jit(solution)/shard_map/ppermute | solution.py:27
  93.1 10.0 %collective-permute-start.9 = (bf16[16,4096]{1,0:T(8,128)(2,1)S(1)}, bf16[16,4096]{1,0:T(8,128)(2,1)S(1)}, u32[]{:S(2)}, u32[]{:S(2)}) collective-permute-start(bf16[16,4096]{1,0:T(8,128)(2,1)S(1)} %fusion.6), channel_id=1, source_target_pairs={{0,192},{64,0},{128,64},{192,128},{1,193},{65,1},{129,65},{193,129... | collective-permute-start | bytes 393224 | tf_op jit(solution)/shard_map/ppermute | solution.py:27
  96.8 6.4 %copy-start.1 = (bf16[2,2,64,4096]{3,2,1,0:T(8,128)(2,1)S(1)}, bf16[2,2,64,4096]{3,2,1,0:T(8,128)(2,1)}, u32[]{:S(2)}) copy-start(bf16[2,2,64,4096]{3,2,1,0:T(8,128)(2,1)} %param.6) | copy-start | bytes 6291460
  96.8 6.4 %copy-start.2 = (f32[4,64,4096]{2,1,0:T(8,128)S(1)}, f32[4,64,4096]{2,1,0:T(8,128)}, u32[]{:S(2)}) copy-start(f32[4,64,4096]{2,1,0:T(8,128)} %get-tuple-element.11) | copy-start | bytes 12582916

commit v10 on v9

--- a/solution.py
+++ b/solution.py
@@ -10,21 +10,27 @@
 INTERPRET = False
 
 
-def con_sum(part, link_type):
+def con_pairs(shift):
+    count = lax.axis_size("con")
+    return [(i, (i + shift) % count) for i in range(count)]
+
+
+def con_scatter(part, link_type):
     count = lax.axis_size("con")
     me = lax.axis_index("con")
     rows = part.shape[0]
     quarters = part.reshape((count, rows // count) + part.shape[1:])
     total = lax.dynamic_index_in_dim(quarters, me, 0, keepdims=False).astype(jnp.float32)
     for shift in range(1, count):
-        pairs = [(i, (i + shift) % count) for i in range(count)]
         piece = lax.dynamic_index_in_dim(quarters, (me + shift) % count, 0, keepdims=False)
-        total = total + lax.ppermute(piece.astype(link_type), "con", pairs).astype(jnp.float32)
-    mine = total.astype(link_type)
-    pieces = [mine]
-    for shift in range(1, count):
-        pairs = [(i, (i + shift) % count) for i in range(count)]
-        pieces.append(lax.ppermute(mine, "con", pairs))
+        total = total + lax.ppermute(piece.astype(link_type), "con", con_pairs(shift)).astype(jnp.float32)
+    return total.astype(link_type)
+
+
+def con_gather(mine, axis):
+    count = lax.axis_size("con")
+    me = lax.axis_index("con")
+    pieces = [mine] + [lax.ppermute(mine, "con", con_pairs(shift)) for shift in range(1, count)]
     slots = []
     for q in range(count):
         source = (me - q) % count
@@ -32,7 +38,7 @@
         for shift in range(1, count):
             slot = jnp.where(source == shift, pieces[shift], slot)
         slots.append(slot)
-    return jnp.concatenate(slots, axis=0).astype(jnp.float32)
+    return jnp.concatenate(slots, axis=axis).astype(jnp.float32)
 
 
 def x_solve_kernel(s_ref, w_ref, o_ref):
@@ -119,10 +125,11 @@
     across = x_solve(seed_adjoint.reshape(con_local * 2 * cols_local, full_side), inv_x)
     arrived = lax.all_to_all(across, "grid", split_axis=0, concat_axis=0, tiled=True)
     arrived, local_squares = lax.optimization_barrier((arrived, local_squares))
-    squares = con_sum(local_squares, jnp.bfloat16)
+    squares_mine = con_scatter(local_squares, jnp.bfloat16)
     solved, local_inner = y_solve(arrived, land_mask, inv_y, velocity.reshape(con_local * 2, rows_local, full_side))
     rhs_adjoint = solved.reshape(con_local, 2, rows_local, full_side)
-    inner = con_sum(local_inner, jnp.bfloat16)
+    inner_mine = con_scatter(local_inner, jnp.bfloat16)
+    squares, inner = con_gather(jnp.stack([squares_mine, inner_mine]), axis=1)
     speed = jnp.sqrt(0.25 + squares)
     first = -0.5 * sea_float * speed * rhs_adjoint
     second = -0.5 * sea_float * weight_full * vel_float * inner / speed

time: 107 us -> 113 us (1.056)
  the two profiles are of different devices: /device:TPU:48 before, /device:TPU:2 now
where the time goes in v10:
time: 113 us
  waiting for transfers between devices  60.7 us (54%)
  starting transfers between devices  31.6 us (28%)
  Pallas kernels  9.88 us (9%)
  other arithmetic  6.15 us (5%)
  local copies, waits for them, and re-layouts  4.43 us (4%)
    all_to_all x1, waiting for transfers between devices, local(): lax.all_to_all(across, 'grid', split_axis=0, concat_axis=0, tiled=True)  27 us
    ppermute x3, waiting for transfers between devices, con_gather(): lax.ppermute(mine, 'con', con_pairs(shift))  23.6 us
    ppermute x6, starting transfers between devices, con_scatter(): lax.ppermute(piece.astype(link_type), 'con', con_pairs(shift))  15.7 us
    ppermute x6, waiting for transfers between devices, con_scatter(): lax.ppermute(piece.astype(link_type), 'con', con_pairs(shift))  10.1 us
    all_to_all x1, starting transfers between devices, local(): lax.all_to_all(across, 'grid', split_axis=0, concat_axis=0, tiled=True)  9.7 us
    pallas_call x1, Pallas kernels, y_solve(): pl.pallas_call(y_solve_kernel, grid=(nblocks // GROUP,), in_specs=[pl.Blo...  6.64 us
    ppermute x3, starting transfers between devices, con_gather(): lax.ppermute(mine, 'con', con_pairs(shift))  6.15 us
    unnamed x10, local copies, waits for them, and re-layouts  3.24 us
  transfers between devices with their start and end apart: 10, of which 6 were waited for; matrix products, arithmetic and copies ran while one was open for 2% of the time, Pallas kernels for 6%

profile of v10, /device:TPU:2, one launch (start us, length us, event | category | flops | bytes accessed | tf_op | source)
XLA Modules:
  0.0 112.9 jit_solution(7042384030634721976)
XLA Ops:
  0.0 3.2 %shard_map.64 = bf16[4096,256]{1,0:T(8,128)(2,1)} custom-call(bf16[256,4096]{1,0:T(8,128)(2,1)} %bitcast.54, bf16[32,128,128]{2,1,0:T(8,128)(2,1)} %w_ref.2), custom_call_target="tpu_custom_call" | custom-call | tf_op jit(solution)/shard_map/pallas_call | solution.py:54
  3.2 9.7 %all-to-all-start = ((bf16[64,64,256]{2,1,0:T(8,128)(2,1)}), bf16[64,64,256]{2,1,0:T(8,128)(2,1)}, u32[]{:S(2)}, u32[]{:S(2)}) async-start(bf16[64,64,256]{2,1,0:T(8,128)(2,1)} %bitcast.50), calls=%async_computation | async-start | bytes 4194304 | tf_op jit(solution)/shard_map/all_to_all | solution.py:126
  13.0 0.7 fusion.3
  13.7 27.0 %all-to-all-done = bf16[64,64,256]{2,1,0:T(8,128)(2,1)} async-done(((bf16[64,64,256]{2,1,0:T(8,128)(2,1)}), bf16[64,64,256]{2,1,0:T(8,128)(2,1)}, u32[]{:S(2)}, u32[]{:S(2)}) %all-to-all-start) | async-done | bytes 2097184 | tf_op jit(solution)/shard_map/all_to_all | solution.py:126
  40.8 3.3 %collective-permute-start = (bf16[16,4096]{1,0:T(8,128)(2,1)S(1)}, bf16[16,4096]{1,0:T(8,128)(2,1)S(1)}, u32[]{:S(2)}, u32[]{:S(2)}) collective-permute-start(bf16[16,4096]{1,0:T(8,128)(2,1)S(1)} %get-tuple-element.20), channel_id=1, source_target_pairs={{0,64},{64,128},{128,192},{192,0},{1,65},{65,129},{129,193},{193,1... | collective-permute-start | bytes 393224 | tf_op jit(solution)/shard_map/ppermute | solution.py:26
  44.1 2.2 %collective-permute-start.2 = (bf16[16,4096]{1,0:T(8,128)(2,1)S(1)}, bf16[16,4096]{1,0:T(8,128)(2,1)S(1)}, u32[]{:S(2)}, u32[]{:S(2)}) collective-permute-start(bf16[16,4096]{1,0:T(8,128)(2,1)S(1)} %get-tuple-element.21), channel_id=1, source_target_pairs={{0,192},{64,0},{128,64},{192,128},{1,193},{65,1},{129,65},{193,129... | collective-permute-start | bytes 393224 | tf_op jit(solution)/shard_map/ppermute | solution.py:26
  46.3 4.9 %collective-permute-start.1 = (bf16[16,4096]{1,0:T(8,128)(2,1)S(1)}, bf16[16,4096]{1,0:T(8,128)(2,1)S(1)}, u32[]{:S(2)}, u32[]{:S(2)}) collective-permute-start(bf16[16,4096]{1,0:T(8,128)(2,1)S(1)} %get-tuple-element.22), channel_id=1, source_target_pairs={{0,128},{64,192},{128,0},{192,64},{1,129},{65,193},{129,1},{193,65... | collective-permute-start | bytes 393224 | tf_op jit(solution)/shard_map/ppermute | solution.py:26
  51.3 6.6 %shard_map.65 = (f32[4,64,4096]{2,1,0:T(8,128)}, f32[64,4096]{1,0:T(8,128)}) custom-call(bf16[4096,256]{1,0:T(8,128)(2,1)} %bitcast.2.r_ref, s32[64,4096]{1,0:T(8,128)} %m_ref.1, bf16[32,128,128]{2,1,0:T(8,128)(2,1)} %w_ref.3, bf16[4,64,4096]{2,1,0:T(8,128)(2,1)} %bitcast.49), custom_call_target="tpu_custom_call" | custom-call | tf_op jit(solution)/shard_map/pallas_call | solution.py:95
  57.9 1.1 %fusion.15 = (bf16[16,4096]{1,0:T(8,128)(2,1)S(1)}, bf16[16,4096]{1,0:T(8,128)(2,1)S(1)}, bf16[16,4096]{1,0:T(8,128)(2,1)S(1)}) fusion(f32[4,16,4096]{2,1,0:T(8,128)} %bitcast.55, s32[]{:T(128)S(6)} %select_n.132, s32[]{:T(128)S(6)} %select_n.136, s32[]{:T(128)S(6)} %select_n.134), kind=kLoop, calls=%fused_computation.35 | loop fusion | bytes 786444 | tf_op jit(solution)/shard_map/convert_element_type | solution.py:26
  59.4 3.9 %collective-permute-start.5 = (bf16[16,4096]{1,0:T(8,128)(2,1)S(1)}, bf16[16,4096]{1,0:T(8,128)(2,1)S(1)}, u32[]{:S(2)}, u32[]{:S(2)}) collective-permute-start(bf16[16,4096]{1,0:T(8,128)(2,1)S(1)} %get-tuple-element.24), channel_id=1, source_target_pairs={{0,192},{64,0},{128,64},{192,128},{1,193},{65,1},{129,65},{193,129... | collective-permute-start | bytes 393224 | tf_op jit(solution)/shard_map/ppermute | solution.py:26
  63.3 1.0 collective-permute-start.4
  64.3 7.2 %collective-permute-done.3 = bf16[16,4096]{1,0:T(8,128)(2,1)S(1)} collective-permute-done((bf16[16,4096]{1,0:T(8,128)(2,1)S(1)}, bf16[16,4096]{1,0:T(8,128)(2,1)S(1)}, u32[]{:S(2)}, u32[]{:S(2)}) %collective-permute-start.3) | collective-permute-done | bytes 131104 | tf_op jit(solution)/shard_map/ppermute | solution.py:26
  71.6 2.9 %collective-permute-done.4 = bf16[16,4096]{1,0:T(8,128)(2,1)S(1)} collective-permute-done((bf16[16,4096]{1,0:T(8,128)(2,1)S(1)}, bf16[16,4096]{1,0:T(8,128)(2,1)S(1)}, u32[]{:S(2)}, u32[]{:S(2)}) %collective-permute-start.4) | collective-permute-done | bytes 131104 | tf_op jit(solution)/shard_map/ppermute | solution.py:26
  74.4 1.0 fusion.19
  75.5 2.5 %collective-permute-start.8 = (bf16[2,16,4096]{2,1,0:T(8,128)(2,1)S(1)}, bf16[2,16,4096]{2,1,0:T(8,128)(2,1)S(1)}, u32[]{:S(2)}, u32[]{:S(2)}) collective-permute-start(bf16[2,16,4096]{2,1,0:T(8,128)(2,1)S(1)} %pad_maximum_fusion), channel_id=1, source_target_pairs={{0,64},{64,128},{128,192},{192,0},{1,65},{65,129},{129,193},{193,1... | collective-permute-start | bytes 786440 | tf_op jit(solution)/shard_map/ppermute | solution.py:33
  78.0 1.9 %collective-permute-start.7 = (bf16[2,16,4096]{2,1,0:T(8,128)(2,1)S(1)}, bf16[2,16,4096]{2,1,0:T(8,128)(2,1)S(1)}, u32[]{:S(2)}, u32[]{:S(2)}) collective-permute-start(bf16[2,16,4096]{2,1,0:T(8,128)(2,1)S(1)} %pad_maximum_fusion), channel_id=1, source_target_pairs={{0,128},{64,192},{128,0},{192,64},{1,129},{65,193},{129,1},{193,65... | collective-permute-start | bytes 786440 | tf_op jit(solution)/shard_map/ppermute | solution.py:33
  79.9 1.8 %collective-permute-start.6 = (bf16[2,16,4096]{2,1,0:T(8,128)(2,1)S(1)}, bf16[2,16,4096]{2,1,0:T(8,128)(2,1)S(1)}, u32[]{:S(2)}, u32[]{:S(2)}) collective-permute-start(bf16[2,16,4096]{2,1,0:T(8,128)(2,1)S(1)} %pad_maximum_fusion), channel_id=1, source_target_pairs={{0,192},{64,0},{128,64},{192,128},{1,193},{65,1},{129,65},{193,129... | collective-permute-start | bytes 786440 | tf_op jit(solution)/shard_map/ppermute | solution.py:33
  81.6 6.4 %collective-permute-done.8 = bf16[2,16,4096]{2,1,0:T(8,128)(2,1)S(1)} collective-permute-done((bf16[2,16,4096]{2,1,0:T(8,128)(2,1)S(1)}, bf16[2,16,4096]{2,1,0:T(8,128)(2,1)S(1)}, u32[]{:S(2)}, u32[]{:S(2)}) %collective-permute-start.8) | collective-permute-done | bytes 262176 | tf_op jit(solution)/shard_map/ppermute | solution.py:33
  88.0 12.4 %collective-permute-done.7 = bf16[2,16,4096]{2,1,0:T(8,128)(2,1)S(1)} collective-permute-done((bf16[2,16,4096]{2,1,0:T(8,128)(2,1)S(1)}, bf16[2,16,4096]{2,1,0:T(8,128)(2,1)S(1)}, u32[]{:S(2)}, u32[]{:S(2)}) %collective-permute-start.7) | collective-permute-done | bytes 262176 | tf_op jit(solution)/shard_map/ppermute | solution.py:33
  100.4 4.8 %collective-permute-done.6 = bf16[2,16,4096]{2,1,0:T(8,128)(2,1)S(1)} collective-permute-done((bf16[2,16,4096]{2,1,0:T(8,128)(2,1)S(1)}, bf16[2,16,4096]{2,1,0:T(8,128)(2,1)S(1)}, u32[]{:S(2)}, u32[]{:S(2)}) %collective-permute-start.6) | collective-permute-done | bytes 262176 | tf_op jit(solution)/shard_map/ppermute | solution.py:33
  105.9 0.9 copy-done.3
  107.5 1.5 %copy-done.2 = f32[4,64,4096]{2,1,0:T(8,128)S(1)} copy-done((f32[4,64,4096]{2,1,0:T(8,128)S(1)}, f32[4,64,4096]{2,1,0:T(8,128)}, u32[]{:S(2)}) %copy-start.2) | copy-done | bytes 4194328
  109.0 0.8 copy-done.1
  109.8 3.1 %fusion.2 = f32[2,2,64,4096]{3,2,1,0:T(8,128)} fusion(bf16[2,2,64,4096]{3,2,1,0:T(8,128)(2,1)S(1)} %copy-done.1, f32[2,2,64,4096]{3,2,1,0:T(8,128)S(1)} %bitcast.51, f32[64,4096]{1,0:T(8,128)S(1)} %get-tuple-element.14, f32[64,4096]{1,0:T(8,128)S(1)} %get-tuple-element.13, f32[2,64,4096]{2,1,0:T(8,128)S(1)} %broadcast_multiply_fusion, ...), kind=kLoop, calls=%fused_computation.4 | loop fusion | flops 6291456 | bytes 15728640 | tf_op jit(solution)/shard_map/add | solution.py:136
  (21 shorter events, 1.8 us)
Async XLA Ops:
  3.2 9.8 %copy-start = (bf16[2,2,64,4096]{3,2,1,0:T(8,128)(2,1)S(1)}, bf16[2,2,64,4096]{3,2,1,0:T(8,128)(2,1)}, u32[]{:S(2)}) copy-start(bf16[2,2,64,4096]{3,2,1,0:T(8,128)(2,1)} %param.6) | copy-start | bytes 6291460
  3.2 9.8 %copy-start.4 = (f32[2]{0:T(128)S(1)}, f32[2]{0:T(128)}, u32[]{:S(2)}) copy-start(f32[2]{0:T(128)} %param.11) | copy-start | bytes 28
  3.2 37.5 %all-to-all-start = ((bf16[64,64,256]{2,1,0:T(8,128)(2,1)}), bf16[64,64,256]{2,1,0:T(8,128)(2,1)}, u32[]{:S(2)}, u32[]{:S(2)}) async-start(bf16[64,64,256]{2,1,0:T(8,128)(2,1)} %bitcast.50), calls=%async_computation | async-start | bytes 4194304 | tf_op jit(solution)/shard_map/all_to_all | solution.py:126
  40.8 22.5 %collective-permute-start = (bf16[16,4096]{1,0:T(8,128)(2,1)S(1)}, bf16[16,4096]{1,0:T(8,128)(2,1)S(1)}, u32[]{:S(2)}, u32[]{:S(2)}) collective-permute-start(bf16[16,4096]{1,0:T(8,128)(2,1)S(1)} %get-tuple-element.20), channel_id=1, source_target_pairs={{0,64},{64,128},{128,192},{192,0},{1,65},{65,129},{129,193},{193,1... | collective-permute-start | bytes 393224 | tf_op jit(solution)/shard_map/ppermute | solution.py:26
  44.1 20.2 %collective-permute-start.2 = (bf16[16,4096]{1,0:T(8,128)(2,1)S(1)}, bf16[16,4096]{1,0:T(8,128)(2,1)S(1)}, u32[]{:S(2)}, u32[]{:S(2)}) collective-permute-start(bf16[16,4096]{1,0:T(8,128)(2,1)S(1)} %get-tuple-element.21), channel_id=1, source_target_pairs={{0,192},{64,0},{128,64},{192,128},{1,193},{65,1},{129,65},{193,129... | collective-permute-start | bytes 393224 | tf_op jit(solution)/shard_map/ppermute | solution.py:26
  46.3 17.9 %collective-permute-start.1 = (bf16[16,4096]{1,0:T(8,128)(2,1)S(1)}, bf16[16,4096]{1,0:T(8,128)(2,1)S(1)}, u32[]{:S(2)}, u32[]{:S(2)}) collective-permute-start(bf16[16,4096]{1,0:T(8,128)(2,1)S(1)} %get-tuple-element.22), channel_id=1, source_target_pairs={{0,128},{64,192},{128,0},{192,64},{1,129},{65,193},{129,1},{193,65... | collective-permute-start | bytes 393224 | tf_op jit(solution)/shard_map/ppermute | solution.py:26
  59.1 12.5 %collective-permute-start.3 = (bf16[16,4096]{1,0:T(8,128)(2,1)S(1)}, bf16[16,4096]{1,0:T(8,128)(2,1)S(1)}, u32[]{:S(2)}, u32[]{:S(2)}) collective-permute-start(bf16[16,4096]{1,0:T(8,128)(2,1)S(1)} %get-tuple-element.23), channel_id=1, source_target_pairs={{0,64},{64,128},{128,192},{192,0},{1,65},{65,129},{129,193},{193,1... | collective-permute-start | bytes 393224 | tf_op jit(solution)/shard_map/ppermute | solution.py:26
  59.4 12.2 %collective-permute-start.5 = (bf16[16,4096]{1,0:T(8,128)(2,1)S(1)}, bf16[16,4096]{1,0:T(8,128)(2,1)S(1)}, u32[]{:S(2)}, u32[]{:S(2)}) collective-permute-start(bf16[16,4096]{1,0:T(8,128)(2,1)S(1)} %get-tuple-element.24), channel_id=1, source_target_pairs={{0,192},{64,0},{128,64},{192,128},{1,193},{65,1},{129,65},{193,129... | collective-permute-start | bytes 393224 | tf_op jit(solution)/shard_map/ppermute | solution.py:26
  63.3 11.2 %collective-permute-start.4 = (bf16[16,4096]{1,0:T(8,128)(2,1)S(1)}, bf16[16,4096]{1,0:T(8,128)(2,1)S(1)}, u32[]{:S(2)}, u32[]{:S(2)}) collective-permute-start(bf16[16,4096]{1,0:T(8,128)(2,1)S(1)} %get-tuple-element.25), channel_id=1, source_target_pairs={{0,128},{64,192},{128,0},{192,64},{1,129},{65,193},{129,1},{193,65... | collective-permute-start | bytes 393224 | tf_op jit(solution)/shard_map/ppermute | solution.py:26
  75.5 12.5 %collective-permute-start.8 = (bf16[2,16,4096]{2,1,0:T(8,128)(2,1)S(1)}, bf16[2,16,4096]{2,1,0:T(8,128)(2,1)S(1)}, u32[]{:S(2)}, u32[]{:S(2)}) collective-permute-start(bf16[2,16,4096]{2,1,0:T(8,128)(2,1)S(1)} %pad_maximum_fusion), channel_id=1, source_target_pairs={{0,64},{64,128},{128,192},{192,0},{1,65},{65,129},{129,193},{193,1... | collective-permute-start | bytes 786440 | tf_op jit(solution)/shard_map/ppermute | solution.py:33
  78.0 22.5 %collective-permute-start.7 = (bf16[2,16,4096]{2,1,0:T(8,128)(2,1)S(1)}, bf16[2,16,4096]{2,1,0:T(8,128)(2,1)S(1)}, u32[]{:S(2)}, u32[]{:S(2)}) collective-permute-start(bf16[2,16,4096]{2,1,0:T(8,128)(2,1)S(1)} %pad_maximum_fusion), channel_id=1, source_target_pairs={{0,128},{64,192},{128,0},{192,64},{1,129},{65,193},{129,1},{193,65... | collective-permute-start | bytes 786440 | tf_op jit(solution)/shard_map/ppermute | solution.py:33
  79.9 25.4 %collective-permute-start.6 = (bf16[2,16,4096]{2,1,0:T(8,128)(2,1)S(1)}, bf16[2,16,4096]{2,1,0:T(8,128)(2,1)S(1)}, u32[]{:S(2)}, u32[]{:S(2)}) collective-permute-start(bf16[2,16,4096]{2,1,0:T(8,128)(2,1)S(1)} %pad_maximum_fusion), channel_id=1, source_target_pairs={{0,192},{64,0},{128,64},{192,128},{1,193},{65,1},{129,65},{193,129... | collective-permute-start | bytes 786440 | tf_op jit(solution)/shard_map/ppermute | solution.py:33
  105.6 1.2 %copy-start.3 = (s32[64,4096]{1,0:T(8,128)S(1)}, s32[64,4096]{1,0:T(8,128)}, u32[]{:S(2)}) copy-start(s32[64,4096]{1,0:T(8,128)} %m_ref.1) | copy-start | bytes 3145732
  106.8 2.2 %copy-start.2 = (f32[4,64,4096]{2,1,0:T(8,128)S(1)}, f32[4,64,4096]{2,1,0:T(8,128)}, u32[]{:S(2)}) copy-start(f32[4,64,4096]{2,1,0:T(8,128)} %get-tuple-element.12) | copy-start | bytes 12582916
  107.2 2.6 %copy-start.1 = (bf16[2,2,64,4096]{3,2,1,0:T(8,128)(2,1)S(1)}, bf16[2,2,64,4096]{3,2,1,0:T(8,128)(2,1)}, u32[]{:S(2)}) copy-start(bf16[2,2,64,4096]{3,2,1,0:T(8,128)(2,1)} %param.6) | copy-start | bytes 6291460

commit v11 on v9

--- a/solution.py
+++ b/solution.py
@@ -118,8 +118,7 @@
     sea_float = (land_mask == 1).astype(jnp.float32)
     across = x_solve(seed_adjoint.reshape(con_local * 2 * cols_local, full_side), inv_x)
     arrived = lax.all_to_all(across, "grid", split_axis=0, concat_axis=0, tiled=True)
-    arrived, local_squares = lax.optimization_barrier((arrived, local_squares))
-    squares = con_sum(local_squares, jnp.bfloat16)
+    squares = lax.psum(local_squares.astype(jnp.bfloat16), "con").astype(jnp.float32)
     solved, local_inner = y_solve(arrived, land_mask, inv_y, velocity.reshape(con_local * 2, rows_local, full_side))
     rhs_adjoint = solved.reshape(con_local, 2, rows_local, full_side)
     inner = con_sum(local_inner, jnp.bfloat16)

time: 107 us -> 121 us (1.13)
  the two profiles are of different devices: /device:TPU:48 before, /device:TPU:1 now
where the time goes in v11:
time: 121 us; the launch traced here: 120 us
  waiting for transfers between devices  59.7 us (49%)
  starting transfers between devices  28.2 us (23%)
  between operations  13.6 us (11%)
  Pallas kernels  10.1 us (8%)
  other arithmetic  7.66 us (6%)
    all_to_all x1, waiting for transfers between devices, local(): lax.all_to_all(across, 'grid', split_axis=0, concat_axis=0, tiled=True)  32.3 us
    psum x1, waiting for transfers between devices, local(): lax.psum(local_squares.astype(jnp.bfloat16), 'con').astype(jnp.float32)  17.2 us
    ppermute x3, starting transfers between devices, con_sum(): lax.ppermute(piece.astype(link_type), 'con', pairs).astype(jnp.float32)  11.4 us
    all_to_all x1, starting transfers between devices, local(): lax.all_to_all(across, 'grid', split_axis=0, concat_axis=0, tiled=True)  10.5 us
    ppermute x3, waiting for transfers between devices, con_sum(): pieces.append(lax.ppermute(mine, 'con', pairs))  10.2 us
    pallas_call x1, Pallas kernels, y_solve(): pl.pallas_call(y_solve_kernel, grid=(nblocks // GROUP,), in_specs=[pl.Blo...  6.67 us
    ppermute x3, starting transfers between devices, con_sum(): pieces.append(lax.ppermute(mine, 'con', pairs))  6.23 us
    pallas_call x1, Pallas kernels, x_solve(): pl.pallas_call(x_solve_kernel, grid=(nblocks // GROUP,), in_specs=[pl.Blo...  3.39 us
  transfers between devices with their start and end apart: 8, of which 5 were waited for; matrix products, arithmetic and copies ran while one was open for 4% of the time, Pallas kernels for 6%

profile of v11, /device:TPU:1, one launch (start us, length us, event | category | flops | bytes accessed | tf_op | source)
XLA Modules:
  0.0 120.5 jit_solution(11043714290774784865)
XLA Ops:
  6.5 3.4 %shard_map.64 = bf16[4096,256]{1,0:T(8,128)(2,1)} custom-call(bf16[256,4096]{1,0:T(8,128)(2,1)} %bitcast.23, bf16[32,128,128]{2,1,0:T(8,128)(2,1)} %w_ref.2), custom_call_target="tpu_custom_call" | custom-call | tf_op jit(solution)/shard_map/pallas_call | solution.py:48
  9.9 10.5 %all-to-all-start = ((bf16[64,64,256]{2,1,0:T(8,128)(2,1)}), bf16[64,64,256]{2,1,0:T(8,128)(2,1)}, u32[]{:S(2)}, u32[]{:S(2)}) async-start(bf16[64,64,256]{2,1,0:T(8,128)(2,1)} %bitcast.21), calls=%async_computation | async-start | bytes 4194304 | tf_op jit(solution)/shard_map/all_to_all | solution.py:120
  20.5 0.0 all-reduce.2.cloned.1.call-start
  20.6 1.5 %fusion.3 = bf16[64,4096]{1,0:T(8,128)(2,1)} fusion(bf16[2,2,64,4096]{3,2,1,0:T(8,128)(2,1)S(1)} %copy-done, f32[2]{0:T(128)S(1)} %copy-done.4), kind=kLoop, calls=%fused_computation.5 | loop fusion | flops 3932160 | bytes 2621448 | tf_op jit(solution)/shard_map/reduce_sum | solution.py:117
  22.1 0.0 all-reduce.2.cloned.1.call-update
  22.2 32.3 %all-to-all-done = bf16[64,64,256]{2,1,0:T(8,128)(2,1)} async-done(((bf16[64,64,256]{2,1,0:T(8,128)(2,1)}), bf16[64,64,256]{2,1,0:T(8,128)(2,1)}, u32[]{:S(2)}, u32[]{:S(2)}) %all-to-all-start) | async-done | bytes 2097184 | tf_op jit(solution)/shard_map/all_to_all | solution.py:120
  54.6 6.7 %shard_map.65 = (f32[4,64,4096]{2,1,0:T(8,128)}, f32[64,4096]{1,0:T(8,128)}) custom-call(bf16[4096,256]{1,0:T(8,128)(2,1)} %bitcast.2.r_ref, s32[64,4096]{1,0:T(8,128)} %m_ref.1, bf16[32,128,128]{2,1,0:T(8,128)(2,1)} %w_ref.3, bf16[4,64,4096]{2,1,0:T(8,128)(2,1)} %bitcast.20), custom_call_target="tpu_custom_call" | custom-call | tf_op jit(solution)/shard_map/pallas_call | solution.py:89
  61.2 1.1 fusion.8
  62.4 4.8 %collective-permute-start = (bf16[16,4096]{1,0:T(8,128)(2,1)S(1)}, bf16[16,4096]{1,0:T(8,128)(2,1)S(1)}, u32[]{:S(2)}, u32[]{:S(2)}) collective-permute-start(bf16[16,4096]{1,0:T(8,128)(2,1)S(1)} %get-tuple-element.11), channel_id=1, source_target_pairs={{0,64},{64,128},{128,192},{192,0},{1,65},{65,129},{129,193},{193,1... | collective-permute-start | bytes 393224 | tf_op jit(solution)/shard_map/ppermute | solution.py:22
  67.2 2.2 %collective-permute-start.2 = (bf16[16,4096]{1,0:T(8,128)(2,1)S(1)}, bf16[16,4096]{1,0:T(8,128)(2,1)S(1)}, u32[]{:S(2)}, u32[]{:S(2)}) collective-permute-start(bf16[16,4096]{1,0:T(8,128)(2,1)S(1)} %get-tuple-element.12), channel_id=1, source_target_pairs={{0,192},{64,0},{128,64},{192,128},{1,193},{65,1},{129,65},{193,129... | collective-permute-start | bytes 393224 | tf_op jit(solution)/shard_map/ppermute | solution.py:22
  69.4 4.4 %collective-permute-start.1 = (bf16[16,4096]{1,0:T(8,128)(2,1)S(1)}, bf16[16,4096]{1,0:T(8,128)(2,1)S(1)}, u32[]{:S(2)}, u32[]{:S(2)}) collective-permute-start(bf16[16,4096]{1,0:T(8,128)(2,1)S(1)} %get-tuple-element.13), channel_id=1, source_target_pairs={{0,128},{64,192},{128,0},{192,64},{1,129},{65,193},{129,1},{193,65... | collective-permute-start | bytes 393224 | tf_op jit(solution)/shard_map/ppermute | solution.py:22
  73.8 17.2 %all-reduce.2.cloned.1.call-done = bf16[64,4096]{1,0:T(8,128)(2,1)} async-done(((bf16[64,4096]{1,0:T(8,128)(2,1)}), bf16[64,4096]{1,0:T(8,128)(2,1)}) %all-reduce.2.cloned.1.call-update) | async-done | bytes 524304 | tf_op jit(solution)/shard_map/psum | solution.py:121
  91.0 1.5 %fusion.7 = (f32[64,4096]{1,0:T(8,128)S(1)}, f32[64,4096]{1,0:T(8,128)S(1)}, f32[64,4096]{1,0:T(8,128)S(1)}) fusion(bf16[64,4096]{1,0:T(8,128)(2,1)} %all-reduce.2.cloned.1.call-done, s32[64,4096]{1,0:T(8,128)S(1)} %copy-done.3), kind=kLoop, calls=%fused_computation.17 | loop fusion | flops 1310720 | bytes 4718592 | tf_op jit(solution)/shard_map/mul | solution.py:126
  92.5 1.2 fusion.6
  93.7 2.5 %collective-permute-start.5 = (bf16[16,4096]{1,0:T(8,128)(2,1)S(1)}, bf16[16,4096]{1,0:T(8,128)(2,1)S(1)}, u32[]{:S(2)}, u32[]{:S(2)}) collective-permute-start(bf16[16,4096]{1,0:T(8,128)(2,1)S(1)} %fusion.6), channel_id=1, source_target_pairs={{0,64},{64,128},{128,192},{192,0},{1,65},{65,129},{129,193},{193,1... | collective-permute-start | bytes 393224 | tf_op jit(solution)/shard_map/ppermute | solution.py:27
  96.2 0.5 collective-permute-start.4
  96.7 3.2 %collective-permute-start.3 = (bf16[16,4096]{1,0:T(8,128)(2,1)S(1)}, bf16[16,4096]{1,0:T(8,128)(2,1)S(1)}, u32[]{:S(2)}, u32[]{:S(2)}) collective-permute-start(bf16[16,4096]{1,0:T(8,128)(2,1)S(1)} %fusion.6), channel_id=1, source_target_pairs={{0,192},{64,0},{128,64},{192,128},{1,193},{65,1},{129,65},{193,129... | collective-permute-start | bytes 393224 | tf_op jit(solution)/shard_map/ppermute | solution.py:27
  99.9 0.3 broadcast_multiply_fusion
  100.2 2.3 %collective-permute-done.5 = bf16[16,4096]{1,0:T(8,128)(2,1)S(1)} collective-permute-done((bf16[16,4096]{1,0:T(8,128)(2,1)S(1)}, bf16[16,4096]{1,0:T(8,128)(2,1)S(1)}, u32[]{:S(2)}, u32[]{:S(2)}) %collective-permute-start.5) | collective-permute-done | bytes 131104 | tf_op jit(solution)/shard_map/ppermute | solution.py:27
  102.5 3.1 %collective-permute-done.4 = bf16[16,4096]{1,0:T(8,128)(2,1)S(1)} collective-permute-done((bf16[16,4096]{1,0:T(8,128)(2,1)S(1)}, bf16[16,4096]{1,0:T(8,128)(2,1)S(1)}, u32[]{:S(2)}, u32[]{:S(2)}) %collective-permute-start.4) | collective-permute-done | bytes 131104 | tf_op jit(solution)/shard_map/ppermute | solution.py:27
  105.6 4.8 %collective-permute-done.3 = bf16[16,4096]{1,0:T(8,128)(2,1)S(1)} collective-permute-done((bf16[16,4096]{1,0:T(8,128)(2,1)S(1)}, bf16[16,4096]{1,0:T(8,128)(2,1)S(1)}, u32[]{:S(2)}, u32[]{:S(2)}) %collective-permute-start.3) | collective-permute-done | bytes 131104 | tf_op jit(solution)/shard_map/ppermute | solution.py:27
  110.4 0.1 select_select_fusion.3
  110.4 0.1 maximum_convert_fusion
  110.5 3.1 %fusion.2 = f32[2,2,64,4096]{3,2,1,0:T(8,128)} fusion(bf16[2,2,64,4096]{3,2,1,0:T(8,128)(2,1)S(1)} %copy-done.1, f32[2,2,64,4096]{3,2,1,0:T(8,128)S(1)} %bitcast.22, f32[64,4096]{1,0:T(8,128)S(1)} %get-tuple-element.14, f32[64,4096]{1,0:T(8,128)S(1)} %maximum_convert_fusion, f32[2,64,4096]{2,1,0:T(8,128)S(1)} %broadcast_multiply_fusion, ...), kind=kLoop, calls=%fused_computation.4 | loop fusion | flops 6291456 | bytes 15728640 | tf_op jit(solution)/shard_map/add | solution.py:128
  (13 shorter events, 0.0 us)
Async XLA Ops:
  6.5 14.0 %copy-start = (bf16[2,2,64,4096]{3,2,1,0:T(8,128)(2,1)S(1)}, bf16[2,2,64,4096]{3,2,1,0:T(8,128)(2,1)}, u32[]{:S(2)}) copy-start(bf16[2,2,64,4096]{3,2,1,0:T(8,128)(2,1)} %param.6) | copy-start | bytes 6291460
  6.5 14.0 %copy-start.4 = (f32[2]{0:T(128)S(1)}, f32[2]{0:T(128)}, u32[]{:S(2)}) copy-start(f32[2]{0:T(128)} %param.11) | copy-start | bytes 28
  9.9 44.6 %all-to-all-start = ((bf16[64,64,256]{2,1,0:T(8,128)(2,1)}), bf16[64,64,256]{2,1,0:T(8,128)(2,1)}, u32[]{:S(2)}, u32[]{:S(2)}) async-start(bf16[64,64,256]{2,1,0:T(8,128)(2,1)} %bitcast.21), calls=%async_computation | async-start | bytes 4194304 | tf_op jit(solution)/shard_map/all_to_all | solution.py:120
  20.5 70.5 %all-reduce.2.cloned.1.call-start = ((), (), s32[]{:S(2)}) async-start(), calls=%async_computation.1 | async-start | bytes 1048576 | tf_op jit(solution)/shard_map/psum | solution.py:121
  22.1 68.9 %copy-start.3 = (s32[64,4096]{1,0:T(8,128)S(1)}, s32[64,4096]{1,0:T(8,128)}, u32[]{:S(2)}) copy-start(s32[64,4096]{1,0:T(8,128)} %m_ref.1) | copy-start | bytes 3145732
  62.4 30.1 %collective-permute-start = (bf16[16,4096]{1,0:T(8,128)(2,1)S(1)}, bf16[16,4096]{1,0:T(8,128)(2,1)S(1)}, u32[]{:S(2)}, u32[]{:S(2)}) collective-permute-start(bf16[16,4096]{1,0:T(8,128)(2,1)S(1)} %get-tuple-element.11), channel_id=1, source_target_pairs={{0,64},{64,128},{128,192},{192,0},{1,65},{65,129},{129,193},{193,1... | collective-permute-start | bytes 393224 | tf_op jit(solution)/shard_map/ppermute | solution.py:22
  67.2 25.3 %collective-permute-start.2 = (bf16[16,4096]{1,0:T(8,128)(2,1)S(1)}, bf16[16,4096]{1,0:T(8,128)(2,1)S(1)}, u32[]{:S(2)}, u32[]{:S(2)}) collective-permute-start(bf16[16,4096]{1,0:T(8,128)(2,1)S(1)} %get-tuple-element.12), channel_id=1, source_target_pairs={{0,192},{64,0},{128,64},{192,128},{1,193},{65,1},{129,65},{193,129... | collective-permute-start | bytes 393224 | tf_op jit(solution)/shard_map/ppermute | solution.py:22
  69.4 23.1 %collective-permute-start.1 = (bf16[16,4096]{1,0:T(8,128)(2,1)S(1)}, bf16[16,4096]{1,0:T(8,128)(2,1)S(1)}, u32[]{:S(2)}, u32[]{:S(2)}) collective-permute-start(bf16[16,4096]{1,0:T(8,128)(2,1)S(1)} %get-tuple-element.13), channel_id=1, source_target_pairs={{0,128},{64,192},{128,0},{192,64},{1,129},{65,193},{129,1},{193,65... | collective-permute-start | bytes 393224 | tf_op jit(solution)/shard_map/ppermute | solution.py:22
  92.5 18.1 %copy-start.1 = (bf16[2,2,64,4096]{3,2,1,0:T(8,128)(2,1)S(1)}, bf16[2,2,64,4096]{3,2,1,0:T(8,128)(2,1)}, u32[]{:S(2)}) copy-start(bf16[2,2,64,4096]{3,2,1,0:T(8,128)(2,1)} %param.6) | copy-start | bytes 6291460
  92.5 18.1 %copy-start.2 = (f32[4,64,4096]{2,1,0:T(8,128)S(1)}, f32[4,64,4096]{2,1,0:T(8,128)}, u32[]{:S(2)}) copy-start(f32[4,64,4096]{2,1,0:T(8,128)} %get-tuple-element.7) | copy-start | bytes 12582916
  93.7 8.8 %collective-permute-start.5 = (bf16[16,4096]{1,0:T(8,128)(2,1)S(1)}, bf16[16,4096]{1,0:T(8,128)(2,1)S(1)}, u32[]{:S(2)}, u32[]{:S(2)}) collective-permute-start(bf16[16,4096]{1,0:T(8,128)(2,1)S(1)} %fusion.6), channel_id=1, source_target_pairs={{0,64},{64,128},{128,192},{192,0},{1,65},{65,129},{129,193},{193,1... | collective-permute-start | bytes 393224 | tf_op jit(solution)/shard_map/ppermute | solution.py:27
  96.2 9.4 %collective-permute-start.4 = (bf16[16,4096]{1,0:T(8,128)(2,1)S(1)}, bf16[16,4096]{1,0:T(8,128)(2,1)S(1)}, u32[]{:S(2)}, u32[]{:S(2)}) collective-permute-start(bf16[16,4096]{1,0:T(8,128)(2,1)S(1)} %fusion.6), channel_id=1, source_target_pairs={{0,128},{64,192},{128,0},{192,64},{1,129},{65,193},{129,1},{193,65... | collective-permute-start | bytes 393224 | tf_op jit(solution)/shard_map/ppermute | solution.py:27
  96.7 13.6 %collective-permute-start.3 = (bf16[16,4096]{1,0:T(8,128)(2,1)S(1)}, bf16[16,4096]{1,0:T(8,128)(2,1)S(1)}, u32[]{:S(2)}, u32[]{:S(2)}) collective-permute-start(bf16[16,4096]{1,0:T(8,128)(2,1)S(1)} %fusion.6), channel_id=1, source_target_pairs={{0,192},{64,0},{128,64},{192,128},{1,193},{65,1},{129,65},{193,129... | collective-permute-start | bytes 393224 | tf_op jit(solution)/shard_map/ppermute | solution.py:27
Sparse Core Ops, SparseCore 0:
  23.9 67.0 all-reduce.1

commit v12 on v11

--- a/solution.py
+++ b/solution.py
@@ -118,9 +118,10 @@
     sea_float = (land_mask == 1).astype(jnp.float32)
     across = x_solve(seed_adjoint.reshape(con_local * 2 * cols_local, full_side), inv_x)
     arrived = lax.all_to_all(across, "grid", split_axis=0, concat_axis=0, tiled=True)
-    squares = lax.psum(local_squares.astype(jnp.bfloat16), "con").astype(jnp.float32)
     solved, local_inner = y_solve(arrived, land_mask, inv_y, velocity.reshape(con_local * 2, rows_local, full_side))
     rhs_adjoint = solved.reshape(con_local, 2, rows_local, full_side)
+    local_inner, local_squares = lax.optimization_barrier((local_inner, local_squares))
+    squares = con_sum(local_squares, jnp.bfloat16)
     inner = con_sum(local_inner, jnp.bfloat16)
     speed = jnp.sqrt(0.25 + squares)
     first = -0.5 * sea_float * speed * rhs_adjoint

time: 121 us -> 116 us (0.959)
  the two profiles are of different devices: /device:TPU:1 before, /device:TPU:48 now
where the time goes in v12:
time: 116 us
  starting transfers between devices  69.4 us (60%)
  waiting for transfers between devices  27.8 us (24%)
  Pallas kernels  10.1 us (9%)
  other arithmetic  6.78 us (6%)
  local copies, waits for them, and re-layouts  1.22 us (1%)
    ppermute x6, starting transfers between devices, con_sum(): lax.ppermute(piece.astype(link_type), 'con', pairs).astype(jnp.float32)  46 us
    all_to_all x1, waiting for transfers between devices, local(): lax.all_to_all(across, 'grid', split_axis=0, concat_axis=0, tiled=True)  23.6 us
    ppermute x6, starting transfers between devices, con_sum(): pieces.append(lax.ppermute(mine, 'con', pairs))  14.2 us
    all_to_all x1, starting transfers between devices, local(): lax.all_to_all(across, 'grid', split_axis=0, concat_axis=0, tiled=True)  9.12 us
    pallas_call x1, Pallas kernels, y_solve(): pl.pallas_call(y_solve_kernel, grid=(nblocks // GROUP,), in_specs=[pl.Blo...  6.72 us
    ppermute x6, waiting for transfers between devices, con_sum(): pieces.append(lax.ppermute(mine, 'con', pairs))  4.03 us
    pallas_call x1, Pallas kernels, x_solve(): pl.pallas_call(x_solve_kernel, grid=(nblocks // GROUP,), in_specs=[pl.Blo...  3.4 us
    add x1, other arithmetic, local(): return first + second  3.12 us
  transfers between devices with their start and end apart: 13, of which 4 were waited for; matrix products, arithmetic and copies ran while one was open for 4% of the time, Pallas kernels for 0%

profile of v12, /device:TPU:48, one launch (start us, length us, event | category | flops | bytes accessed | tf_op | source)
XLA Modules:
  0.0 115.6 jit_solution(3806066184496527914)
XLA Ops:
  0.0 3.4 %shard_map.64 = bf16[4096,256]{1,0:T(8,128)(2,1)} custom-call(bf16[256,4096]{1,0:T(8,128)(2,1)} %bitcast.40, bf16[32,128,128]{2,1,0:T(8,128)(2,1)} %w_ref.2), custom_call_target="tpu_custom_call" | custom-call | tf_op jit(solution)/shard_map/pallas_call | solution.py:48
  3.4 9.1 %all-to-all-start = ((bf16[64,64,256]{2,1,0:T(8,128)(2,1)}), bf16[64,64,256]{2,1,0:T(8,128)(2,1)}, u32[]{:S(2)}, u32[]{:S(2)}) async-start(bf16[64,64,256]{2,1,0:T(8,128)(2,1)} %bitcast.36), calls=%async_computation | async-start | bytes 4194304 | tf_op jit(solution)/shard_map/all_to_all | solution.py:120
  12.7 1.6 %fusion.3 = f32[64,4096]{1,0:T(8,128)} fusion(bf16[2,2,64,4096]{3,2,1,0:T(8,128)(2,1)S(1)} %copy-done, f32[2]{0:T(128)S(1)} %copy-done.5), kind=kLoop, calls=%fused_computation.5 | loop fusion | flops 3932160 | bytes 3145736 | tf_op jit(solution)/shard_map/reduce_sum | solution.py:117
  14.3 23.6 %all-to-all-done = bf16[64,64,256]{2,1,0:T(8,128)(2,1)} async-done(((bf16[64,64,256]{2,1,0:T(8,128)(2,1)}), bf16[64,64,256]{2,1,0:T(8,128)(2,1)}, u32[]{:S(2)}, u32[]{:S(2)}) %all-to-all-start) | async-done | bytes 2097184 | tf_op jit(solution)/shard_map/all_to_all | solution.py:120
  37.9 6.7 %shard_map.65 = (f32[4,64,4096]{2,1,0:T(8,128)}, f32[64,4096]{1,0:T(8,128)}) custom-call(bf16[4096,256]{1,0:T(8,128)(2,1)} %bitcast.2.r_ref, s32[64,4096]{1,0:T(8,128)} %m_ref.1, bf16[32,128,128]{2,1,0:T(8,128)(2,1)} %w_ref.3, bf16[4,64,4096]{2,1,0:T(8,128)(2,1)} %bitcast.35), custom_call_target="tpu_custom_call" | custom-call | tf_op jit(solution)/shard_map/pallas_call | solution.py:89
  44.7 3.3 %collective-permute-start = (bf16[16,4096]{1,0:T(8,128)(2,1)S(1)}, bf16[16,4096]{1,0:T(8,128)(2,1)S(1)}, u32[]{:S(2)}, u32[]{:S(2)}) collective-permute-start(bf16[16,4096]{1,0:T(8,128)(2,1)S(1)} %get-tuple-element.18), channel_id=1, source_target_pairs={{0,64},{64,128},{128,192},{192,0},{1,65},{65,129},{129,193},{193,1... | collective-permute-start | bytes 393224 | tf_op jit(solution)/shard_map/ppermute | solution.py:22
  48.1 2.2 %collective-permute-start.2 = (bf16[16,4096]{1,0:T(8,128)(2,1)S(1)}, bf16[16,4096]{1,0:T(8,128)(2,1)S(1)}, u32[]{:S(2)}, u32[]{:S(2)}) collective-permute-start(bf16[16,4096]{1,0:T(8,128)(2,1)S(1)} %get-tuple-element.19), channel_id=1, source_target_pairs={{0,192},{64,0},{128,64},{192,128},{1,193},{65,1},{129,65},{193,129... | collective-permute-start | bytes 393224 | tf_op jit(solution)/shard_map/ppermute | solution.py:22
  50.3 4.9 %collective-permute-start.1 = (bf16[16,4096]{1,0:T(8,128)(2,1)S(1)}, bf16[16,4096]{1,0:T(8,128)(2,1)S(1)}, u32[]{:S(2)}, u32[]{:S(2)}) collective-permute-start(bf16[16,4096]{1,0:T(8,128)(2,1)S(1)} %get-tuple-element.20), channel_id=1, source_target_pairs={{0,128},{64,192},{128,0},{192,64},{1,129},{65,193},{129,1},{193,65... | collective-permute-start | bytes 393224 | tf_op jit(solution)/shard_map/ppermute | solution.py:22
  55.2 1.1 fusion.13
  56.4 0.3 collective-permute-start.6
  56.7 3.9 %collective-permute-start.8 = (bf16[16,4096]{1,0:T(8,128)(2,1)S(1)}, bf16[16,4096]{1,0:T(8,128)(2,1)S(1)}, u32[]{:S(2)}, u32[]{:S(2)}) collective-permute-start(bf16[16,4096]{1,0:T(8,128)(2,1)S(1)} %get-tuple-element.16), channel_id=1, source_target_pairs={{0,192},{64,0},{128,64},{192,128},{1,193},{65,1},{129,65},{193,129... | collective-permute-start | bytes 393224 | tf_op jit(solution)/shard_map/ppermute | solution.py:22
  60.6 31.3 %collective-permute-start.7 = (bf16[16,4096]{1,0:T(8,128)(2,1)S(1)}, bf16[16,4096]{1,0:T(8,128)(2,1)S(1)}, u32[]{:S(2)}, u32[]{:S(2)}) collective-permute-start(bf16[16,4096]{1,0:T(8,128)(2,1)S(1)} %get-tuple-element.17), channel_id=1, source_target_pairs={{0,128},{64,192},{128,0},{192,64},{1,129},{65,193},{129,1},{193,65... | collective-permute-start | bytes 393224 | tf_op jit(solution)/shard_map/ppermute | solution.py:22
  92.1 1.6 %collective-permute-start.4 = (bf16[16,4096]{1,0:T(8,128)(2,1)S(1)}, bf16[16,4096]{1,0:T(8,128)(2,1)S(1)}, u32[]{:S(2)}, u32[]{:S(2)}) collective-permute-start(bf16[16,4096]{1,0:T(8,128)(2,1)S(1)} %fusion.9), channel_id=1, source_target_pairs={{0,128},{64,192},{128,0},{192,64},{1,129},{65,193},{129,1},{193,65... | collective-permute-start | bytes 393224 | tf_op jit(solution)/shard_map/ppermute | solution.py:27
  93.7 2.5 %collective-permute-start.3 = (bf16[16,4096]{1,0:T(8,128)(2,1)S(1)}, bf16[16,4096]{1,0:T(8,128)(2,1)S(1)}, u32[]{:S(2)}, u32[]{:S(2)}) collective-permute-start(bf16[16,4096]{1,0:T(8,128)(2,1)S(1)} %fusion.9), channel_id=1, source_target_pairs={{0,192},{64,0},{128,64},{192,128},{1,193},{65,1},{129,65},{193,129... | collective-permute-start | bytes 393224 | tf_op jit(solution)/shard_map/ppermute | solution.py:27
  96.2 0.1 collective-permute-done.7
  96.3 1.0 fusion.6
  97.4 2.3 %collective-permute-start.11 = (bf16[16,4096]{1,0:T(8,128)(2,1)S(1)}, bf16[16,4096]{1,0:T(8,128)(2,1)S(1)}, u32[]{:S(2)}, u32[]{:S(2)}) collective-permute-start(bf16[16,4096]{1,0:T(8,128)(2,1)S(1)} %fusion.6), channel_id=1, source_target_pairs={{0,64},{64,128},{128,192},{192,0},{1,65},{65,129},{129,193},{193,1... | collective-permute-start | bytes 393224 | tf_op jit(solution)/shard_map/ppermute | solution.py:27
  99.7 3.7 %collective-permute-start.10 = (bf16[16,4096]{1,0:T(8,128)(2,1)S(1)}, bf16[16,4096]{1,0:T(8,128)(2,1)S(1)}, u32[]{:S(2)}, u32[]{:S(2)}) collective-permute-start(bf16[16,4096]{1,0:T(8,128)(2,1)S(1)} %fusion.6), channel_id=1, source_target_pairs={{0,128},{64,192},{128,0},{192,64},{1,129},{65,193},{129,1},{193,65... | collective-permute-start | bytes 393224 | tf_op jit(solution)/shard_map/ppermute | solution.py:27
  103.3 4.0 %collective-permute-start.9 = (bf16[16,4096]{1,0:T(8,128)(2,1)S(1)}, bf16[16,4096]{1,0:T(8,128)(2,1)S(1)}, u32[]{:S(2)}, u32[]{:S(2)}) collective-permute-start(bf16[16,4096]{1,0:T(8,128)(2,1)S(1)} %fusion.6), channel_id=1, source_target_pairs={{0,192},{64,0},{128,64},{192,128},{1,193},{65,1},{129,65},{193,129... | collective-permute-start | bytes 393224 | tf_op jit(solution)/shard_map/ppermute | solution.py:27
  107.5 0.4 fusion.16
  107.9 0.3 broadcast_multiply_fusion
  108.3 1.9 %collective-permute-done.10 = bf16[16,4096]{1,0:T(8,128)(2,1)S(1)} collective-permute-done((bf16[16,4096]{1,0:T(8,128)(2,1)S(1)}, bf16[16,4096]{1,0:T(8,128)(2,1)S(1)}, u32[]{:S(2)}, u32[]{:S(2)}) %collective-permute-start.10) | collective-permute-done | bytes 131104 | tf_op jit(solution)/shard_map/ppermute | solution.py:27
  110.2 2.1 %collective-permute-done.9 = bf16[16,4096]{1,0:T(8,128)(2,1)S(1)} collective-permute-done((bf16[16,4096]{1,0:T(8,128)(2,1)S(1)}, bf16[16,4096]{1,0:T(8,128)(2,1)S(1)}, u32[]{:S(2)}, u32[]{:S(2)}) %collective-permute-start.9) | collective-permute-done | bytes 131104 | tf_op jit(solution)/shard_map/ppermute | solution.py:27
  112.4 3.1 %fusion.2 = f32[2,2,64,4096]{3,2,1,0:T(8,128)} fusion(bf16[2,2,64,4096]{3,2,1,0:T(8,128)(2,1)S(1)} %copy-done.1, f32[2,2,64,4096]{3,2,1,0:T(8,128)S(1)} %bitcast.37, f32[64,4096]{1,0:T(8,128)S(1)} %get-tuple-element.21, f32[64,4096]{1,0:T(8,128)S(1)} %maximum_convert_fusion, f32[2,64,4096]{2,1,0:T(8,128)S(1)} %broadcast_multiply_fusion, ...), kind=kLoop, calls=%fused_computation.4 | loop fusion | flops 6291456 | bytes 15728640 | tf_op jit(solution)/shard_map/add | solution.py:129
  (27 shorter events, 0.5 us)
Async XLA Ops:
  0.0 12.7 %copy-start = (bf16[2,2,64,4096]{3,2,1,0:T(8,128)(2,1)S(1)}, bf16[2,2,64,4096]{3,2,1,0:T(8,128)(2,1)}, u32[]{:S(2)}) copy-start(bf16[2,2,64,4096]{3,2,1,0:T(8,128)(2,1)} %param.6) | copy-start | bytes 6291460
  0.0 12.7 %copy-start.5 = (f32[2]{0:T(128)S(1)}, f32[2]{0:T(128)}, u32[]{:S(2)}) copy-start(f32[2]{0:T(128)} %param.11) | copy-start | bytes 28
  3.4 34.5 %all-to-all-start = ((bf16[64,64,256]{2,1,0:T(8,128)(2,1)}), bf16[64,64,256]{2,1,0:T(8,128)(2,1)}, u32[]{:S(2)}, u32[]{:S(2)}) async-start(bf16[64,64,256]{2,1,0:T(8,128)(2,1)} %bitcast.36), calls=%async_computation | async-start | bytes 4194304 | tf_op jit(solution)/shard_map/all_to_all | solution.py:120
  14.3 30.3 %copy-start.4 = (f32[64,4096]{1,0:T(8,128)S(1)}, f32[64,4096]{1,0:T(8,128)}, u32[]{:S(2)}) copy-start(f32[64,4096]{1,0:T(8,128)} %fusion.3) | copy-start | bytes 3145732
  37.9 69.6 %copy-start.3 = (s32[64,4096]{1,0:T(8,128)S(1)}, s32[64,4096]{1,0:T(8,128)}, u32[]{:S(2)}) copy-start(s32[64,4096]{1,0:T(8,128)} %m_ref.1) | copy-start | bytes 3145732
  44.7 15.9 %collective-permute-start = (bf16[16,4096]{1,0:T(8,128)(2,1)S(1)}, bf16[16,4096]{1,0:T(8,128)(2,1)S(1)}, u32[]{:S(2)}, u32[]{:S(2)}) collective-permute-start(bf16[16,4096]{1,0:T(8,128)(2,1)S(1)} %get-tuple-element.18), channel_id=1, source_target_pairs={{0,64},{64,128},{128,192},{192,0},{1,65},{65,129},{129,193},{193,1... | collective-permute-start | bytes 393224 | tf_op jit(solution)/shard_map/ppermute | solution.py:22
  48.1 43.8 %collective-permute-start.2 = (bf16[16,4096]{1,0:T(8,128)(2,1)S(1)}, bf16[16,4096]{1,0:T(8,128)(2,1)S(1)}, u32[]{:S(2)}, u32[]{:S(2)}) collective-permute-start(bf16[16,4096]{1,0:T(8,128)(2,1)S(1)} %get-tuple-element.19), channel_id=1, source_target_pairs={{0,192},{64,0},{128,64},{192,128},{1,193},{65,1},{129,65},{193,129... | collective-permute-start | bytes 393224 | tf_op jit(solution)/shard_map/ppermute | solution.py:22
  50.3 41.6 %collective-permute-start.1 = (bf16[16,4096]{1,0:T(8,128)(2,1)S(1)}, bf16[16,4096]{1,0:T(8,128)(2,1)S(1)}, u32[]{:S(2)}, u32[]{:S(2)}) collective-permute-start(bf16[16,4096]{1,0:T(8,128)(2,1)S(1)} %get-tuple-element.20), channel_id=1, source_target_pairs={{0,128},{64,192},{128,0},{192,64},{1,129},{65,193},{129,1},{193,65... | collective-permute-start | bytes 393224 | tf_op jit(solution)/shard_map/ppermute | solution.py:22
  56.4 37.3 %collective-permute-start.6 = (bf16[16,4096]{1,0:T(8,128)(2,1)S(1)}, bf16[16,4096]{1,0:T(8,128)(2,1)S(1)}, u32[]{:S(2)}, u32[]{:S(2)}) collective-permute-start(bf16[16,4096]{1,0:T(8,128)(2,1)S(1)} %get-tuple-element.15), channel_id=1, source_target_pairs={{0,64},{64,128},{128,192},{192,0},{1,65},{65,129},{129,193},{193,1... | collective-permute-start | bytes 393224 | tf_op jit(solution)/shard_map/ppermute | solution.py:22
  56.7 39.5 %collective-permute-start.8 = (bf16[16,4096]{1,0:T(8,128)(2,1)S(1)}, bf16[16,4096]{1,0:T(8,128)(2,1)S(1)}, u32[]{:S(2)}, u32[]{:S(2)}) collective-permute-start(bf16[16,4096]{1,0:T(8,128)(2,1)S(1)} %get-tuple-element.16), channel_id=1, source_target_pairs={{0,192},{64,0},{128,64},{192,128},{1,193},{65,1},{129,65},{193,129... | collective-permute-start | bytes 393224 | tf_op jit(solution)/shard_map/ppermute | solution.py:22
  60.6 35.8 %collective-permute-start.7 = (bf16[16,4096]{1,0:T(8,128)(2,1)S(1)}, bf16[16,4096]{1,0:T(8,128)(2,1)S(1)}, u32[]{:S(2)}, u32[]{:S(2)}) collective-permute-start(bf16[16,4096]{1,0:T(8,128)(2,1)S(1)} %get-tuple-element.17), channel_id=1, source_target_pairs={{0,128},{64,192},{128,0},{192,64},{1,129},{65,193},{129,1},{193,65... | collective-permute-start | bytes 393224 | tf_op jit(solution)/shard_map/ppermute | solution.py:22
  92.0 11.4 %collective-permute-start.5 = (bf16[16,4096]{1,0:T(8,128)(2,1)S(1)}, bf16[16,4096]{1,0:T(8,128)(2,1)S(1)}, u32[]{:S(2)}, u32[]{:S(2)}) collective-permute-start(bf16[16,4096]{1,0:T(8,128)(2,1)S(1)} %fusion.9), channel_id=1, source_target_pairs={{0,64},{64,128},{128,192},{192,0},{1,65},{65,129},{129,193},{193,1... | collective-permute-start | bytes 393224 | tf_op jit(solution)/shard_map/ppermute | solution.py:27
  92.1 15.3 %collective-permute-start.4 = (bf16[16,4096]{1,0:T(8,128)(2,1)S(1)}, bf16[16,4096]{1,0:T(8,128)(2,1)S(1)}, u32[]{:S(2)}, u32[]{:S(2)}) collective-permute-start(bf16[16,4096]{1,0:T(8,128)(2,1)S(1)} %fusion.9), channel_id=1, source_target_pairs={{0,128},{64,192},{128,0},{192,64},{1,129},{65,193},{129,1},{193,65... | collective-permute-start | bytes 393224 | tf_op jit(solution)/shard_map/ppermute | solution.py:27
  93.7 13.7 %collective-permute-start.3 = (bf16[16,4096]{1,0:T(8,128)(2,1)S(1)}, bf16[16,4096]{1,0:T(8,128)(2,1)S(1)}, u32[]{:S(2)}, u32[]{:S(2)}) collective-permute-start(bf16[16,4096]{1,0:T(8,128)(2,1)S(1)} %fusion.9), channel_id=1, source_target_pairs={{0,192},{64,0},{128,64},{192,128},{1,193},{65,1},{129,65},{193,129... | collective-permute-start | bytes 393224 | tf_op jit(solution)/shard_map/ppermute | solution.py:27
  97.4 10.9 %collective-permute-start.11 = (bf16[16,4096]{1,0:T(8,128)(2,1)S(1)}, bf16[16,4096]{1,0:T(8,128)(2,1)S(1)}, u32[]{:S(2)}, u32[]{:S(2)}) collective-permute-start(bf16[16,4096]{1,0:T(8,128)(2,1)S(1)} %fusion.6), channel_id=1, source_target_pairs={{0,64},{64,128},{128,192},{192,0},{1,65},{65,129},{129,193},{193,1... | collective-permute-start | bytes 393224 | tf_op jit(solution)/shard_map/ppermute | solution.py:27
  99.7 10.5 %collective-permute-start.10 = (bf16[16,4096]{1,0:T(8,128)(2,1)S(1)}, bf16[16,4096]{1,0:T(8,128)(2,1)S(1)}, u32[]{:S(2)}, u32[]{:S(2)}) collective-permute-start(bf16[16,4096]{1,0:T(8,128)(2,1)S(1)} %fusion.6), channel_id=1, source_target_pairs={{0,128},{64,192},{128,0},{192,64},{1,129},{65,193},{129,1},{193,65... | collective-permute-start | bytes 393224 | tf_op jit(solution)/shard_map/ppermute | solution.py:27
  103.3 8.9 %collective-permute-start.9 = (bf16[16,4096]{1,0:T(8,128)(2,1)S(1)}, bf16[16,4096]{1,0:T(8,128)(2,1)S(1)}, u32[]{:S(2)}, u32[]{:S(2)}) collective-permute-start(bf16[16,4096]{1,0:T(8,128)(2,1)S(1)} %fusion.6), channel_id=1, source_target_pairs={{0,192},{64,0},{128,64},{192,128},{1,193},{65,1},{129,65},{193,129... | collective-permute-start | bytes 393224 | tf_op jit(solution)/shard_map/ppermute | solution.py:27
  107.5 4.9 %copy-start.1 = (bf16[2,2,64,4096]{3,2,1,0:T(8,128)(2,1)S(1)}, bf16[2,2,64,4096]{3,2,1,0:T(8,128)(2,1)}, u32[]{:S(2)}) copy-start(bf16[2,2,64,4096]{3,2,1,0:T(8,128)(2,1)} %param.6) | copy-start | bytes 6291460
  107.5 4.9 %copy-start.2 = (f32[4,64,4096]{2,1,0:T(8,128)S(1)}, f32[4,64,4096]{2,1,0:T(8,128)}, u32[]{:S(2)}) copy-start(f32[4,64,4096]{2,1,0:T(8,128)} %get-tuple-element.11) | copy-start | bytes 12582916
